TPU v7x, 128 devices: a whole 4x4x4 slice. The times are simulated.
128 devices in a mesh: wide: 16 (over x, y_hi, core), head: 8 (over z, y_lo).
Axes of the slice: x: 4, y: 4 (y_hi: 2, y_lo: 2; y = y_hi * 2 + y_lo), z: 4, core: 2. Of those that a mesh axis runs over, the one named last changes fastest.
Arguments:
- tokens: bfloat16 [16384, 2048], P('wide', 'head'), may hold values from -6 to 6
- lengths: int32 [32], P('wide'), may hold values from 32 to 512, as said below
- positions: int32 [32, 512], P('wide'), may hold values from 0 to 1022, as said below
- attn_gain: float32 [2048], replicated, may hold values from 0.1 to 1.9
- qkv_weight: float32 [2048, 6144], P('wide', 'head'), may hold values from -8 to 8
- lambdas: float32 [4, 8, 128], P(None, 'head'), may hold values from -0.6 to 0.6
- sub_gain: float32 [8, 256], P('head'), may hold values from 0.1 to 1.9
- out_weight: float32 [2048, 2048], P('head', 'wide'), may hold values from -0.125 to 0.125
- ffn_gain: float32 [2048], replicated, may hold values from 0.1 to 1.9
- gate_up_weight: float32 [2048, 2, 5632], P('wide', None, 'head'), may hold values from -0.125 to 0.125
- down_weight: float32 [5632, 2048], P('head', 'wide'), may hold values from -0.078125 to 0.078125
Outputs:
- result: bfloat16 [16384, 2048], P('wide', 'head')
Inputs may be any that keep to these rules, and one draw needn't show every extreme that they name: `lengths`: each prompt's live slots are its first ones; some prompt has all 512 slots live. Each prompt's positions start at 0 and rise by 1 or 2 from slot to slot; some prompt's positions rise by 2 throughout.
All inputs are finite; a program needn't handle non-finite values.
Results may differ from a plain program's by a relative error of at most 0.017.
The roundings to bfloat16 on the way count: a program that leaves them out, or rounds other values in their place, can miss the bound.
Values may be sent and summed in bfloat16 or wider, within the bound.
No kernel may reach another device: no remote copies, remote signals or barrier semaphores. Data moves between devices by JAX's collectives and lax.ppermute only.
A program may use at most 128 MiB of HBM per device.

v0:
```python
import jax
import jax.numpy as jnp
from jax import lax
from jax.sharding import PartitionSpec as P

HALF = 128
VDIM = 256


lambda_base = 0.2


def rms_scale(values, gain):
    flat = values.astype(jnp.float32)
    return flat * lax.rsqrt(jnp.mean(flat * flat, axis=-1, keepdims=True) + 1e-05) * gain


def rotate(quads, places):
    width = quads.shape[-1]
    half = width // 2
    freq = 10000.0 ** (-(jnp.arange(half, dtype=jnp.float32) * 2.0 / width))
    angle = places.astype(jnp.float32)[:, None] * freq[None, :]
    cosine = jnp.cos(angle)[:, None, None, :]
    sine = jnp.sin(angle)[:, None, None, :]
    first = quads[..., :half]
    second = quads[..., half:]
    return jnp.concatenate(
        [first * cosine - second * sine, second * cosine + first * sine], axis=-1
    )


def diff_attend(first_q, second_q, first_k, second_k, values, rows_at, length, balance, gain):
    scale = first_q.shape[-1] ** (-0.5)
    keys_at = jnp.arange(first_k.shape[0], dtype=jnp.int32)
    allowed = (keys_at[None, :] <= rows_at[:, None]) & (keys_at[None, :] < length)
    one = jnp.einsum("rhd,shd->hrs", first_q, first_k, preferred_element_type=jnp.float32) * scale
    two = jnp.einsum("rhd,shd->hrs", second_q, second_k, preferred_element_type=jnp.float32) * scale
    one = jax.nn.softmax(jnp.where(allowed[None], one, -1e30), axis=-1)
    two = jax.nn.softmax(jnp.where(allowed[None], two, -1e30), axis=-1)
    weights = (one - balance[:, None, None] * two).astype(jnp.bfloat16)
    merged = jnp.einsum("hrs,shv->rhv", weights, values, preferred_element_type=jnp.float32)
    merged = rms_scale(merged, gain[None]) * (1.0 - lambda_base)
    merged = jnp.where((rows_at < length)[:, None, None], merged, 0.0)
    return merged.reshape(merged.shape[0], -1).astype(jnp.bfloat16)


def body(
    tokens,
    lengths,
    positions,
    attn_gain,
    qkv_weight,
    lambdas,
    sub_gain,
    out_weight,
    ffn_gain,
    gate_up_weight,
    down_weight,
):
    prompts_here = lengths.shape[0]
    slots = positions.shape[1]
    width = 4 * HALF + VDIM
    full_rows = lax.all_gather(tokens, "head", axis=1, tiled=True)
    normed = rms_scale(full_rows, attn_gain).astype(jnp.bfloat16)
    qkv_local = qkv_weight.astype(jnp.bfloat16)
    columns = normed
    joined = jnp.dot(
        columns,
        lax.all_gather(qkv_local, "wide", axis=0, tiled=True),
        preferred_element_type=jnp.float32,
    )
    heads_here = qkv_local.shape[1] // width
    balance = (
        jnp.exp(jnp.sum(lambdas[0] * lambdas[1], -1))
        - jnp.exp(jnp.sum(lambdas[2] * lambdas[3], -1))
        + lambda_base
    )
    outputs = []
    for prompt in range(prompts_here):
        block = joined[prompt * slots : (prompt + 1) * slots].reshape(slots, heads_here, width)
        quads = rotate(
            block[..., : 4 * HALF].reshape(slots, heads_here, 4, HALF), positions[prompt]
        ).astype(jnp.bfloat16)
        values = block[..., 4 * HALF :].astype(jnp.bfloat16)
        length = lengths[prompt]
        first_k = quads[:, :, 2]
        second_k = quads[:, :, 3]
        attended = diff_attend(
            quads[:, :, 0],
            quads[:, :, 1],
            first_k,
            second_k,
            values,
            jnp.arange(slots, dtype=jnp.int32),
            length,
            balance,
            sub_gain,
        )
        outputs.append(attended)
    attn = jnp.concatenate(outputs, axis=0)
    mix_terms = jnp.dot(
        attn,
        lax.all_gather(out_weight.astype(jnp.bfloat16), "wide", axis=1, tiled=True),
        preferred_element_type=jnp.float32,
    )
    mix = lax.psum_scatter(
        mix_terms.astype(jnp.bfloat16), "head", scatter_dimension=1, tiled=True
    ).astype(jnp.float32)
    middle = (tokens.astype(jnp.float32) + mix).astype(jnp.bfloat16)
    middle_full = lax.all_gather(middle, "head", axis=1, tiled=True)
    normed2 = rms_scale(middle_full, ffn_gain).astype(jnp.bfloat16)
    gate_up_local = gate_up_weight.astype(jnp.bfloat16)
    columns = normed2
    both = jnp.einsum(
        "td,dgf->tgf",
        columns,
        lax.all_gather(gate_up_local, "wide", axis=0, tiled=True),
        preferred_element_type=jnp.float32,
    )
    hidden = (jax.nn.silu(both[:, 0]) * both[:, 1]).astype(jnp.bfloat16)
    ffn_terms = jnp.dot(
        hidden,
        lax.all_gather(down_weight.astype(jnp.bfloat16), "wide", axis=1, tiled=True),
        preferred_element_type=jnp.float32,
    )
    ffn = lax.psum_scatter(
        ffn_terms.astype(jnp.bfloat16), "head", scatter_dimension=1, tiled=True
    ).astype(jnp.float32)
    return (middle.astype(jnp.float32) + ffn).astype(jnp.bfloat16)


def solution(mesh):
    placed = (
        P("wide", "head"),
        P("wide"),
        P("wide", None),
        P(),
        P("wide", "head"),
        P(None, "head", None),
        P("head", None),
        P("head", "wide"),
        P(),
        P("wide", None, "head"),
        P("head", "wide"),
    )
    return jax.shard_map(
        body, mesh=mesh, in_specs=placed, out_specs=P("wide", "head"), check_vma=False
    )
```

profile of v0, /device:TPU:2, one launch (start us, length us, event | category | flops | bytes accessed | tf_op | source)
XLA Modules:
  0.0 619.8 jit_solution(14409823518793805101)
XLA Ops:
  6.5 0.7 all-gather.7.cloned.1.call-update
  7.3 1.7 convert_element_type.110
  9.1 1.5 convert_element_type.119
  10.7 0.8 slice_convert_fusion.3
  11.5 1.4 fusion.68
  12.9 1.4 multiply_reduce_fusion.2
  15.6 1.2 iota_compare_fusion.1
  16.8 1.0 multiply_cosine_fusion.1
  17.8 82.9 %all-gather.7.cloned.1.call-done = bf16[1024,2048]{1,0:T(8,128)(2,1)} async-done(((bf16[1024,256]{1,0:T(8,128)(2,1)}), bf16[1024,2048]{1,0:T(8,128)(2,1)}) %all-gather.7.cloned.1.call-update) | async-done | bytes 4194320 | tf_op jit(solution)/shard_map/all_gather | solution.py:63
  100.7 3.1 fusion
  103.8 52.1 %all-gather.9.cloned.1.call-done = bf16[2048,768]{1,0:T(8,128)(2,1)} async-done(((bf16[128,768]{1,0:T(8,128)(2,1)}), bf16[2048,768]{1,0:T(8,128)(2,1)}) %all-gather.9.cloned.1.call-update) | async-done | bytes 3145744 | tf_op jit(solution)/shard_map/all_gather | solution.py:69
  155.9 6.6 %fusion.9 = f32[1024,768]{0,1:T(8,128)S(1)} fusion(bf16[2048,768]{1,0:T(8,128)(2,1)} %all-gather.9.cloned.1.call-done, bf16[1024,2048]{1,0:T(8,128)(2,1)} %all-gather.7.cloned.1.call-done, f32[2048]{0:T(1024)S(1)} %copy-done.5, f32[1024]{0:T(1024)S(1)} %add_rsqrt_fusion.1), kind=kOutput, calls=%fused_computation.12 | convolution fusion | flops 3229614080 | bytes 10498048 | tf_op jit(solution)/shard_map/dot_general | solution.py:67
  163.0 0.4 add_convert_fusion.2
  163.8 0.4 fusion.71
  164.6 0.4 fusion.70
  165.2 0.4 fusion.69
  165.8 0.6 multiply_reduce_fusion
  166.4 0.6 multiply_reduce_fusion.1
  167.3 35.0 %all-gather.11.cloned.1.call-done = bf16[256,2048]{1,0:T(8,128)(2,1)} async-done(((bf16[256,128]{1,0:T(8,128)(2,1)}), bf16[256,2048]{1,0:T(8,128)(2,1)}) %all-gather.11.cloned.1.call-update) | async-done | bytes 1048592 | tf_op jit(solution)/shard_map/all_gather | solution.py:103
  202.2 4.5 convolution_convert_fusion.1
  206.8 90.7 %reduce-scatter.3.cloned.1.call-done = bf16[1024,256]{1,0:T(8,128)(2,1)} async-done(((bf16[1024,2048]{1,0:T(8,128)(2,1)}), bf16[1024,256]{1,0:T(8,128)(2,1)}) %reduce-scatter.3.cloned.1.call-update) | async-done | bytes 524304 | tf_op jit(solution)/shard_map/reduce_scatter | solution.py:106
  297.6 2.0 add_convert_fusion.1
  299.6 0.8 convert_element_type.126
  300.5 0.7 convert_element_type.128
  301.4 87.4 %all-gather.13.cloned.1.call-done = bf16[1024,2048]{1,0:T(8,128)(2,1)} async-done(((bf16[1024,256]{1,0:T(8,128)(2,1)}), bf16[1024,2048]{1,0:T(8,128)(2,1)}) %all-gather.13.cloned.1.call-update) | async-done | bytes 4194320 | tf_op jit(solution)/shard_map/all_gather | solution.py:110
  388.8 3.1 fusion.3
  391.9 65.8 %all-gather.15.cloned.1.call-done = bf16[2048,2,704]{0,2,1:T(8,128)(2,1)} async-done(((bf16[128,2,704]{0,2,1:T(8,128)(2,1)}), bf16[2048,2,704]{0,2,1:T(8,128)(2,1)}) %all-gather.15.cloned.1.call-update) | async-done | bytes 5767184 | tf_op jit(solution)/shard_map/all_gather | solution.py:117
  457.7 11.8 %fusion.7 = f32[1024,2,704]{0,2,1:T(8,128)} fusion(bf16[2048,2,704]{0,2,1:T(8,128)(2,1)} %all-gather.15.cloned.1.call-done, bf16[1024,2048]{1,0:T(8,128)(2,1)} %all-gather.13.cloned.1.call-done, f32[2048]{0:T(1024)S(1)} %copy-done.6, f32[1024]{0:T(1024)S(1)} %add_rsqrt_fusion), kind=kOutput, calls=%fused_computation.11 | convolution fusion | flops 5913968640 | bytes 15740928 | tf_op jit(solution)/shard_map/td,dgf->tgf/dot_general | solution.py:114
  469.5 41.7 %all-gather.17.cloned.1.call-done = bf16[704,2048]{1,0:T(8,128)(2,1)} async-done(((bf16[704,128]{1,0:T(8,128)(2,1)}), bf16[704,2048]{1,0:T(8,128)(2,1)}) %all-gather.17.cloned.1.call-update) | async-done | bytes 2883600 | tf_op jit(solution)/shard_map/all_gather | solution.py:123
  511.2 9.0 %convolution_convert_fusion = bf16[1024,2048]{1,0:T(8,128)(2,1)} fusion(bf16[704,2048]{1,0:T(8,128)(2,1)} %all-gather.17.cloned.1.call-done, f32[1024,2,704]{0,2,1:T(8,128)} %fusion.7), kind=kOutput, calls=%fused_computation.17 | convolution fusion | flops 2959212544 | bytes 12845056 | tf_op jit(solution)/shard_map/dot_general | solution.py:121
  520.2 90.7 %reduce-scatter.5.cloned.1.call-done = bf16[1024,256]{1,0:T(8,128)(2,1)} async-done(((bf16[1024,2048]{1,0:T(8,128)(2,1)}), bf16[1024,256]{1,0:T(8,128)(2,1)}) %reduce-scatter.5.cloned.1.call-update) | async-done | bytes 524304 | tf_op jit(solution)/shard_map/reduce_scatter | solution.py:126
  611.0 2.0 add_convert_fusion
  (43 shorter events, 2.6 us)
Async XLA Ops:
  6.5 149.3 %copy-start.5 = (f32[2048]{0:T(1024)S(1)}, f32[2048]{0:T(1024)}, u32[]{:S(2)}) copy-start(f32[2048]{0:T(1024)} %param.14) | copy-start | bytes 24580
  6.5 94.1 %all-gather.7.cloned.1.call-start = ((), (), s32[]{:S(2)}) async-start(), calls=%async_computation.2 | async-start | bytes 4718592 | tf_op jit(solution)/shard_map/all_gather | solution.py:63
  7.3 148.6 %all-gather.9.cloned.1.call-start = ((), (), s32[]{:S(2)}) async-start(), calls=%async_computation.3 | async-start | bytes 3342336 | tf_op jit(solution)/shard_map/all_gather | solution.py:69
  9.0 193.2 %all-gather.11.cloned.1.call-start = ((), (), s32[]{:S(2)}) async-start(), calls=%async_computation.4 | async-start | bytes 1114112 | tf_op jit(solution)/shard_map/all_gather | solution.py:103
  10.6 286.9 %reduce-scatter.3.cloned.1.call-start = ((), (), s32[]{:S(2)}) async-start(), calls=%async_computation.5 | async-start | bytes 4718592 | tf_op jit(solution)/shard_map/reduce_scatter | solution.py:106
  166.4 0.7 copy-start.4
  202.2 95.3 %copy-start.1 = (bf16[1024,256]{1,0:T(8,128)(2,1)S(1)}, bf16[1024,256]{1,0:T(8,128)(2,1)}, u32[]{:S(2)}) copy-start(bf16[1024,256]{1,0:T(8,128)(2,1)} %param.11) | copy-start | bytes 1572868
  206.7 92.9 %copy-start.2 = (f32[128,2,704]{0,2,1:T(8,128)S(1)}, f32[128,2,704]{0,2,1:T(8,128)}, u32[]{:S(2)}) copy-start(f32[128,2,704]{0,2,1:T(8,128)} %param.20) | copy-start | bytes 2162692
  206.7 93.7 %copy-start.3 = (f32[704,128]{1,0:T(8,128)S(1)}, f32[704,128]{1,0:T(8,128)}, u32[]{:S(2)}) copy-start(f32[704,128]{1,0:T(8,128)} %param.21) | copy-start | bytes 1081348
  206.8 251.0 %copy-start.6 = (f32[2048]{0:T(1024)S(1)}, f32[2048]{0:T(1024)}, u32[]{:S(2)}) copy-start(f32[2048]{0:T(1024)} %param.19) | copy-start | bytes 24580
  206.8 182.1 %all-gather.13.cloned.1.call-start = ((), (), s32[]{:S(2)}) async-start(), calls=%async_computation.6 | async-start | bytes 4718592 | tf_op jit(solution)/shard_map/all_gather | solution.py:110
  299.5 158.2 %all-gather.15.cloned.1.call-start = ((), (), s32[]{:S(2)}) async-start(), calls=%async_computation.7 | async-start | bytes 6127616 | tf_op jit(solution)/shard_map/all_gather | solution.py:117
  300.4 210.8 %all-gather.17.cloned.1.call-start = ((), (), s32[]{:S(2)}) async-start(), calls=%async_computation.8 | async-start | bytes 3063808 | tf_op jit(solution)/shard_map/all_gather | solution.py:123
  301.2 309.8 %reduce-scatter.5.cloned.1.call-start = ((), (), s32[]{:S(2)}) async-start(), calls=%async_computation.9 | async-start | bytes 4718592 | tf_op jit(solution)/shard_map/reduce_scatter | solution.py:126
  520.2 90.8 %copy-start = (bf16[1024,256]{1,0:T(8,128)(2,1)S(1)}, bf16[1024,256]{1,0:T(8,128)(2,1)}, u32[]{:S(2)}) copy-start(bf16[1024,256]{1,0:T(8,128)(2,1)} %add_convert_fusion.1) | copy-start | bytes 1572868
Sparse Core Ops, SparseCore 0:
  8.9 91.7 all-gather.6
  103.1 52.7 all-gather.8
  158.1 44.0 all-gather.10
  206.9 90.6 reduce-scatter.2
  299.7 89.1 all-gather.12
  390.9 66.7 all-gather.14
  460.0 51.1 all-gather.16
  520.3 90.5 reduce-scatter.4
where the time goes:
time: 621 us; the launch traced here: 620 us
  waiting for transfers between devices  547 us (88%)
  matrix products  34.6 us (6%)
  other arithmetic  20.6 us (3%)
  between operations  15 us (2%)
    reduce_scatter x1, waiting for transfers between devices, body(): lax.psum_scatter(ffn_terms.astype(jnp.bfloat16), 'head', scatter_dimensio...  90.7 us
    reduce_scatter x1, waiting for transfers between devices, body(): lax.psum_scatter(mix_terms.astype(jnp.bfloat16), 'head', scatter_dimensio...  90.7 us
    all_gather x1, waiting for transfers between devices, body(): middle_full = lax.all_gather(middle, 'head', axis=1, tiled=True)  87.4 us
    all_gather x1, waiting for transfers between devices, body(): full_rows = lax.all_gather(tokens, 'head', axis=1, tiled=True)  82.9 us
    all_gather x1, waiting for transfers between devices, body(): lax.all_gather(gate_up_local, 'wide', axis=0, tiled=True)  65.8 us
    all_gather x1, waiting for transfers between devices, body(): lax.all_gather(qkv_local, 'wide', axis=0, tiled=True)  52.1 us
    all_gather x1, waiting for transfers between devices, body(): lax.all_gather(down_weight.astype(jnp.bfloat16), 'wide', axis=1, tiled=True)  41.7 us
    all_gather x1, waiting for transfers between devices, body(): lax.all_gather(out_weight.astype(jnp.bfloat16), 'wide', axis=1, tiled=True)  35 us
  transfers between devices with their start and end apart: 8, of which 8 were waited for; matrix products, arithmetic and copies ran while one was open for 6% of the time, Pallas kernels for 0%

commit v1 on v0

--- a/solution.py
+++ b/solution.py
@@ -27,6 +27,22 @@
     return jnp.concatenate(
         [first * cosine - second * sine, second * cosine + first * sine], axis=-1
     )
+
+
+def gather_blocks(x, axis, n, dim):
+    spread = jnp.broadcast_to(x[None], (n,) + x.shape)
+    got = lax.all_to_all(spread, axis, 0, 0, tiled=True)
+    got = jnp.moveaxis(got, 0, dim)
+    shape = list(x.shape)
+    shape[dim] *= n
+    return got.reshape(shape)
+
+
+def scatter_sum(terms, axis, n):
+    rows, cols = terms.shape
+    parts = terms.astype(jnp.bfloat16).reshape(rows, n, cols // n)
+    got = lax.all_to_all(parts, axis, 1, 1, tiled=True)
+    return jnp.sum(got.astype(jnp.float32), axis=1)
 
 
 def diff_attend(first_q, second_q, first_k, second_k, values, rows_at, length, balance, gain):
@@ -60,13 +76,15 @@
     prompts_here = lengths.shape[0]
     slots = positions.shape[1]
     width = 4 * HALF + VDIM
-    full_rows = lax.all_gather(tokens, "head", axis=1, tiled=True)
+    n_head = lax.axis_size("head")
+    n_wide = lax.axis_size("wide")
+    full_rows = gather_blocks(tokens, "head", n_head, 1)
     normed = rms_scale(full_rows, attn_gain).astype(jnp.bfloat16)
     qkv_local = qkv_weight.astype(jnp.bfloat16)
     columns = normed
     joined = jnp.dot(
         columns,
-        lax.all_gather(qkv_local, "wide", axis=0, tiled=True),
+        gather_blocks(qkv_local, "wide", n_wide, 0),
         preferred_element_type=jnp.float32,
     )
     heads_here = qkv_local.shape[1] // width
@@ -100,32 +118,28 @@
     attn = jnp.concatenate(outputs, axis=0)
     mix_terms = jnp.dot(
         attn,
-        lax.all_gather(out_weight.astype(jnp.bfloat16), "wide", axis=1, tiled=True),
+        gather_blocks(out_weight.astype(jnp.bfloat16), "wide", n_wide, 1),
         preferred_element_type=jnp.float32,
     )
-    mix = lax.psum_scatter(
-        mix_terms.astype(jnp.bfloat16), "head", scatter_dimension=1, tiled=True
-    ).astype(jnp.float32)
+    mix = scatter_sum(mix_terms, "head", n_head)
     middle = (tokens.astype(jnp.float32) + mix).astype(jnp.bfloat16)
-    middle_full = lax.all_gather(middle, "head", axis=1, tiled=True)
+    middle_full = gather_blocks(middle, "head", n_head, 1)
     normed2 = rms_scale(middle_full, ffn_gain).astype(jnp.bfloat16)
     gate_up_local = gate_up_weight.astype(jnp.bfloat16)
     columns = normed2
     both = jnp.einsum(
         "td,dgf->tgf",
         columns,
-        lax.all_gather(gate_up_local, "wide", axis=0, tiled=True),
+        gather_blocks(gate_up_local, "wide", n_wide, 0),
         preferred_element_type=jnp.float32,
     )
     hidden = (jax.nn.silu(both[:, 0]) * both[:, 1]).astype(jnp.bfloat16)
     ffn_terms = jnp.dot(
         hidden,
-        lax.all_gather(down_weight.astype(jnp.bfloat16), "wide", axis=1, tiled=True),
+        gather_blocks(down_weight.astype(jnp.bfloat16), "wide", n_wide, 1),
         preferred_element_type=jnp.float32,
     )
-    ffn = lax.psum_scatter(
-        ffn_terms.astype(jnp.bfloat16), "head", scatter_dimension=1, tiled=True
-    ).astype(jnp.float32)
+    ffn = scatter_sum(ffn_terms, "head", n_head)
     return (middle.astype(jnp.float32) + ffn).astype(jnp.bfloat16)
 
 

time: 621 us -> 459 us (0.74)
  waiting for transfers between devices: 547 us -> 257 us
  starting transfers between devices: 0.47 us -> 67.7 us
  blocking collectives: 0 us -> 52.5 us
  local copies, waits for them, and re-layouts: 1.92 us -> 27.5 us
  between operations: 15 us -> 1.69 us
  matrix products: 34.6 us -> 26.6 us
    all_gather x6 -> x0, waiting for transfers between devices: 365 us -> none  [the longest x1 87.4 us: body(): middle_full = lax.all_gather(middle, 'head', axis=1, tiled=True)]
    all_to_all x0 -> x7, waiting for transfers between devices: none -> 257 us  [the longest x6 208 us: gather_blocks(): got = lax.all_to_all(spread, axis, 0, 0, tiled=True)]
    reduce_scatter x2 -> x0, waiting for transfers between devices: 181 us -> none  [the longest x1 90.7 us: body(): lax.psum_scatter(ffn_terms.astype(jnp.bfloat16), 'head', scatter_dimensio...]
    all_to_all x0 -> x7, starting transfers between devices: none -> 67.7 us  [the longest x6 62.9 us: gather_blocks(): got = lax.all_to_all(spread, axis, 0, 0, tiled=True)]
    all_to_all x0 -> x1, blocking collectives: none -> 52.5 us  [scatter_sum(): got = lax.all_to_all(parts, axis, 1, 1, tiled=True)]
    broadcast_in_dim x0 -> x6, local copies, waits for them, and re-layouts: none -> 14.8 us  [gather_blocks(): spread = jnp.broadcast_to(x[None], (n,) + x.shape)]
    dot_general x4, matrix products: 31.9 us -> 23.9 us  [the longest x1 9.87 us: body(): jnp.einsum('td,dgf->tgf', columns, gather_blocks(gate_up_local, 'wide', n...]
    all_to_all x0 -> x1, local copies, waits for them, and re-layouts: none -> 6.44 us  [gather_blocks(): got = lax.all_to_all(spread, axis, 0, 0, tiled=True)]
  transfers between devices with their start and end apart: 8 -> 7, of which waited for: 8 -> 7; matrix products, arithmetic and copies ran while one was open for 6% -> 10% of each run, Pallas kernels for 0% -> 0%
where the time goes in v1:
time: 459 us; the launch traced here: 455 us
  waiting for transfers between devices  257 us (56%)
  starting transfers between devices  67.7 us (15%)
  blocking collectives  52.5 us (11%)
  local copies, waits for them, and re-layouts  27.5 us (6%)
  matrix products  26.6 us (6%)
  other arithmetic  21.2 us (5%)
    all_to_all x6, waiting for transfers between devices, gather_blocks(): got = lax.all_to_all(spread, axis, 0, 0, tiled=True)  208 us
    all_to_all x6, starting transfers between devices, gather_blocks(): got = lax.all_to_all(spread, axis, 0, 0, tiled=True)  62.9 us
    all_to_all x1, blocking collectives, scatter_sum(): got = lax.all_to_all(parts, axis, 1, 1, tiled=True)  52.5 us
    all_to_all x1, waiting for transfers between devices, scatter_sum(): got = lax.all_to_all(parts, axis, 1, 1, tiled=True)  49.5 us
    broadcast_in_dim x6, local copies, waits for them, and re-layouts, gather_blocks(): spread = jnp.broadcast_to(x[None], (n,) + x.shape)  14.8 us
    dot_general x1, matrix products, body(): jnp.einsum('td,dgf->tgf', columns, gather_blocks(gate_up_local, 'wide', n...  9.87 us
  transfers between devices with their start and end apart: 7, of which 7 were waited for; matrix products, arithmetic and copies ran while one was open for 10% of the time, Pallas kernels for 0%

profile of v1, /device:TPU:2, one launch (start us, length us, event | category | flops | bytes accessed | tf_op | source)
XLA Modules:
  0.0 454.5 jit_solution(13879153306003415051)
XLA Ops:
  1.3 2.5 broadcast_in_dim.38
  3.8 6.5 %all-to-all-start = ((bf16[8,1024,256]{1,2,0:T(8,128)(2,1)}), bf16[8,1024,256]{1,2,0:T(8,128)(2,1)}, u32[]{:S(2)}, u32[]{:S(2)}) async-start(bf16[8,1024,256]{1,2,0:T(8,128)(2,1)} %broadcast_in_dim.38), calls=%async_computation | async-start | bytes 8388608 | tf_op jit(solution)/shard_map/all_to_all | solution.py:34
  10.3 49.5 %all-to-all-done = bf16[8,1024,256]{1,2,0:T(8,128)(2,1)} async-done(((bf16[8,1024,256]{1,2,0:T(8,128)(2,1)}), bf16[8,1024,256]{1,2,0:T(8,128)(2,1)}, u32[]{:S(2)}, u32[]{:S(2)}) %all-to-all-start) | async-done | bytes 4194336 | tf_op jit(solution)/shard_map/all_to_all | solution.py:34
  59.8 2.1 broadcast_in_dim.39
  61.8 7.2 %all-to-all-start.1 = ((bf16[16,128,768]{2,1,0:T(8,128)(2,1)}), bf16[16,128,768]{2,1,0:T(8,128)(2,1)S(1)}, u32[]{:S(2)}, u32[]{:S(2)}) async-start(bf16[16,128,768]{2,1,0:T(8,128)(2,1)} %broadcast_in_dim.39), calls=%async_computation.1 | async-start | bytes 6291456 | tf_op jit(solution)/shard_map/all_to_all | solution.py:34
  73.7 1.7 multiply_cosine_fusion.1
  75.4 3.1 fusion
  78.5 4.1 fusion.2
  82.6 25.2 %all-to-all-done.1 = bf16[16,128,768]{2,1,0:T(8,128)(2,1)S(1)} async-done(((bf16[16,128,768]{2,1,0:T(8,128)(2,1)}), bf16[16,128,768]{2,1,0:T(8,128)(2,1)S(1)}, u32[]{:S(2)}, u32[]{:S(2)}) %all-to-all-start.1) | async-done | bytes 3145760 | tf_op jit(solution)/shard_map/all_to_all | solution.py:34
  107.9 2.0 broadcast_in_dim.43
  109.8 10.6 %all-to-all-start.2 = ((bf16[16,256,128]{1,2,0:T(8,128)(2,1)}), bf16[16,256,128]{1,2,0:T(8,128)(2,1)S(1)}, u32[]{:S(2)}, u32[]{:S(2)}) async-start(bf16[16,256,128]{1,2,0:T(8,128)(2,1)} %broadcast_in_dim.43), calls=%async_computation.2 | async-start | bytes 2097152 | tf_op jit(solution)/shard_map/all_to_all | solution.py:34
  120.4 6.2 %fusion.68 = f32[1024,768]{0,1:T(8,128)S(1)} fusion(bf16[1024,2048]{0,1:T(8,128)(2,1)} %bitcast.121, bf16[2048,768]{1,0:T(8,128)(2,1)} %bitcast.124), kind=kOutput, calls=%fused_computation.124 | convolution fusion | flops 3221225472 | bytes 10485760 | tf_op jit(solution)/shard_map/dot_general | solution.py:85
  131.8 4.5 all-to-all-done.2
  136.3 1.3 convolution_convert_fusion.1
  137.6 2.2 copy.45
  139.8 4.9 %all-to-all-start.3 = ((bf16[1024,8,256]{2,0,1:T(8,128)(2,1)}), bf16[1024,8,256]{2,0,1:T(8,128)(2,1)}, u32[]{:S(2)}, u32[]{:S(2)}) async-start(bf16[1024,8,256]{2,0,1:T(8,128)(2,1)} %bitcast.116), calls=%async_computation.3 | async-start | bytes 8388608 | tf_op jit(solution)/shard_map/all_to_all | solution.py:44
  144.7 49.5 %all-to-all-done.3 = bf16[1024,8,256]{2,0,1:T(8,128)(2,1)} async-done(((bf16[1024,8,256]{2,0,1:T(8,128)(2,1)}), bf16[1024,8,256]{2,0,1:T(8,128)(2,1)}, u32[]{:S(2)}, u32[]{:S(2)}) %all-to-all-start.3) | async-done | bytes 4194336 | tf_op jit(solution)/shard_map/all_to_all | solution.py:44
  194.2 3.9 broadcast_in_dim.45
  198.0 6.2 %all-to-all-start.5 = ((bf16[16,128,2,704]{1,3,2,0:T(8,128)(2,1)}), bf16[16,128,2,704]{1,3,2,0:T(8,128)(2,1)}, u32[]{:S(2)}, u32[]{:S(2)}) async-start(bf16[16,128,2,704]{1,3,2,0:T(8,128)(2,1)} %broadcast_in_dim.45), calls=%async_computation.5 | async-start | bytes 11534336 | tf_op jit(solution)/shard_map/all_to_all | solution.py:34
  204.2 2.9 convert_reduce_fusion.1
  207.2 64.0 %all-to-all-done.5 = bf16[16,128,2,704]{1,3,2,0:T(8,128)(2,1)} async-done(((bf16[16,128,2,704]{1,3,2,0:T(8,128)(2,1)}), bf16[16,128,2,704]{1,3,2,0:T(8,128)(2,1)}, u32[]{:S(2)}, u32[]{:S(2)}) %all-to-all-start.5) | async-done | bytes 5767200 | tf_op jit(solution)/shard_map/all_to_all | solution.py:34
  271.3 2.3 broadcast_in_dim.44
  273.6 4.7 %all-to-all-start.4 = ((bf16[8,1024,256]{2,1,0:T(8,128)(2,1)}), bf16[8,1024,256]{2,1,0:T(8,128)(2,1)}, u32[]{:S(2)}, u32[]{:S(2)}) async-start(bf16[8,1024,256]{2,1,0:T(8,128)(2,1)} %broadcast_in_dim.44), calls=%async_computation.4 | async-start | bytes 8388608 | tf_op jit(solution)/shard_map/all_to_all | solution.py:34
  278.4 49.4 %all-to-all-done.4 = bf16[8,1024,256]{2,1,0:T(8,128)(2,1)} async-done(((bf16[8,1024,256]{2,1,0:T(8,128)(2,1)}), bf16[8,1024,256]{2,1,0:T(8,128)(2,1)}, u32[]{:S(2)}, u32[]{:S(2)}) %all-to-all-start.4) | async-done | bytes 4194336 | tf_op jit(solution)/shard_map/all_to_all | solution.py:34
  327.8 2.1 broadcast_in_dim.46
  329.9 27.8 %all-to-all-start.6 = ((bf16[16,704,128]{2,1,0:T(8,128)(2,1)}), bf16[16,704,128]{2,1,0:T(8,128)(2,1)S(1)}, u32[]{:S(2)}, u32[]{:S(2)}) async-start(bf16[16,704,128]{2,1,0:T(8,128)(2,1)} %broadcast_in_dim.46), calls=%async_computation.6 | async-start | bytes 5767168 | tf_op jit(solution)/shard_map/all_to_all | solution.py:34
  357.7 6.4 %copy.23 = bf16[8,1024,256]{1,2,0:T(8,128)(2,1)} copy(bf16[8,1024,256]{2,1,0:T(8,128)(2,1)} %all-to-all-done.4) | data formatting | bytes 8388608 | tf_op jit(solution)/shard_map/all_to_all | solution.py:34
  364.1 3.3 fusion.3
  368.6 9.9 %fusion.6 = f32[1024,2,704]{0,2,1:T(8,128)} fusion(bf16[1024,2048,1]{0,1,2:T(8,128)(2,1)S(1)} %bitcast.122, bf16[16,128,2,704]{1,3,2,0:T(8,128)(2,1)} %all-to-all-done.5), kind=kOutput, calls=%fused_computation.12 | convolution fusion | flops 5905580032 | bytes 15728640 | tf_op jit(solution)/shard_map/td,dgf->tgf/dot_general | solution.py:130
  378.5 15.2 %all-to-all-done.6 = bf16[16,704,128]{2,1,0:T(8,128)(2,1)S(1)} async-done(((bf16[16,704,128]{2,1,0:T(8,128)(2,1)}), bf16[16,704,128]{2,1,0:T(8,128)(2,1)S(1)}, u32[]{:S(2)}, u32[]{:S(2)}) %all-to-all-start.6) | async-done | bytes 2883616 | tf_op jit(solution)/shard_map/all_to_all | solution.py:34
  393.7 6.5 %convolution_convert_fusion = bf16[1024,2048]{1,0:T(8,128)(2,1)S(1)} fusion(f32[1024,2,704]{0,2,1:T(8,128)} %fusion.6, bf16[16,704,128]{2,1,0:T(8,128)(2,1)S(1)} %all-to-all-done.6), kind=kOutput, calls=%fused_computation.17 | convolution fusion | flops 2959212544 | bytes 12845056 | tf_op jit(solution)/shard_map/dot_general | solution.py:137
  400.5 52.5 %all_to_all.40 = bf16[1024,8,256]{2,0,1:T(8,128)(2,1)S(1)} all-to-all(bf16[1024,8,256]{2,0,1:T(8,128)(2,1)S(1)} %bitcast.117), channel_id=1, replica_groups=mesh['wide'=16,'head'=8] {'head'}, dimensions={1} | all-to-all | bytes 8388608 | tf_op jit(solution)/shard_map/all_to_all | solution.py:44
  (65 shorter events, 12.8 us)
Async XLA Ops:
  3.8 6.5 %copy-start.5 = (f32[128,768]{1,0:T(8,128)S(1)}, f32[128,768]{1,0:T(8,128)}, u32[]{:S(2)}) copy-start(f32[128,768]{1,0:T(8,128)} %param.15) | copy-start | bytes 1179652
  3.8 56.0 %all-to-all-start = ((bf16[8,1024,256]{1,2,0:T(8,128)(2,1)}), bf16[8,1024,256]{1,2,0:T(8,128)(2,1)}, u32[]{:S(2)}, u32[]{:S(2)}) async-start(bf16[8,1024,256]{1,2,0:T(8,128)(2,1)} %broadcast_in_dim.38), calls=%async_computation | async-start | bytes 8388608 | tf_op jit(solution)/shard_map/all_to_all | solution.py:34
  10.3 58.8 %copy-start.8 = (f32[2048]{0:T(1024)S(1)}, f32[2048]{0:T(1024)}, u32[]{:S(2)}) copy-start(f32[2048]{0:T(1024)} %param.14) | copy-start | bytes 24580
  10.3 58.8 %copy-start.11 = (f32[4,1,128]{2,1,0:T(1,128)S(1)}, f32[4,1,128]{2,1,0:T(1,128)}, u32[]{:S(2)}) copy-start(f32[4,1,128]{2,1,0:T(1,128)} %param.16) | copy-start | bytes 6148
  10.3 60.7 %copy-start.7 = (f32[256,128]{1,0:T(8,128)S(1)}, f32[256,128]{1,0:T(8,128)}, u32[]{:S(2)}) copy-start(f32[256,128]{1,0:T(8,128)} %param.18) | copy-start | bytes 393220
  10.3 61.5 %copy-start.12 = (s32[2]{0:T(128)S(1)}, s32[2]{0:T(128)}, u32[]{:S(2)}) copy-start(s32[2]{0:T(128)} %param.12) | copy-start | bytes 28
  10.3 63.4 %copy-start.10 = (s32[2,512]{1,0:T(2,128)S(1)}, s32[2,512]{1,0:T(2,128)}, u32[]{:S(2)}) copy-start(s32[2,512]{1,0:T(2,128)} %param.13) | copy-start | bytes 12292
  61.8 46.0 %all-to-all-start.1 = ((bf16[16,128,768]{2,1,0:T(8,128)(2,1)}), bf16[16,128,768]{2,1,0:T(8,128)(2,1)S(1)}, u32[]{:S(2)}, u32[]{:S(2)}) async-start(bf16[16,128,768]{2,1,0:T(8,128)(2,1)} %broadcast_in_dim.39), calls=%async_computation.1 | async-start | bytes 6291456 | tf_op jit(solution)/shard_map/all_to_all | solution.py:34
  107.9 2.0 copy-start.1
  109.8 26.4 %all-to-all-start.2 = ((bf16[16,256,128]{1,2,0:T(8,128)(2,1)}), bf16[16,256,128]{1,2,0:T(8,128)(2,1)S(1)}, u32[]{:S(2)}, u32[]{:S(2)}) async-start(bf16[16,256,128]{1,2,0:T(8,128)(2,1)} %broadcast_in_dim.43), calls=%async_computation.2 | async-start | bytes 2097152 | tf_op jit(solution)/shard_map/all_to_all | solution.py:34
  126.6 0.9 copy-start.4
  130.9 0.7 copy-start.13
  139.8 4.9 %copy-start.3 = (f32[128,2,704]{0,2,1:T(8,128)S(1)}, f32[128,2,704]{0,2,1:T(8,128)}, u32[]{:S(2)}) copy-start(f32[128,2,704]{0,2,1:T(8,128)} %param.20) | copy-start | bytes 2162692
  139.8 54.4 %all-to-all-start.3 = ((bf16[1024,8,256]{2,0,1:T(8,128)(2,1)}), bf16[1024,8,256]{2,0,1:T(8,128)(2,1)}, u32[]{:S(2)}, u32[]{:S(2)}) async-start(bf16[1024,8,256]{2,0,1:T(8,128)(2,1)} %bitcast.116), calls=%async_computation.3 | async-start | bytes 8388608 | tf_op jit(solution)/shard_map/all_to_all | solution.py:44
  198.0 73.2 %all-to-all-start.5 = ((bf16[16,128,2,704]{1,3,2,0:T(8,128)(2,1)}), bf16[16,128,2,704]{1,3,2,0:T(8,128)(2,1)}, u32[]{:S(2)}, u32[]{:S(2)}) async-start(bf16[16,128,2,704]{1,3,2,0:T(8,128)(2,1)} %broadcast_in_dim.45), calls=%async_computation.5 | async-start | bytes 11534336 | tf_op jit(solution)/shard_map/all_to_all | solution.py:34
  204.2 2.9 copy-start.2
  273.6 4.7 %copy-start.6 = (f32[704,128]{1,0:T(8,128)S(1)}, f32[704,128]{1,0:T(8,128)}, u32[]{:S(2)}) copy-start(f32[704,128]{1,0:T(8,128)} %param.21) | copy-start | bytes 1081348
  273.6 54.2 %all-to-all-start.4 = ((bf16[8,1024,256]{2,1,0:T(8,128)(2,1)}), bf16[8,1024,256]{2,1,0:T(8,128)(2,1)}, u32[]{:S(2)}, u32[]{:S(2)}) async-start(bf16[8,1024,256]{2,1,0:T(8,128)(2,1)} %broadcast_in_dim.44), calls=%async_computation.4 | async-start | bytes 8388608 | tf_op jit(solution)/shard_map/all_to_all | solution.py:34
  278.4 79.3 %copy-start.9 = (f32[2048]{0:T(1024)S(1)}, f32[2048]{0:T(1024)}, u32[]{:S(2)}) copy-start(f32[2048]{0:T(1024)} %param.19) | copy-start | bytes 24580
  329.9 63.8 %all-to-all-start.6 = ((bf16[16,704,128]{2,1,0:T(8,128)(2,1)}), bf16[16,704,128]{2,1,0:T(8,128)(2,1)S(1)}, u32[]{:S(2)}, u32[]{:S(2)}) async-start(bf16[16,704,128]{2,1,0:T(8,128)(2,1)} %broadcast_in_dim.46), calls=%async_computation.6 | async-start | bytes 5767168 | tf_op jit(solution)/shard_map/all_to_all | solution.py:34
  364.1 3.4 copy-start

commit v2 on v1

--- a/solution.py
+++ b/solution.py
@@ -84,7 +84,7 @@
     columns = normed
     joined = jnp.dot(
         columns,
-        gather_blocks(qkv_local, "wide", n_wide, 0),
+        lax.all_gather(qkv_local, "wide", axis=0, tiled=True),
         preferred_element_type=jnp.float32,
     )
     heads_here = qkv_local.shape[1] // width
@@ -118,7 +118,7 @@
     attn = jnp.concatenate(outputs, axis=0)
     mix_terms = jnp.dot(
         attn,
-        gather_blocks(out_weight.astype(jnp.bfloat16), "wide", n_wide, 1),
+        lax.all_gather(out_weight.astype(jnp.bfloat16), "wide", axis=1, tiled=True),
         preferred_element_type=jnp.float32,
     )
     mix = scatter_sum(mix_terms, "head", n_head)
@@ -130,13 +130,13 @@
     both = jnp.einsum(
         "td,dgf->tgf",
         columns,
-        gather_blocks(gate_up_local, "wide", n_wide, 0),
+        lax.all_gather(gate_up_local, "wide", axis=0, tiled=True),
         preferred_element_type=jnp.float32,
     )
     hidden = (jax.nn.silu(both[:, 0]) * both[:, 1]).astype(jnp.bfloat16)
     ffn_terms = jnp.dot(
         hidden,
-        gather_blocks(down_weight.astype(jnp.bfloat16), "wide", n_wide, 1),
+        lax.all_gather(down_weight.astype(jnp.bfloat16), "wide", axis=1, tiled=True),
         preferred_element_type=jnp.float32,
     )
     ffn = scatter_sum(ffn_terms, "head", n_head)

time: 459 us -> 353 us (0.77)
  waiting for transfers between devices: 257 us -> 134 us
  blocking collectives: 52.5 us -> 124 us
  starting transfers between devices: 67.7 us -> 11.3 us
  between operations: 1.69 us -> 14.7 us
  local copies, waits for them, and re-layouts: 27.5 us -> 14.9 us
    all_to_all x6 -> x2, waiting for transfers between devices: 208 us -> 111 us  [gather_blocks(): got = lax.all_to_all(spread, axis, 0, 0, tiled=True)]
    all_to_all x1 -> x2, blocking collectives: 52.5 us -> 124 us  [scatter_sum(): got = lax.all_to_all(parts, axis, 1, 1, tiled=True)]
    all_to_all x6 -> x2, starting transfers between devices: 62.9 us -> 11.2 us  [gather_blocks(): got = lax.all_to_all(spread, axis, 0, 0, tiled=True)]
    all_to_all x1 -> x0, waiting for transfers between devices: 49.5 us -> none  [scatter_sum(): got = lax.all_to_all(parts, axis, 1, 1, tiled=True)]
    all_gather x0 -> x4, waiting for transfers between devices: none -> 23.2 us  [the longest x1 23.2 us: body(): lax.all_gather(out_weight.astype(jnp.bfloat16), 'wide', axis=1, tiled=True)]
    broadcast_in_dim x6 -> x2, local copies, waits for them, and re-layouts: 14.8 us -> 4.96 us  [gather_blocks(): spread = jnp.broadcast_to(x[None], (n,) + x.shape)]
    all_to_all x1 -> x0, starting transfers between devices: 4.86 us -> none  [scatter_sum(): got = lax.all_to_all(parts, axis, 1, 1, tiled=True)]
  transfers between devices with their start and end apart: 7 -> 6, of which waited for: 7 -> 3; matrix products, arithmetic and copies ran while one was open for 10% -> 16% of each run, Pallas kernels for 0% -> 0%
where the time goes in v2:
time: 353 us
  waiting for transfers between devices  134 us (38%)
  blocking collectives  124 us (35%)
  matrix products  29.5 us (8%)
  other arithmetic  23.5 us (7%)
  local copies, waits for them, and re-layouts  14.9 us (4%)
  between operations  14.7 us (4%)
  starting transfers between devices  11.3 us (3%)
    all_to_all x2, blocking collectives, scatter_sum(): got = lax.all_to_all(parts, axis, 1, 1, tiled=True)  124 us
    all_to_all x2, waiting for transfers between devices, gather_blocks(): got = lax.all_to_all(spread, axis, 0, 0, tiled=True)  111 us
    all_gather x1, waiting for transfers between devices, body(): lax.all_gather(out_weight.astype(jnp.bfloat16), 'wide', axis=1, tiled=True)  23.2 us
    all_to_all x2, starting transfers between devices, gather_blocks(): got = lax.all_to_all(spread, axis, 0, 0, tiled=True)  11.2 us
    dot_general x1, matrix products, body(): jnp.einsum('td,dgf->tgf', columns, lax.all_gather(gate_up_local, 'wide',...  10.9 us
    dot_general x1, matrix products, body(): jnp.dot(hidden, lax.all_gather(down_weight.astype(jnp.bfloat16), 'wide',...  7.06 us
  transfers between devices with their start and end apart: 6, of which 3 were waited for; matrix products, arithmetic and copies ran while one was open for 16% of the time, Pallas kernels for 0%

profile of v2, /device:TPU:2, one launch (start us, length us, event | category | flops | bytes accessed | tf_op | source)
XLA Modules:
  0.0 352.6 jit_solution(14366745864308537554)
XLA Ops:
  6.5 1.7 convert_element_type.133
  8.3 1.2 copy.16
  9.5 2.6 broadcast_in_dim.26
  12.1 6.5 %all-to-all-start = ((bf16[8,1024,256]{1,2,0:T(8,128)(2,1)}), bf16[8,1024,256]{1,2,0:T(8,128)(2,1)}, u32[]{:S(2)}, u32[]{:S(2)}) async-start(bf16[8,1024,256]{1,2,0:T(8,128)(2,1)} %broadcast_in_dim.26), calls=%async_computation | async-start | bytes 8388608 | tf_op jit(solution)/shard_map/all_to_all | solution.py:34
  18.7 0.6 convert_element_type.142
  19.4 0.8 convert_element_type.152
  20.3 0.7 multiply_reduce_fusion.4
  22.3 0.6 fusion.59
  22.9 1.3 iota_compare_fusion.1
  24.2 1.0 multiply_cosine_fusion.1
  25.2 53.5 %all-to-all-done = bf16[8,1024,256]{1,2,0:T(8,128)(2,1)} async-done(((bf16[8,1024,256]{1,2,0:T(8,128)(2,1)}), bf16[8,1024,256]{1,2,0:T(8,128)(2,1)}, u32[]{:S(2)}, u32[]{:S(2)}) %all-to-all-start) | async-done | bytes 4194336 | tf_op jit(solution)/shard_map/all_to_all | solution.py:34
  78.7 3.1 multiply_reduce_fusion.1
  81.8 4.2 %fusion.3 = bf16[1024,2048]{0,1:T(8,128)(2,1)} fusion(f32[2048]{0:T(1024)S(1)} %copy-done.5, f32[1024]{0:T(1024)S(1)} %add_rsqrt_fusion.1, bf16[8,1024,256]{1,2,0:T(8,128)(2,1)} %all-to-all-done), kind=kLoop, calls=%fused_computation.5 | loop fusion | flops 8388608 | bytes 8400896 | tf_op jit(solution)/shard_map/convert_element_type | solution.py:82
  86.0 6.2 %fusion.64 = f32[1024,768]{0,1:T(8,128)S(1)} fusion(bf16[1024,2048]{0,1:T(8,128)(2,1)} %fusion.3, bf16[2048,768]{1,0:T(8,128)(2,1)} %all-gather.5.cloned.1.call-done), kind=kOutput, calls=%fused_computation.121 | convolution fusion | flops 3221225472 | bytes 10485760 | tf_op jit(solution)/shard_map/dot_general | solution.py:85
  95.5 0.6 multiply_reduce_fusion.2
  96.1 0.6 multiply_reduce_fusion.3
  97.0 23.2 %all-gather.7.cloned.1.call-done = bf16[256,2048]{1,0:T(8,128)(2,1)} async-done(((bf16[256,128]{1,0:T(8,128)(2,1)}), bf16[256,2048]{1,0:T(8,128)(2,1)}) %all-gather.7.cloned.1.call-update) | async-done | bytes 1048592 | tf_op jit(solution)/shard_map/all_gather | solution.py:121
  120.2 2.5 convolution_convert_fusion.1
  123.0 73.4 %all_to_all.20 = bf16[1024,8,256]{2,0,1:T(8,128)(2,1)S(1)} all-to-all(bf16[1024,8,256]{2,0,1:T(8,128)(2,1)S(1)} %bitcast.118), channel_id=1, replica_groups=mesh['wide'=16,'head'=8] {'head'}, dimensions={1} | all-to-all | bytes 8388608 | tf_op jit(solution)/shard_map/all_to_all | solution.py:44
  196.3 0.6 convert_reduce_fusion.1
  197.5 2.3 broadcast_in_dim.34
  199.9 4.7 %all-to-all-start.2 = ((bf16[8,1024,256]{2,1,0:T(8,128)(2,1)}), bf16[8,1024,256]{2,1,0:T(8,128)(2,1)}, u32[]{:S(2)}, u32[]{:S(2)}) async-start(bf16[8,1024,256]{2,1,0:T(8,128)(2,1)} %broadcast_in_dim.34), calls=%async_computation.2 | async-start | bytes 8388608 | tf_op jit(solution)/shard_map/all_to_all | solution.py:34
  204.6 0.7 convert_element_type.154
  205.3 57.6 %all-to-all-done.2 = bf16[8,1024,256]{2,1,0:T(8,128)(2,1)} async-done(((bf16[8,1024,256]{2,1,0:T(8,128)(2,1)}), bf16[8,1024,256]{2,1,0:T(8,128)(2,1)}, u32[]{:S(2)}, u32[]{:S(2)}) %all-to-all-start.2) | async-done | bytes 4194336 | tf_op jit(solution)/shard_map/all_to_all | solution.py:34
  262.9 6.4 %copy.18 = bf16[8,1024,256]{1,2,0:T(8,128)(2,1)} copy(bf16[8,1024,256]{2,1,0:T(8,128)(2,1)} %all-to-all-done.2) | data formatting | bytes 8388608 | tf_op jit(solution)/shard_map/all_to_all | solution.py:34
  269.4 3.3 multiply_reduce_fusion
  272.8 2.6 fusion.1
  275.4 10.9 %fusion.4 = f32[1024,2,704]{0,2,1:T(8,128)} fusion(bf16[2048,2,704]{0,2,1:T(8,128)(2,1)} %all-gather.9.cloned.1.call-done, bf16[1024,2048]{0,1:T(8,128)(2,1)} %fusion.1), kind=kOutput, calls=%fused_computation.12 | convolution fusion | flops 5905580032 | bytes 15728640 | tf_op jit(solution)/shard_map/td,dgf->tgf/dot_general | solution.py:130
  286.3 7.1 %convolution_convert_fusion = bf16[1024,2048]{1,0:T(8,128)(2,1)S(1)} fusion(bf16[704,2048]{1,0:T(8,128)(2,1)} %all-gather.11.cloned.1.call-done, f32[1024,2,704]{0,2,1:T(8,128)} %fusion.4), kind=kOutput, calls=%fused_computation.14 | convolution fusion | flops 2959212544 | bytes 12845056 | tf_op jit(solution)/shard_map/dot_general | solution.py:137
  293.7 50.9 %all_to_all.21 = bf16[1024,8,256]{2,0,1:T(8,128)(2,1)S(1)} all-to-all(bf16[1024,8,256]{2,0,1:T(8,128)(2,1)S(1)} %bitcast.119), channel_id=1, replica_groups=mesh['wide'=16,'head'=8] {'head'}, dimensions={1} | all-to-all | bytes 8388608 | tf_op jit(solution)/shard_map/all_to_all | solution.py:44
  344.6 0.6 convert_reduce_fusion
  345.2 0.9 add_convert_fusion
  (55 shorter events, 5.0 us)
Async XLA Ops:
  6.5 79.5 %all-gather.5.cloned.1.call-start = ((), (), s32[]{:S(2)}) async-start(), calls=%async_computation.4 | async-start | bytes 3342336 | tf_op jit(solution)/shard_map/all_gather | solution.py:87
  12.1 6.6 %copy-start.4 = (f32[256,128]{1,0:T(8,128)S(1)}, f32[256,128]{1,0:T(8,128)}, u32[]{:S(2)}) copy-start(f32[256,128]{1,0:T(8,128)} %param.18) | copy-start | bytes 393220
  12.1 7.3 %copy-start.2 = (f32[128,2,704]{0,2,1:T(8,128)S(1)}, f32[128,2,704]{0,2,1:T(8,128)}, u32[]{:S(2)}) copy-start(f32[128,2,704]{0,2,1:T(8,128)} %param.20) | copy-start | bytes 2162692
  12.1 8.1 %copy-start.8 = (f32[4,1,128]{2,1,0:T(1,128)S(1)}, f32[4,1,128]{2,1,0:T(1,128)}, u32[]{:S(2)}) copy-start(f32[4,1,128]{2,1,0:T(1,128)} %param.16) | copy-start | bytes 6148
  12.1 10.2 %copy-start.9 = (s32[2]{0:T(128)S(1)}, s32[2]{0:T(128)}, u32[]{:S(2)}) copy-start(s32[2]{0:T(128)} %param.12) | copy-start | bytes 28
  12.1 12.0 %copy-start.7 = (s32[2,512]{1,0:T(2,128)S(1)}, s32[2,512]{1,0:T(2,128)}, u32[]{:S(2)}) copy-start(s32[2,512]{1,0:T(2,128)} %param.13) | copy-start | bytes 12292
  12.1 66.6 %all-to-all-start = ((bf16[8,1024,256]{1,2,0:T(8,128)(2,1)}), bf16[8,1024,256]{1,2,0:T(8,128)(2,1)}, u32[]{:S(2)}, u32[]{:S(2)}) async-start(bf16[8,1024,256]{1,2,0:T(8,128)(2,1)} %broadcast_in_dim.26), calls=%async_computation | async-start | bytes 8388608 | tf_op jit(solution)/shard_map/all_to_all | solution.py:34
  18.6 63.2 %copy-start.5 = (f32[2048]{0:T(1024)S(1)}, f32[2048]{0:T(1024)}, u32[]{:S(2)}) copy-start(f32[2048]{0:T(1024)} %param.14) | copy-start | bytes 24580
  18.6 101.6 %all-gather.7.cloned.1.call-start = ((), (), s32[]{:S(2)}) async-start(), calls=%async_computation.5 | async-start | bytes 1114112 | tf_op jit(solution)/shard_map/all_gather | solution.py:121
  19.4 256.0 %all-gather.9.cloned.1.call-start = ((), (), s32[]{:S(2)}) async-start(), calls=%async_computation.6 | async-start | bytes 6127616 | tf_op jit(solution)/shard_map/all_gather | solution.py:133
  96.1 0.7 copy-start.10
  196.3 1.0 copy-start.1
  199.9 4.8 %copy-start.3 = (f32[704,128]{1,0:T(8,128)S(1)}, f32[704,128]{1,0:T(8,128)}, u32[]{:S(2)}) copy-start(f32[704,128]{1,0:T(8,128)} %param.21) | copy-start | bytes 1081348
  199.9 63.1 %all-to-all-start.2 = ((bf16[8,1024,256]{2,1,0:T(8,128)(2,1)}), bf16[8,1024,256]{2,1,0:T(8,128)(2,1)}, u32[]{:S(2)}, u32[]{:S(2)}) async-start(bf16[8,1024,256]{2,1,0:T(8,128)(2,1)} %broadcast_in_dim.34), calls=%async_computation.2 | async-start | bytes 8388608 | tf_op jit(solution)/shard_map/all_to_all | solution.py:34
  204.6 81.8 %all-gather.11.cloned.1.call-start = ((), (), s32[]{:S(2)}) async-start(), calls=%async_computation.7 | async-start | bytes 3063808 | tf_op jit(solution)/shard_map/all_gather | solution.py:139
  269.4 3.4 copy-start
  269.4 3.4 copy-start.6
Sparse Core Ops, SparseCore 0:
  9.7 64.1 all-gather.4
  76.1 44.0 all-gather.6
  122.5 82.1 all-gather.8
  207.3 60.5 all-gather.10

commit v3 on v2

--- a/solution.py
+++ b/solution.py
@@ -81,10 +81,19 @@
     full_rows = gather_blocks(tokens, "head", n_head, 1)
     normed = rms_scale(full_rows, attn_gain).astype(jnp.bfloat16)
     qkv_local = qkv_weight.astype(jnp.bfloat16)
+    qkv_cols = qkv_local.shape[1]
+    attn_pack = jnp.concatenate([qkv_local, out_weight.astype(jnp.bfloat16).T], axis=1)
+    attn_pack = lax.all_gather(attn_pack, "wide", axis=0, tiled=True)
+    gate_up_local = gate_up_weight.astype(jnp.bfloat16)
+    gu_shape = gate_up_local.shape
+    ffn_pack = jnp.concatenate(
+        [gate_up_local.reshape(gu_shape[0], -1), down_weight.astype(jnp.bfloat16).T], axis=1
+    )
+    ffn_pack = lax.all_gather(ffn_pack, "wide", axis=0, tiled=True)
     columns = normed
     joined = jnp.dot(
         columns,
-        lax.all_gather(qkv_local, "wide", axis=0, tiled=True),
+        attn_pack[:, :qkv_cols],
         preferred_element_type=jnp.float32,
     )
     heads_here = qkv_local.shape[1] // width
@@ -116,27 +125,29 @@
         )
         outputs.append(attended)
     attn = jnp.concatenate(outputs, axis=0)
-    mix_terms = jnp.dot(
+    mix_terms = lax.dot_general(
         attn,
-        lax.all_gather(out_weight.astype(jnp.bfloat16), "wide", axis=1, tiled=True),
+        attn_pack[:, qkv_cols:],
+        (((1,), (1,)), ((), ())),
         preferred_element_type=jnp.float32,
     )
     mix = scatter_sum(mix_terms, "head", n_head)
     middle = (tokens.astype(jnp.float32) + mix).astype(jnp.bfloat16)
     middle_full = gather_blocks(middle, "head", n_head, 1)
     normed2 = rms_scale(middle_full, ffn_gain).astype(jnp.bfloat16)
-    gate_up_local = gate_up_weight.astype(jnp.bfloat16)
     columns = normed2
+    gu_cols = gu_shape[1] * gu_shape[2]
     both = jnp.einsum(
         "td,dgf->tgf",
         columns,
-        lax.all_gather(gate_up_local, "wide", axis=0, tiled=True),
+        ffn_pack[:, :gu_cols].reshape(-1, gu_shape[1], gu_shape[2]),
         preferred_element_type=jnp.float32,
     )
     hidden = (jax.nn.silu(both[:, 0]) * both[:, 1]).astype(jnp.bfloat16)
-    ffn_terms = jnp.dot(
+    ffn_terms = lax.dot_general(
         hidden,
-        lax.all_gather(down_weight.astype(jnp.bfloat16), "wide", axis=1, tiled=True),
+        ffn_pack[:, gu_cols:],
+        (((1,), (1,)), ((), ())),
         preferred_element_type=jnp.float32,
     )
     ffn = scatter_sum(ffn_terms, "head", n_head)

time: 353 us -> 324 us (0.918)
  waiting for transfers between devices: 134 us -> 105 us
  matrix products: 29.5 us -> 24.7 us
    all_gather x4 -> x2, waiting for transfers between devices: 23.2 us -> 0.01 us  [the longest x1 0.01 us: body(): attn_pack = lax.all_gather(attn_pack, 'wide', axis=0, tiled=True)]
    all_to_all x2, waiting for transfers between devices: 111 us -> 105 us  [gather_blocks(): got = lax.all_to_all(spread, axis, 0, 0, tiled=True)]
    dot_general x4, matrix products: 26.7 us -> 21.9 us  [the longest x1 8.98 us: body(): jnp.einsum('td,dgf->tgf', columns, ffn_pack[:, :gu_cols].reshape(-1, gu_s...]
  transfers between devices with their start and end apart: 6 -> 4, of which waited for: 3 -> 2; matrix products, arithmetic and copies ran while one was open for 16% -> 14% of each run, Pallas kernels for 0% -> 0%
where the time goes in v3:
time: 324 us; the launch traced here: 323 us
  blocking collectives  127 us (39%)
  waiting for transfers between devices  105 us (32%)
  matrix products  24.7 us (8%)
  other arithmetic  22.9 us (7%)
  local copies, waits for them, and re-layouts  17.4 us (5%)
  between operations  15 us (5%)
  starting transfers between devices  11.2 us (3%)
    all_to_all x2, blocking collectives, scatter_sum(): got = lax.all_to_all(parts, axis, 1, 1, tiled=True)  127 us
    all_to_all x2, waiting for transfers between devices, gather_blocks(): got = lax.all_to_all(spread, axis, 0, 0, tiled=True)  105 us
    all_to_all x2, starting transfers between devices, gather_blocks(): got = lax.all_to_all(spread, axis, 0, 0, tiled=True)  11.2 us
    dot_general x1, matrix products, body(): jnp.einsum('td,dgf->tgf', columns, ffn_pack[:, :gu_cols].reshape(-1, gu_s...  8.98 us
    dot_general x1, matrix products, body(): jnp.dot(columns, attn_pack[:, :qkv_cols], preferred_element_type=jnp.floa...  6.52 us
  transfers between devices with their start and end apart: 4, of which 2 were waited for; matrix products, arithmetic and copies ran while one was open for 14% of the time, Pallas kernels for 0%

profile of v3, /device:TPU:2, one launch (start us, length us, event | category | flops | bytes accessed | tf_op | source)
XLA Modules:
  0.0 323.1 jit_solution(16716047884549979128)
XLA Ops:
  6.5 0.9 convert_bitcast_fusion.1
  7.6 1.0 convert_element_type.132
  8.6 0.7 pad_maximum_fusion.1
  9.3 1.2 copy.19
  10.6 2.5 broadcast_in_dim.26
  13.1 6.5 %all-to-all-start = ((bf16[8,1024,256]{1,2,0:T(8,128)(2,1)}), bf16[8,1024,256]{1,2,0:T(8,128)(2,1)}, u32[]{:S(2)}, u32[]{:S(2)}) async-start(bf16[8,1024,256]{1,2,0:T(8,128)(2,1)} %broadcast_in_dim.26), calls=%async_computation | async-start | bytes 8388608 | tf_op jit(solution)/shard_map/all_to_all | solution.py:34
  19.7 0.8 pad_maximum_fusion
  20.6 0.6 multiply_reduce_fusion.3
  22.5 0.6 fusion.62
  23.1 1.2 iota_compare_fusion.1
  24.3 1.0 multiply_cosine_fusion.1
  25.3 57.9 %all-to-all-done = bf16[8,1024,256]{1,2,0:T(8,128)(2,1)} async-done(((bf16[8,1024,256]{1,2,0:T(8,128)(2,1)}), bf16[8,1024,256]{1,2,0:T(8,128)(2,1)}, u32[]{:S(2)}, u32[]{:S(2)}) %all-to-all-start) | async-done | bytes 4194336 | tf_op jit(solution)/shard_map/all_to_all | solution.py:34
  83.2 3.1 multiply_reduce_fusion
  86.3 4.1 %fusion.4 = bf16[1024,2048]{0,1:T(8,128)(2,1)} fusion(f32[2048]{0:T(1024)S(1)} %copy-done.4, f32[1024]{0:T(1024)S(1)} %add_rsqrt_fusion.1, bf16[8,1024,256]{1,2,0:T(8,128)(2,1)} %all-to-all-done), kind=kLoop, calls=%fused_computation.7 | loop fusion | flops 8388608 | bytes 8400896 | tf_op jit(solution)/shard_map/convert_element_type | solution.py:82
  90.4 6.5 %fusion.5 = f32[1024,768]{0,1:T(8,128)S(1)} fusion(bf16[1024,2048]{0,1:T(8,128)(2,1)} %fusion.4, bf16[2048,1024]{1,0:T(8,128)(2,1)} %all-gather.3.cloned.1.call-done), kind=kOutput, calls=%fused_computation.15 | convolution fusion | flops 3221225472 | bytes 10485760 | tf_op jit(solution)/shard_map/dot_general | solution.py:94
  100.1 0.6 multiply_reduce_fusion.1
  100.7 0.6 multiply_reduce_fusion.2
  101.6 2.5 convolution_convert_fusion.1
  104.4 74.0 %all_to_all.20 = bf16[1024,8,256]{2,0,1:T(8,128)(2,1)S(1)} all-to-all(bf16[1024,8,256]{2,0,1:T(8,128)(2,1)S(1)} %bitcast.116), channel_id=1, replica_groups=mesh['wide'=16,'head'=8] {'head'}, dimensions={1} | all-to-all | bytes 8388608 | tf_op jit(solution)/shard_map/all_to_all | solution.py:44
  178.4 0.6 convert_reduce_fusion.1
  179.6 2.2 broadcast_in_dim.34
  181.8 4.7 %all-to-all-start.2 = ((bf16[8,1024,256]{2,1,0:T(8,128)(2,1)}), bf16[8,1024,256]{2,1,0:T(8,128)(2,1)}, u32[]{:S(2)}, u32[]{:S(2)}) async-start(bf16[8,1024,256]{2,1,0:T(8,128)(2,1)} %broadcast_in_dim.34), calls=%async_computation.2 | async-start | bytes 8388608 | tf_op jit(solution)/shard_map/all_to_all | solution.py:34
  186.5 47.3 %all-to-all-done.2 = bf16[8,1024,256]{2,1,0:T(8,128)(2,1)} async-done(((bf16[8,1024,256]{2,1,0:T(8,128)(2,1)}), bf16[8,1024,256]{2,1,0:T(8,128)(2,1)}, u32[]{:S(2)}, u32[]{:S(2)}) %all-to-all-start.2) | async-done | bytes 4194336 | tf_op jit(solution)/shard_map/all_to_all | solution.py:34
  233.8 6.4 %copy.22 = bf16[8,1024,256]{1,2,0:T(8,128)(2,1)} copy(bf16[8,1024,256]{2,1,0:T(8,128)(2,1)} %all-to-all-done.2) | data formatting | bytes 8388608 | tf_op jit(solution)/shard_map/all_to_all | solution.py:34
  240.2 3.3 %fusion = f32[1024]{0:T(1024)S(1)} fusion(bf16[8,1024,256]{1,2,0:T(8,128)(2,1)} %copy.22), kind=kLoop, calls=%fused_computation.2 | loop fusion | flops 6290432 | bytes 4198400 | tf_op jit(solution)/shard_map/reduce_sum | solution.py:15
  243.7 2.5 fusion.2
  246.2 2.6 slice-done.3
  248.8 9.0 %fusion.67 = f32[1024,2,704]{0,2,1:T(8,128)S(1)} fusion(bf16[1024,2048,1]{0,1,2:T(8,128)(2,1)} %bitcast.123, bf16[2048,2,704]{0,2,1:T(8,128)(2,1)S(1)} %bitcast.120), kind=kOutput, calls=%fused_computation.128 | convolution fusion | flops 5905580032 | bytes 15728640 | tf_op jit(solution)/shard_map/td,dgf->tgf/dot_general | solution.py:140
  257.8 3.9 %convolution_convert_fusion = bf16[1024,2048]{1,0:T(8,128)(2,1)S(1)} fusion(bf16[2048,2112]{0,1:T(8,128)(2,1)S(1)} %bitcast.119, f32[1024,2,704]{0,2,1:T(8,128)S(1)} %fusion.67), kind=kOutput, calls=%fused_computation.13 | convolution fusion | flops 2959212544 | bytes 12845056 | tf_op jit(solution)/shard_map/dot_general | solution.py:147
  262.0 52.7 %all_to_all.21 = bf16[1024,8,256]{2,0,1:T(8,128)(2,1)S(1)} all-to-all(bf16[1024,8,256]{2,0,1:T(8,128)(2,1)S(1)} %bitcast.117), channel_id=1, replica_groups=mesh['wide'=16,'head'=8] {'head'}, dimensions={1} | all-to-all | bytes 8388608 | tf_op jit(solution)/shard_map/all_to_all | solution.py:44
  314.7 0.6 convert_reduce_fusion
  315.3 0.9 add_convert_fusion
  (60 shorter events, 5.1 us)
Async XLA Ops:
  6.5 83.8 %all-gather.3.cloned.1.call-start = ((), (), s32[]{:S(2)}) async-start(), calls=%async_computation.4 | async-start | bytes 4456448 | tf_op jit(solution)/shard_map/all_gather | solution.py:86
  13.1 6.5 %copy-start.2 = (f32[128,2,704]{0,2,1:T(8,128)S(1)}, f32[128,2,704]{0,2,1:T(8,128)}, u32[]{:S(2)}) copy-start(f32[128,2,704]{0,2,1:T(8,128)} %param.20) | copy-start | bytes 2162692
  13.1 6.6 %copy-start.3 = (f32[704,128]{1,0:T(8,128)S(1)}, f32[704,128]{1,0:T(8,128)}, u32[]{:S(2)}) copy-start(f32[704,128]{1,0:T(8,128)} %param.21) | copy-start | bytes 1081348
  13.1 7.5 %copy-start.7 = (f32[4,1,128]{2,1,0:T(1,128)S(1)}, f32[4,1,128]{2,1,0:T(1,128)}, u32[]{:S(2)}) copy-start(f32[4,1,128]{2,1,0:T(1,128)} %param.16) | copy-start | bytes 6148
  13.1 9.4 %copy-start.8 = (s32[2]{0:T(128)S(1)}, s32[2]{0:T(128)}, u32[]{:S(2)}) copy-start(s32[2]{0:T(128)} %param.12) | copy-start | bytes 28
  13.1 11.2 %copy-start.6 = (s32[2,512]{1,0:T(2,128)S(1)}, s32[2,512]{1,0:T(2,128)}, u32[]{:S(2)}) copy-start(s32[2,512]{1,0:T(2,128)} %param.13) | copy-start | bytes 12292
  13.1 70.1 %all-to-all-start = ((bf16[8,1024,256]{1,2,0:T(8,128)(2,1)}), bf16[8,1024,256]{1,2,0:T(8,128)(2,1)}, u32[]{:S(2)}, u32[]{:S(2)}) async-start(bf16[8,1024,256]{1,2,0:T(8,128)(2,1)} %broadcast_in_dim.26), calls=%async_computation | async-start | bytes 8388608 | tf_op jit(solution)/shard_map/all_to_all | solution.py:34
  19.6 66.7 %copy-start.4 = (f32[2048]{0:T(1024)S(1)}, f32[2048]{0:T(1024)}, u32[]{:S(2)}) copy-start(f32[2048]{0:T(1024)} %param.14) | copy-start | bytes 24580
  19.6 226.6 %all-gather.5.cloned.1.call-start = ((), (), s32[]{:S(2)}) async-start(), calls=%async_computation.5 | async-start | bytes 9191424 | tf_op jit(solution)/shard_map/all_gather | solution.py:92
  100.7 0.7 copy-start.9
  178.4 1.0 copy-start.1
  181.8 4.7 %copy-start.5 = (f32[2048]{0:T(1024)S(1)}, f32[2048]{0:T(1024)}, u32[]{:S(2)}) copy-start(f32[2048]{0:T(1024)} %param.19) | copy-start | bytes 24580
  181.8 52.0 %all-to-all-start.2 = ((bf16[8,1024,256]{2,1,0:T(8,128)(2,1)}), bf16[8,1024,256]{2,1,0:T(8,128)(2,1)}, u32[]{:S(2)}, u32[]{:S(2)}) async-start(bf16[8,1024,256]{2,1,0:T(8,128)(2,1)} %broadcast_in_dim.34), calls=%async_computation.2 | async-start | bytes 8388608 | tf_op jit(solution)/shard_map/all_to_all | solution.py:34
  240.2 3.4 %copy-start = (bf16[8,1024,256]{1,2,0:T(8,128)(2,1)S(1)}, bf16[8,1024,256]{1,2,0:T(8,128)(2,1)}, u32[]{:S(2)}) copy-start(bf16[8,1024,256]{1,2,0:T(8,128)(2,1)} %copy.22) | copy-start | bytes 12582916
  246.2 2.6 slice-start.3
  246.2 11.6 %slice-start = ((s8[8650752]{0:T(1024)(128)(4,1)}), s8[4194304]{0:T(1024)(128)(4,1)S(1)}, s32[]{:S(2)}) async-start(s8[8650752]{0:T(1024)(128)(4,1)} %bitcast.118), calls=%async_computation.6 | async-start | bytes 8388608
  248.8 9.0 %slice-start.1 = ((s8[8650752]{0:T(1024)(128)(4,1)}), s8[4194304]{0:T(1024)(128)(4,1)S(1)}, s32[]{:S(2)}) async-start(s8[8650752]{0:T(1024)(128)(4,1)} %bitcast.118), calls=%async_computation.7 | async-start | bytes 8388608
  248.8 9.0 %slice-start.2 = ((s8[8650752]{0:T(1024)(128)(4,1)}), s8[262144]{0:T(1024)(128)(4,1)S(1)}, s32[]{:S(2)}) async-start(s8[8650752]{0:T(1024)(128)(4,1)} %bitcast.118), calls=%async_computation.8 | async-start | bytes 524288
Sparse Core Ops, SparseCore 0:
  9.7 71.2 all-gather.2
  83.3 102.7 all-gather.4

commit v4 on v3

--- a/solution.py
+++ b/solution.py
@@ -77,81 +77,71 @@
     slots = positions.shape[1]
     width = 4 * HALF + VDIM
     n_head = lax.axis_size("head")
-    n_wide = lax.axis_size("wide")
-    full_rows = gather_blocks(tokens, "head", n_head, 1)
-    normed = rms_scale(full_rows, attn_gain).astype(jnp.bfloat16)
     qkv_local = qkv_weight.astype(jnp.bfloat16)
     qkv_cols = qkv_local.shape[1]
+    heads_here = qkv_cols // width
     attn_pack = jnp.concatenate([qkv_local, out_weight.astype(jnp.bfloat16).T], axis=1)
     attn_pack = lax.all_gather(attn_pack, "wide", axis=0, tiled=True)
     gate_up_local = gate_up_weight.astype(jnp.bfloat16)
     gu_shape = gate_up_local.shape
+    gu_cols = gu_shape[1] * gu_shape[2]
     ffn_pack = jnp.concatenate(
         [gate_up_local.reshape(gu_shape[0], -1), down_weight.astype(jnp.bfloat16).T], axis=1
     )
     ffn_pack = lax.all_gather(ffn_pack, "wide", axis=0, tiled=True)
-    columns = normed
-    joined = jnp.dot(
-        columns,
-        attn_pack[:, :qkv_cols],
-        preferred_element_type=jnp.float32,
-    )
-    heads_here = qkv_local.shape[1] // width
     balance = (
         jnp.exp(jnp.sum(lambdas[0] * lambdas[1], -1))
         - jnp.exp(jnp.sum(lambdas[2] * lambdas[3], -1))
         + lambda_base
     )
-    outputs = []
+    results = []
     for prompt in range(prompts_here):
-        block = joined[prompt * slots : (prompt + 1) * slots].reshape(slots, heads_here, width)
+        stream = tokens[prompt * slots : (prompt + 1) * slots]
+        full_rows = gather_blocks(stream, "head", n_head, 1)
+        normed = rms_scale(full_rows, attn_gain).astype(jnp.bfloat16)
+        joined = jnp.dot(normed, attn_pack[:, :qkv_cols], preferred_element_type=jnp.float32)
+        block = joined.reshape(slots, heads_here, width)
         quads = rotate(
             block[..., : 4 * HALF].reshape(slots, heads_here, 4, HALF), positions[prompt]
         ).astype(jnp.bfloat16)
         values = block[..., 4 * HALF :].astype(jnp.bfloat16)
-        length = lengths[prompt]
-        first_k = quads[:, :, 2]
-        second_k = quads[:, :, 3]
-        attended = diff_attend(
+        attn = diff_attend(
             quads[:, :, 0],
             quads[:, :, 1],
-            first_k,
-            second_k,
+            quads[:, :, 2],
+            quads[:, :, 3],
             values,
             jnp.arange(slots, dtype=jnp.int32),
-            length,
+            lengths[prompt],
             balance,
             sub_gain,
         )
-        outputs.append(attended)
-    attn = jnp.concatenate(outputs, axis=0)
-    mix_terms = lax.dot_general(
-        attn,
-        attn_pack[:, qkv_cols:],
-        (((1,), (1,)), ((), ())),
-        preferred_element_type=jnp.float32,
-    )
-    mix = scatter_sum(mix_terms, "head", n_head)
-    middle = (tokens.astype(jnp.float32) + mix).astype(jnp.bfloat16)
-    middle_full = gather_blocks(middle, "head", n_head, 1)
-    normed2 = rms_scale(middle_full, ffn_gain).astype(jnp.bfloat16)
-    columns = normed2
-    gu_cols = gu_shape[1] * gu_shape[2]
-    both = jnp.einsum(
-        "td,dgf->tgf",
-        columns,
-        ffn_pack[:, :gu_cols].reshape(-1, gu_shape[1], gu_shape[2]),
-        preferred_element_type=jnp.float32,
-    )
-    hidden = (jax.nn.silu(both[:, 0]) * both[:, 1]).astype(jnp.bfloat16)
-    ffn_terms = lax.dot_general(
-        hidden,
-        ffn_pack[:, gu_cols:],
-        (((1,), (1,)), ((), ())),
-        preferred_element_type=jnp.float32,
-    )
-    ffn = scatter_sum(ffn_terms, "head", n_head)
-    return (middle.astype(jnp.float32) + ffn).astype(jnp.bfloat16)
+        mix_terms = lax.dot_general(
+            attn,
+            attn_pack[:, qkv_cols:],
+            (((1,), (1,)), ((), ())),
+            preferred_element_type=jnp.float32,
+        )
+        mix = scatter_sum(mix_terms, "head", n_head)
+        middle = (stream.astype(jnp.float32) + mix).astype(jnp.bfloat16)
+        middle_full = gather_blocks(middle, "head", n_head, 1)
+        normed2 = rms_scale(middle_full, ffn_gain).astype(jnp.bfloat16)
+        both = jnp.einsum(
+            "td,dgf->tgf",
+            normed2,
+            ffn_pack[:, :gu_cols].reshape(-1, gu_shape[1], gu_shape[2]),
+            preferred_element_type=jnp.float32,
+        )
+        hidden = (jax.nn.silu(both[:, 0]) * both[:, 1]).astype(jnp.bfloat16)
+        ffn_terms = lax.dot_general(
+            hidden,
+            ffn_pack[:, gu_cols:],
+            (((1,), (1,)), ((), ())),
+            preferred_element_type=jnp.float32,
+        )
+        ffn = scatter_sum(ffn_terms, "head", n_head)
+        results.append((middle.astype(jnp.float32) + ffn).astype(jnp.bfloat16))
+    return jnp.concatenate(results, axis=0)
 
 
 def solution(mesh):

time: 324 us -> 345 us (1.065)
  blocking collectives: 127 us -> 29.7 us
  waiting for transfers between devices: 105 us -> 177 us
  starting transfers between devices: 11.2 us -> 31.9 us
  local copies, waits for them, and re-layouts: 17.4 us -> 28.9 us
  matrix products: 24.7 us -> 34.6 us
    all_to_all x0 -> x4, waiting for transfers between devices: none -> 104 us  [scatter_sum(): got = lax.all_to_all(parts, axis, 1, 1, tiled=True)]
    all_to_all x2 -> x1, blocking collectives: 127 us -> 29.7 us  [gather_blocks(): got = lax.all_to_all(spread, axis, 0, 0, tiled=True)]
    all_to_all x2 -> x3, waiting for transfers between devices: 105 us -> 72.9 us  [gather_blocks(): got = lax.all_to_all(spread, axis, 0, 0, tiled=True)]
    all_to_all x0 -> x4, starting transfers between devices: none -> 16.4 us  [scatter_sum(): got = lax.all_to_all(parts, axis, 1, 1, tiled=True)]
    reshape x2 -> x4, local copies, waits for them, and re-layouts: 0.54 us -> 5.95 us  [scatter_sum(): parts = terms.astype(jnp.bfloat16).reshape(rows, n, cols // n)]
    all_to_all x2 -> x3, starting transfers between devices: 11.2 us -> 15.4 us  [gather_blocks(): got = lax.all_to_all(spread, axis, 0, 0, tiled=True)]
    dot_general x1 -> x2, matrix products: 3.9 us -> 7.49 us  [body(): lax.dot_general(hidden, ffn_pack[:, gu_cols:], (((1,), (1,)), ((), ())),...]
    dot_general x2 -> x4, matrix products: 15.5 us -> 17.9 us  [the longest x2 9.08 us: body(): jnp.einsum('td,dgf->tgf', normed2, ffn_pack[:, :gu_cols].reshape(-1, gu_s...]
  transfers between devices with their start and end apart: 4 -> 9, of which waited for: 2 -> 7; matrix products, arithmetic and copies ran while one was open for 14% -> 20% of each run, Pallas kernels for 0% -> 0%
where the time goes in v4:
time: 345 us; the launch traced here: 343 us
  waiting for transfers between devices  177 us (51%)
  matrix products  34.6 us (10%)
  starting transfers between devices  31.9 us (9%)
  blocking collectives  29.7 us (9%)
  local copies, waits for them, and re-layouts  28.9 us (8%)
  other arithmetic  26.3 us (8%)
  between operations  15.2 us (4%)
    all_to_all x4, waiting for transfers between devices, scatter_sum(): got = lax.all_to_all(parts, axis, 1, 1, tiled=True)  104 us
    all_to_all x3, waiting for transfers between devices, gather_blocks(): got = lax.all_to_all(spread, axis, 0, 0, tiled=True)  72.9 us
    all_to_all x1, blocking collectives, gather_blocks(): got = lax.all_to_all(spread, axis, 0, 0, tiled=True)  29.7 us
    all_to_all x4, starting transfers between devices, scatter_sum(): got = lax.all_to_all(parts, axis, 1, 1, tiled=True)  16.4 us
    all_to_all x3, starting transfers between devices, gather_blocks(): got = lax.all_to_all(spread, axis, 0, 0, tiled=True)  15.4 us
    dot_general x2, matrix products, body(): jnp.einsum('td,dgf->tgf', normed2, ffn_pack[:, :gu_cols].reshape(-1, gu_s...  9.08 us
    dot_general x2, matrix products, body(): jnp.dot(normed, attn_pack[:, :qkv_cols], preferred_element_type=jnp.float32)  8.81 us
    dot_general x2, matrix products, body(): lax.dot_general(hidden, ffn_pack[:, gu_cols:], (((1,), (1,)), ((), ())),...  7.49 us
  transfers between devices with their start and end apart: 9, of which 7 were waited for; matrix products, arithmetic and copies ran while one was open for 20% of the time, Pallas kernels for 0%

profile of v4, /device:TPU:2, one launch (start us, length us, event | category | flops | bytes accessed | tf_op | source)
XLA Modules:
  0.0 343.1 jit_solution(360155306441928842)
XLA Ops:
  12.1 6.5 %all-to-all-start.4 = ((bf16[8,512,256]{1,2,0:T(8,128)(2,1)}), bf16[8,512,256]{1,2,0:T(8,128)(2,1)S(1)}, u32[]{:S(2)}, u32[]{:S(2)}) async-start(bf16[8,512,256]{1,2,0:T(8,128)(2,1)} %broadcast_in_dim.39), calls=%async_computation.4 | async-start | bytes 4194304 | tf_op jit(solution)/shard_map/all_to_all | solution.py:34
  20.7 27.6 %all-to-all-done.4 = bf16[8,512,256]{1,2,0:T(8,128)(2,1)S(1)} async-done(((bf16[8,512,256]{1,2,0:T(8,128)(2,1)}), bf16[8,512,256]{1,2,0:T(8,128)(2,1)S(1)}, u32[]{:S(2)}, u32[]{:S(2)}) %all-to-all-start.4) | async-done | bytes 2097184 | tf_op jit(solution)/shard_map/all_to_all | solution.py:34
  49.8 4.5 %all-to-all-start = ((bf16[8,512,256]{1,2,0:T(8,128)(2,1)}), bf16[8,512,256]{1,2,0:T(8,128)(2,1)}, u32[]{:S(2)}, u32[]{:S(2)}) async-start(bf16[8,512,256]{1,2,0:T(8,128)(2,1)} %broadcast_in_dim.34), calls=%async_computation | async-start | bytes 4194304 | tf_op jit(solution)/shard_map/all_to_all | solution.py:34
  57.7 3.0 multiply_cosine_fusion.1
  61.1 22.5 %all-to-all-done = bf16[8,512,256]{1,2,0:T(8,128)(2,1)} async-done(((bf16[8,512,256]{1,2,0:T(8,128)(2,1)}), bf16[8,512,256]{1,2,0:T(8,128)(2,1)}, u32[]{:S(2)}, u32[]{:S(2)}) %all-to-all-start) | async-done | bytes 2097184 | tf_op jit(solution)/shard_map/all_to_all | solution.py:34
  83.7 2.2 multiply_reduce_fusion.1
  85.9 3.8 %fusion.9 = (bf16[512,2048]{0,1:T(8,128)(2,1)}, bf16[512,2048]{0,1:T(8,128)(2,1)}) fusion(f32[2048]{0:T(1024)S(1)} %copy-done.10, f32[512]{0:T(512)S(1)} %add_rsqrt_fusion.5, bf16[8,512,256]{1,2,0:T(8,128)(2,1)} %all-to-all-done, f32[512]{0:T(512)S(1)} %add_rsqrt_fusion.2, bf16[8,512,256]{1,2,0:T(8,128)(2,1)S(1)} %all-to-all-done.4), kind=kLoop, calls=%fused_computation.15 | loop fusion | flops 8388608 | bytes 8400896 | tf_op jit(solution)/shard_map/convert_element_type | solution.py:101
  89.6 4.4 %fusion.16 = f32[512,1,768]{2,0,1:T(8,128)S(1)} fusion(bf16[512,2048]{0,1:T(8,128)(2,1)} %get-tuple-element.21, bf16[2048,1024]{1,0:T(8,128)(2,1)} %all-gather.3.cloned.1.call-done), kind=kOutput, calls=%fused_computation.36 | convolution fusion | flops 1610612736 | bytes 6815744 | tf_op jit(solution)/shard_map/dot_general | solution.py:102
  95.7 4.4 %fusion.19 = f32[512,1,768]{2,0,1:T(8,128)S(1)} fusion(bf16[512,2048]{0,1:T(8,128)(2,1)} %get-tuple-element.22, bf16[2048,1024]{1,0:T(8,128)(2,1)} %all-gather.3.cloned.1.call-done), kind=kOutput, calls=%fused_computation.37 | convolution fusion | flops 1610612736 | bytes 6815744 | tf_op jit(solution)/shard_map/dot_general | solution.py:102
  107.0 2.1 convolution_convert_fusion
  110.6 3.8 %all-to-all-start.5 = ((bf16[512,8,256]{2,0,1:T(8,128)(2,1)}), bf16[512,8,256]{2,0,1:T(8,128)(2,1)S(1)}, u32[]{:S(2)}, u32[]{:S(2)}) async-start(bf16[512,8,256]{2,0,1:T(8,128)(2,1)} %bitcast.155), calls=%async_computation.5 | async-start | bytes 4194304 | tf_op jit(solution)/shard_map/all_to_all | solution.py:44
  117.9 2.1 convolution_convert_fusion.1
  121.5 36.9 %all-to-all-done.5 = bf16[512,8,256]{2,0,1:T(8,128)(2,1)S(1)} async-done(((bf16[512,8,256]{2,0,1:T(8,128)(2,1)}), bf16[512,8,256]{2,0,1:T(8,128)(2,1)S(1)}, u32[]{:S(2)}, u32[]{:S(2)}) %all-to-all-start.5) | async-done | bytes 2097184 | tf_op jit(solution)/shard_map/all_to_all | solution.py:44
  158.4 4.4 %all-to-all-start.1 = ((bf16[512,8,256]{2,0,1:T(8,128)(2,1)}), bf16[512,8,256]{2,0,1:T(8,128)(2,1)}, u32[]{:S(2)}, u32[]{:S(2)}) async-start(bf16[512,8,256]{2,0,1:T(8,128)(2,1)} %bitcast.158), calls=%async_computation.1 | async-start | bytes 4194304 | tf_op jit(solution)/shard_map/all_to_all | solution.py:44
  163.1 26.7 %all-to-all-done.1 = bf16[512,8,256]{2,0,1:T(8,128)(2,1)} async-done(((bf16[512,8,256]{2,0,1:T(8,128)(2,1)}), bf16[512,8,256]{2,0,1:T(8,128)(2,1)}, u32[]{:S(2)}, u32[]{:S(2)}) %all-to-all-start.1) | async-done | bytes 2097184 | tf_op jit(solution)/shard_map/all_to_all | solution.py:44
  189.9 1.9 convert_reduce_fusion.3
  192.1 29.7 %all_to_all.40 = bf16[8,512,256]{2,1,0:T(8,128)(2,1)} all-to-all(bf16[8,512,256]{2,1,0:T(8,128)(2,1)S(1)} %broadcast_in_dim.40), channel_id=1, replica_groups=mesh['wide'=16,'head'=8] {'head'}, dimensions={0} | all-to-all | bytes 4194304 | tf_op jit(solution)/shard_map/all_to_all | solution.py:34
  223.2 4.5 %all-to-all-start.2 = ((bf16[8,512,256]{2,1,0:T(8,128)(2,1)}), bf16[8,512,256]{2,1,0:T(8,128)(2,1)}, u32[]{:S(2)}, u32[]{:S(2)}) async-start(bf16[8,512,256]{2,1,0:T(8,128)(2,1)} %broadcast_in_dim.37), calls=%async_computation.2 | async-start | bytes 4194304 | tf_op jit(solution)/shard_map/all_to_all | solution.py:34
  227.7 2.9 copy.43
  230.6 22.8 %all-to-all-done.2 = bf16[8,512,256]{2,1,0:T(8,128)(2,1)} async-done(((bf16[8,512,256]{2,1,0:T(8,128)(2,1)}), bf16[8,512,256]{2,1,0:T(8,128)(2,1)}, u32[]{:S(2)}, u32[]{:S(2)}) %all-to-all-start.2) | async-done | bytes 2097184 | tf_op jit(solution)/shard_map/all_to_all | solution.py:34
  253.4 3.9 %copy.36 = bf16[8,512,256]{1,2,0:T(8,128)(2,1)} copy(bf16[8,512,256]{2,1,0:T(8,128)(2,1)} %all-to-all-done.2) | data formatting | bytes 4194304 | tf_op jit(solution)/shard_map/all_to_all | solution.py:34
  259.4 2.5 fusion.2
  261.9 3.3 slice.154
  265.2 3.3 fusion.102
  268.5 3.7 %convolution_convert_fusion.3 = bf16[512,2048]{1,0:T(8,128)(2,1)S(1)} fusion(bf16[2048,2112]{0,1:T(8,128)(2,1)} %all-gather.5.cloned.1.call-done, f32[512,2,704]{0,2,1:T(8,128)S(1)} %fusion.102), kind=kOutput, calls=%fused_computation.25 | convolution fusion | flops 1479606272 | bytes 7864320 | tf_op jit(solution)/shard_map/dot_general | solution.py:136
  273.8 3.8 %all-to-all-start.3 = ((bf16[512,8,256]{2,0,1:T(8,128)(2,1)}), bf16[512,8,256]{2,0,1:T(8,128)(2,1)S(1)}, u32[]{:S(2)}, u32[]{:S(2)}) async-start(bf16[512,8,256]{2,0,1:T(8,128)(2,1)} %bitcast.157), calls=%async_computation.3 | async-start | bytes 4194304 | tf_op jit(solution)/shard_map/all_to_all | solution.py:44
  277.6 5.8 %fusion.103 = f32[512,2,704]{0,2,1:T(8,128)S(1)} fusion(bf16[512,2048,1]{0,1,2:T(8,128)(2,1)} %bitcast.163, bf16[2048,2,704]{0,2,1:T(8,128)(2,1)} %bitcast.162), kind=kOutput, calls=%fused_computation.172 | convolution fusion | flops 2952790016 | bytes 10747904 | tf_op jit(solution)/shard_map/td,dgf->tgf/dot_general | solution.py:129
  283.4 3.7 %convolution_convert_fusion.2 = bf16[512,2048]{1,0:T(8,128)(2,1)S(1)} fusion(bf16[2048,2112]{0,1:T(8,128)(2,1)} %all-gather.5.cloned.1.call-done, f32[512,2,704]{0,2,1:T(8,128)S(1)} %fusion.103), kind=kOutput, calls=%fused_computation.24 | convolution fusion | flops 1479606272 | bytes 7864320 | tf_op jit(solution)/shard_map/dot_general | solution.py:136
  288.7 14.9 %all-to-all-done.3 = bf16[512,8,256]{2,0,1:T(8,128)(2,1)S(1)} async-done(((bf16[512,8,256]{2,0,1:T(8,128)(2,1)}), bf16[512,8,256]{2,0,1:T(8,128)(2,1)S(1)}, u32[]{:S(2)}, u32[]{:S(2)}) %all-to-all-start.3) | async-done | bytes 2097184 | tf_op jit(solution)/shard_map/all_to_all | solution.py:44
  303.6 4.4 %all-to-all-start.7 = ((bf16[512,8,256]{2,0,1:T(8,128)(2,1)}), bf16[512,8,256]{2,0,1:T(8,128)(2,1)}, u32[]{:S(2)}, u32[]{:S(2)}) async-start(bf16[512,8,256]{2,0,1:T(8,128)(2,1)} %bitcast.156), calls=%async_computation.7 | async-start | bytes 4194304 | tf_op jit(solution)/shard_map/all_to_all | solution.py:44
  308.3 25.2 %all-to-all-done.7 = bf16[512,8,256]{2,0,1:T(8,128)(2,1)} async-done(((bf16[512,8,256]{2,0,1:T(8,128)(2,1)}), bf16[512,8,256]{2,0,1:T(8,128)(2,1)}, u32[]{:S(2)}, u32[]{:S(2)}) %all-to-all-start.7) | async-done | bytes 2097184 | tf_op jit(solution)/shard_map/all_to_all | solution.py:44
  333.5 1.9 convert_reduce_fusion
  (95 shorter events, 34.9 us)
Async XLA Ops:
  6.5 83.1 %all-gather.3.cloned.1.call-start = ((), (), s32[]{:S(2)}) async-start(), calls=%async_computation.8 | async-start | bytes 4456448 | tf_op jit(solution)/shard_map/all_gather | solution.py:84
  12.1 6.5 %copy-start.7 = (f32[128,2,704]{0,2,1:T(8,128)S(1)}, f32[128,2,704]{0,2,1:T(8,128)}, u32[]{:S(2)}) copy-start(f32[128,2,704]{0,2,1:T(8,128)} %param.20) | copy-start | bytes 2162692
  12.1 36.2 %all-to-all-start.4 = ((bf16[8,512,256]{1,2,0:T(8,128)(2,1)}), bf16[8,512,256]{1,2,0:T(8,128)(2,1)S(1)}, u32[]{:S(2)}, u32[]{:S(2)}) async-start(bf16[8,512,256]{1,2,0:T(8,128)(2,1)} %broadcast_in_dim.39), calls=%async_computation.4 | async-start | bytes 4194304 | tf_op jit(solution)/shard_map/all_to_all | solution.py:34
  18.5 243.4 %all-gather.5.cloned.1.call-start = ((), (), s32[]{:S(2)}) async-start(), calls=%async_computation.9 | async-start | bytes 9191424 | tf_op jit(solution)/shard_map/all_gather | solution.py:91
  49.8 4.5 %copy-start.14 = (f32[4,1,128]{2,1,0:T(1,128)S(1)}, f32[4,1,128]{2,1,0:T(1,128)}, u32[]{:S(2)}) copy-start(f32[4,1,128]{2,1,0:T(1,128)} %param.16) | copy-start | bytes 6148
  49.8 6.5 %copy-start.15 = (s32[2]{0:T(128)S(1)}, s32[2]{0:T(128)}, u32[]{:S(2)}) copy-start(s32[2]{0:T(128)} %param.12) | copy-start | bytes 28
  49.8 7.9 %copy-start.12 = (s32[2,512]{1,0:T(2,128)S(1)}, s32[2,512]{1,0:T(2,128)}, u32[]{:S(2)}) copy-start(s32[2,512]{1,0:T(2,128)} %param.13) | copy-start | bytes 12292
  49.8 33.9 %all-to-all-start = ((bf16[8,512,256]{1,2,0:T(8,128)(2,1)}), bf16[8,512,256]{1,2,0:T(8,128)(2,1)}, u32[]{:S(2)}, u32[]{:S(2)}) async-start(bf16[8,512,256]{1,2,0:T(8,128)(2,1)} %broadcast_in_dim.34), calls=%async_computation | async-start | bytes 4194304 | tf_op jit(solution)/shard_map/all_to_all | solution.py:34
  60.6 25.2 %copy-start.10 = (f32[2048]{0:T(1024)S(1)}, f32[2048]{0:T(1024)}, u32[]{:S(2)}) copy-start(f32[2048]{0:T(1024)} %param.14) | copy-start | bytes 24580
  94.0 1.2 copy-start.8
  100.1 1.2 copy-start.9
  102.4 1.0 copy-start.4
  102.4 1.0 copy-start.5
  102.4 1.1 copy-start.6
  105.3 1.7 copy-start.13
  110.6 47.8 %all-to-all-start.5 = ((bf16[512,8,256]{2,0,1:T(8,128)(2,1)}), bf16[512,8,256]{2,0,1:T(8,128)(2,1)S(1)}, u32[]{:S(2)}, u32[]{:S(2)}) async-start(bf16[512,8,256]{2,0,1:T(8,128)(2,1)} %bitcast.155), calls=%async_computation.5 | async-start | bytes 4194304 | tf_op jit(solution)/shard_map/all_to_all | solution.py:44
  158.4 31.5 %all-to-all-start.1 = ((bf16[512,8,256]{2,0,1:T(8,128)(2,1)}), bf16[512,8,256]{2,0,1:T(8,128)(2,1)}, u32[]{:S(2)}, u32[]{:S(2)}) async-start(bf16[512,8,256]{2,0,1:T(8,128)(2,1)} %bitcast.158), calls=%async_computation.1 | async-start | bytes 4194304 | tf_op jit(solution)/shard_map/all_to_all | solution.py:44
  163.1 28.7 %copy-start.3 = (bf16[1024,256]{1,0:T(8,128)(2,1)S(1)}, bf16[1024,256]{1,0:T(8,128)(2,1)}, u32[]{:S(2)}) copy-start(bf16[1024,256]{1,0:T(8,128)(2,1)} %param.11) | copy-start | bytes 1572868
  223.2 4.5 %copy-start.11 = (f32[2048]{0:T(1024)S(1)}, f32[2048]{0:T(1024)}, u32[]{:S(2)}) copy-start(f32[2048]{0:T(1024)} %param.19) | copy-start | bytes 24580
  223.2 30.2 %all-to-all-start.2 = ((bf16[8,512,256]{2,1,0:T(8,128)(2,1)}), bf16[8,512,256]{2,1,0:T(8,128)(2,1)}, u32[]{:S(2)}, u32[]{:S(2)}) async-start(bf16[8,512,256]{2,1,0:T(8,128)(2,1)} %broadcast_in_dim.37), calls=%async_computation.2 | async-start | bytes 4194304 | tf_op jit(solution)/shard_map/all_to_all | solution.py:34
  257.3 1.6 copy-start
  261.9 3.3 copy-start.2
  265.2 3.3 copy-start.1
  273.8 29.8 %all-to-all-start.3 = ((bf16[512,8,256]{2,0,1:T(8,128)(2,1)}), bf16[512,8,256]{2,0,1:T(8,128)(2,1)S(1)}, u32[]{:S(2)}, u32[]{:S(2)}) async-start(bf16[512,8,256]{2,0,1:T(8,128)(2,1)} %bitcast.157), calls=%async_computation.3 | async-start | bytes 4194304 | tf_op jit(solution)/shard_map/all_to_all | solution.py:44
  303.6 29.9 %all-to-all-start.7 = ((bf16[512,8,256]{2,0,1:T(8,128)(2,1)}), bf16[512,8,256]{2,0,1:T(8,128)(2,1)}, u32[]{:S(2)}, u32[]{:S(2)}) async-start(bf16[512,8,256]{2,0,1:T(8,128)(2,1)} %bitcast.156), calls=%async_computation.7 | async-start | bytes 4194304 | tf_op jit(solution)/shard_map/all_to_all | solution.py:44
Sparse Core Ops, SparseCore 0:
  9.7 62.4 all-gather.2
  74.5 94.7 all-gather.4

commit v5 on v3

--- a/solution.py
+++ b/solution.py
@@ -133,12 +133,14 @@
     )
     mix = scatter_sum(mix_terms, "head", n_head)
     middle = (tokens.astype(jnp.float32) + mix).astype(jnp.bfloat16)
-    middle_full = gather_blocks(middle, "head", n_head, 1)
-    normed2 = rms_scale(middle_full, ffn_gain).astype(jnp.bfloat16)
+    middle_cols = gather_blocks(middle.T, "head", n_head, 0)
+    flat = middle_cols.astype(jnp.float32)
+    scale = lax.rsqrt(jnp.mean(flat * flat, axis=0, keepdims=True) + 1e-05)
+    normed2 = (flat * scale * ffn_gain[:, None]).astype(jnp.bfloat16)
     columns = normed2
     gu_cols = gu_shape[1] * gu_shape[2]
     both = jnp.einsum(
-        "td,dgf->tgf",
+        "dt,dgf->tgf",
         columns,
         ffn_pack[:, :gu_cols].reshape(-1, gu_shape[1], gu_shape[2]),
         preferred_element_type=jnp.float32,

time: 324 us -> 319 us (0.985)
  local copies, waits for them, and re-layouts: 17.4 us -> 11.3 us
    all_to_all x1 -> x0, local copies, waits for them, and re-layouts: 6.43 us -> none  [gather_blocks(): got = lax.all_to_all(spread, axis, 0, 0, tiled=True)]
    reduce_sum x2 -> x1, other arithmetic: 6.38 us -> 3.11 us  [rms_scale(): jnp.mean(flat * flat, axis=-1, keepdims=True) + 1e-05]
  transfers between devices with their start and end apart: 4 -> 4, of which waited for: 2 -> 2; matrix products, arithmetic and copies ran while one was open for 14% -> 12% of each run, Pallas kernels for 0% -> 0%
where the time goes in v5:
time: 319 us; the launch traced here: 318 us
  blocking collectives  127 us (40%)
  waiting for transfers between devices  105 us (33%)
  matrix products  24.7 us (8%)
  other arithmetic  24.4 us (8%)
  between operations  15 us (5%)
  starting transfers between devices  11.4 us (4%)
  local copies, waits for them, and re-layouts  11.3 us (4%)
    all_to_all x2, blocking collectives, scatter_sum(): got = lax.all_to_all(parts, axis, 1, 1, tiled=True)  127 us
    all_to_all x2, waiting for transfers between devices, gather_blocks(): got = lax.all_to_all(spread, axis, 0, 0, tiled=True)  105 us
    all_to_all x2, starting transfers between devices, gather_blocks(): got = lax.all_to_all(spread, axis, 0, 0, tiled=True)  11.3 us
    dot_general x1, matrix products, body(): jnp.einsum('dt,dgf->tgf', columns, ffn_pack[:, :gu_cols].reshape(-1, gu_s...  8.98 us
    dot_general x1, matrix products, body(): jnp.dot(columns, attn_pack[:, :qkv_cols], preferred_element_type=jnp.floa...  6.52 us
  transfers between devices with their start and end apart: 4, of which 2 were waited for; matrix products, arithmetic and copies ran while one was open for 12% of the time, Pallas kernels for 0%

profile of v5, /device:TPU:2, one launch (start us, length us, event | category | flops | bytes accessed | tf_op | source)
XLA Modules:
  0.0 318.4 jit_solution(4691463931693684771)
XLA Ops:
  6.5 0.9 convert_bitcast_fusion.1
  7.6 1.0 convert_element_type.128
  8.6 0.7 pad_maximum_fusion.1
  9.3 1.2 copy.17
  10.6 2.5 broadcast_in_dim.26
  13.1 6.5 %all-to-all-start = ((bf16[8,1024,256]{1,2,0:T(8,128)(2,1)}), bf16[8,1024,256]{1,2,0:T(8,128)(2,1)}, u32[]{:S(2)}, u32[]{:S(2)}) async-start(bf16[8,1024,256]{1,2,0:T(8,128)(2,1)} %broadcast_in_dim.26), calls=%async_computation | async-start | bytes 8388608 | tf_op jit(solution)/shard_map/all_to_all | solution.py:34
  19.7 0.8 pad_maximum_fusion
  20.6 0.6 multiply_reduce_fusion.3
  22.5 0.6 fusion.63
  23.1 1.2 iota_compare_fusion.1
  24.3 1.0 multiply_cosine_fusion.1
  25.3 57.9 %all-to-all-done = bf16[8,1024,256]{1,2,0:T(8,128)(2,1)} async-done(((bf16[8,1024,256]{1,2,0:T(8,128)(2,1)}), bf16[8,1024,256]{1,2,0:T(8,128)(2,1)}, u32[]{:S(2)}, u32[]{:S(2)}) %all-to-all-start) | async-done | bytes 4194336 | tf_op jit(solution)/shard_map/all_to_all | solution.py:34
  83.2 3.1 multiply_reduce_fusion
  86.3 4.1 %fusion.4 = bf16[1024,2048]{0,1:T(8,128)(2,1)} fusion(f32[2048]{0:T(1024)S(1)} %copy-done.3, f32[1024]{0:T(1024)S(1)} %add_rsqrt_fusion.1, bf16[8,1024,256]{1,2,0:T(8,128)(2,1)} %all-to-all-done), kind=kLoop, calls=%fused_computation.7 | loop fusion | flops 8388608 | bytes 8400896 | tf_op jit(solution)/shard_map/convert_element_type | solution.py:82
  90.4 6.5 %fusion.5 = f32[1024,768]{0,1:T(8,128)S(1)} fusion(bf16[1024,2048]{0,1:T(8,128)(2,1)} %fusion.4, bf16[2048,1024]{1,0:T(8,128)(2,1)} %all-gather.3.cloned.1.call-done), kind=kOutput, calls=%fused_computation.15 | convolution fusion | flops 3221225472 | bytes 10485760 | tf_op jit(solution)/shard_map/dot_general | solution.py:94
  100.1 0.6 multiply_reduce_fusion.1
  100.7 0.6 multiply_reduce_fusion.2
  101.6 2.5 convolution_convert_fusion.1
  104.4 74.0 %all_to_all.20 = bf16[1024,8,256]{2,0,1:T(8,128)(2,1)S(1)} all-to-all(bf16[1024,8,256]{2,0,1:T(8,128)(2,1)S(1)} %bitcast.116), channel_id=1, replica_groups=mesh['wide'=16,'head'=8] {'head'}, dimensions={1} | all-to-all | bytes 8388608 | tf_op jit(solution)/shard_map/all_to_all | solution.py:44
  178.4 0.6 convert_reduce_fusion.1
  179.0 0.5 copy-done
  179.8 2.5 broadcast_in_dim.34
  182.2 4.8 %all-to-all-start.2 = ((bf16[8,256,1024]{2,1,0:T(8,128)(2,1)}), bf16[8,256,1024]{2,1,0:T(8,128)(2,1)}, u32[]{:S(2)}, u32[]{:S(2)}) async-start(bf16[8,256,1024]{2,1,0:T(8,128)(2,1)} %broadcast_in_dim.34), calls=%async_computation.2 | async-start | bytes 8388608 | tf_op jit(solution)/shard_map/all_to_all | solution.py:34
  187.1 47.1 %all-to-all-done.2 = bf16[8,256,1024]{2,1,0:T(8,128)(2,1)} async-done(((bf16[8,256,1024]{2,1,0:T(8,128)(2,1)}), bf16[8,256,1024]{2,1,0:T(8,128)(2,1)}, u32[]{:S(2)}, u32[]{:S(2)}) %all-to-all-start.2) | async-done | bytes 4194336 | tf_op jit(solution)/shard_map/all_to_all | solution.py:34
  234.3 3.1 fusion
  237.4 4.1 %fusion.2 = bf16[8,256,1024]{2,1,0:T(8,128)(2,1)} fusion(bf16[8,256,1024]{2,1,0:T(8,128)(2,1)} %all-to-all-done.2, f32[8,256]{1,0:T(8,128)S(1)} %mul.305, f32[1024]{0:T(1024)S(1)} %add_rsqrt_fusion), kind=kLoop, calls=%fused_computation.4 | loop fusion | flops 8388608 | bytes 8400896 | tf_op jit(solution)/shard_map/convert_element_type | solution.py:139
  241.5 2.6 slice-done.3
  244.1 9.0 %fusion.68 = f32[1024,2,704]{0,2,1:T(8,128)S(1)} fusion(bf16[2048,1024,1]{1,0,2:T(8,128)(2,1)} %bitcast.123, bf16[2048,2,704]{0,2,1:T(8,128)(2,1)S(1)} %bitcast.120), kind=kOutput, calls=%fused_computation.129 | convolution fusion | flops 5905580032 | bytes 15728640 | tf_op jit(solution)/shard_map/dt,dgf->tgf/dot_general | solution.py:142
  253.1 3.9 %convolution_convert_fusion = bf16[1024,2048]{1,0:T(8,128)(2,1)S(1)} fusion(bf16[2048,2112]{0,1:T(8,128)(2,1)S(1)} %bitcast.119, f32[1024,2,704]{0,2,1:T(8,128)S(1)} %fusion.68), kind=kOutput, calls=%fused_computation.13 | convolution fusion | flops 2959212544 | bytes 12845056 | tf_op jit(solution)/shard_map/dot_general | solution.py:149
  257.3 52.7 %all_to_all.21 = bf16[1024,8,256]{2,0,1:T(8,128)(2,1)S(1)} all-to-all(bf16[1024,8,256]{2,0,1:T(8,128)(2,1)S(1)} %bitcast.117), channel_id=1, replica_groups=mesh['wide'=16,'head'=8] {'head'}, dimensions={1} | all-to-all | bytes 8388608 | tf_op jit(solution)/shard_map/all_to_all | solution.py:44
  310.0 0.6 convert_reduce_fusion
  310.6 1.0 add_convert_fusion
  (58 shorter events, 4.7 us)
Async XLA Ops:
  6.5 83.8 %all-gather.3.cloned.1.call-start = ((), (), s32[]{:S(2)}) async-start(), calls=%async_computation.4 | async-start | bytes 4456448 | tf_op jit(solution)/shard_map/all_gather | solution.py:86
  13.1 6.5 %copy-start.1 = (f32[128,2,704]{0,2,1:T(8,128)S(1)}, f32[128,2,704]{0,2,1:T(8,128)}, u32[]{:S(2)}) copy-start(f32[128,2,704]{0,2,1:T(8,128)} %param.20) | copy-start | bytes 2162692
  13.1 6.6 %copy-start.2 = (f32[704,128]{1,0:T(8,128)S(1)}, f32[704,128]{1,0:T(8,128)}, u32[]{:S(2)}) copy-start(f32[704,128]{1,0:T(8,128)} %param.21) | copy-start | bytes 1081348
  13.1 7.5 %copy-start.6 = (f32[4,1,128]{2,1,0:T(1,128)S(1)}, f32[4,1,128]{2,1,0:T(1,128)}, u32[]{:S(2)}) copy-start(f32[4,1,128]{2,1,0:T(1,128)} %param.16) | copy-start | bytes 6148
  13.1 9.4 %copy-start.7 = (s32[2]{0:T(128)S(1)}, s32[2]{0:T(128)}, u32[]{:S(2)}) copy-start(s32[2]{0:T(128)} %param.12) | copy-start | bytes 28
  13.1 11.2 %copy-start.5 = (s32[2,512]{1,0:T(2,128)S(1)}, s32[2,512]{1,0:T(2,128)}, u32[]{:S(2)}) copy-start(s32[2,512]{1,0:T(2,128)} %param.13) | copy-start | bytes 12292
  13.1 70.1 %all-to-all-start = ((bf16[8,1024,256]{1,2,0:T(8,128)(2,1)}), bf16[8,1024,256]{1,2,0:T(8,128)(2,1)}, u32[]{:S(2)}, u32[]{:S(2)}) async-start(bf16[8,1024,256]{1,2,0:T(8,128)(2,1)} %broadcast_in_dim.26), calls=%async_computation | async-start | bytes 8388608 | tf_op jit(solution)/shard_map/all_to_all | solution.py:34
  19.6 66.7 %copy-start.3 = (f32[2048]{0:T(1024)S(1)}, f32[2048]{0:T(1024)}, u32[]{:S(2)}) copy-start(f32[2048]{0:T(1024)} %param.14) | copy-start | bytes 24580
  19.6 221.9 %all-gather.5.cloned.1.call-start = ((), (), s32[]{:S(2)}) async-start(), calls=%async_computation.5 | async-start | bytes 9191424 | tf_op jit(solution)/shard_map/all_gather | solution.py:92
  100.7 0.7 copy-start.8
  178.4 1.0 copy-start
  182.2 4.9 %copy-start.4 = (f32[2048]{0:T(1024)S(1)}, f32[2048]{0:T(1024)}, u32[]{:S(2)}) copy-start(f32[2048]{0:T(1024)} %param.19) | copy-start | bytes 24580
  182.2 52.0 %all-to-all-start.2 = ((bf16[8,256,1024]{2,1,0:T(8,128)(2,1)}), bf16[8,256,1024]{2,1,0:T(8,128)(2,1)}, u32[]{:S(2)}, u32[]{:S(2)}) async-start(bf16[8,256,1024]{2,1,0:T(8,128)(2,1)} %broadcast_in_dim.34), calls=%async_computation.2 | async-start | bytes 8388608 | tf_op jit(solution)/shard_map/all_to_all | solution.py:34
  241.5 2.6 slice-start.3
  241.5 11.6 %slice-start = ((s8[8650752]{0:T(1024)(128)(4,1)}), s8[4194304]{0:T(1024)(128)(4,1)S(1)}, s32[]{:S(2)}) async-start(s8[8650752]{0:T(1024)(128)(4,1)} %bitcast.118), calls=%async_computation.6 | async-start | bytes 8388608
  244.1 9.0 %slice-start.1 = ((s8[8650752]{0:T(1024)(128)(4,1)}), s8[4194304]{0:T(1024)(128)(4,1)S(1)}, s32[]{:S(2)}) async-start(s8[8650752]{0:T(1024)(128)(4,1)} %bitcast.118), calls=%async_computation.7 | async-start | bytes 8388608
  244.1 9.0 %slice-start.2 = ((s8[8650752]{0:T(1024)(128)(4,1)}), s8[262144]{0:T(1024)(128)(4,1)S(1)}, s32[]{:S(2)}) async-start(s8[8650752]{0:T(1024)(128)(4,1)} %bitcast.118), calls=%async_computation.8 | async-start | bytes 524288
Sparse Core Ops, SparseCore 0:
  9.7 71.2 all-gather.2
  83.3 102.7 all-gather.4

commit v6 on v5

--- a/solution.py
+++ b/solution.py
@@ -137,24 +137,31 @@
     flat = middle_cols.astype(jnp.float32)
     scale = lax.rsqrt(jnp.mean(flat * flat, axis=0, keepdims=True) + 1e-05)
     normed2 = (flat * scale * ffn_gain[:, None]).astype(jnp.bfloat16)
-    columns = normed2
     gu_cols = gu_shape[1] * gu_shape[2]
-    both = jnp.einsum(
-        "dt,dgf->tgf",
-        columns,
-        ffn_pack[:, :gu_cols].reshape(-1, gu_shape[1], gu_shape[2]),
-        preferred_element_type=jnp.float32,
-    )
-    hidden = (jax.nn.silu(both[:, 0]) * both[:, 1]).astype(jnp.bfloat16)
-    ffn_terms = lax.dot_general(
-        hidden,
-        ffn_pack[:, gu_cols:],
-        (((1,), (1,)), ((), ())),
-        preferred_element_type=jnp.float32,
-    )
-    ffn = scatter_sum(ffn_terms, "head", n_head)
-    return (middle.astype(jnp.float32) + ffn).astype(jnp.bfloat16)
-
+    gate_up_full = ffn_pack[:, :gu_cols].reshape(-1, gu_shape[1], gu_shape[2])
+    down_cols = ffn_pack[:, gu_cols:]
+    rows_here = middle.shape[0]
+    piece = rows_here // 2
+    results = []
+    for part in range(2):
+        columns = normed2[:, part * piece : (part + 1) * piece]
+        both = jnp.einsum(
+            "dt,dgf->tgf",
+            columns,
+            gate_up_full,
+            preferred_element_type=jnp.float32,
+        )
+        hidden = (jax.nn.silu(both[:, 0]) * both[:, 1]).astype(jnp.bfloat16)
+        ffn_terms = lax.dot_general(
+            hidden,
+            down_cols,
+            (((1,), (1,)), ((), ())),
+            preferred_element_type=jnp.float32,
+        )
+        ffn = scatter_sum(ffn_terms, "head", n_head)
+        stream = middle[part * piece : (part + 1) * piece].astype(jnp.float32)
+        results.append((stream + ffn).astype(jnp.bfloat16))
+    return jnp.concatenate(results, axis=0)
 
 def solution(mesh):
     placed = (

time: 319 us -> 312 us (0.978)
  waiting for transfers between devices: 105 us -> 94.4 us
  matrix products: 24.7 us -> 28.3 us
    all_to_all x2 -> x1, blocking collectives: 127 us -> 74 us  [scatter_sum(): got = lax.all_to_all(parts, axis, 1, 1, tiled=True)]
    all_to_all x0 -> x1, blocking collectives: none -> 49.7 us  [gather_blocks(): got = lax.all_to_all(spread, axis, 0, 0, tiled=True)]
    all_to_all x2 -> x1, waiting for transfers between devices: 105 us -> 57.9 us  [gather_blocks(): got = lax.all_to_all(spread, axis, 0, 0, tiled=True)]
    all_to_all x0 -> x2, waiting for transfers between devices: none -> 36.5 us  [scatter_sum(): got = lax.all_to_all(parts, axis, 1, 1, tiled=True)]
    all_to_all x0 -> x2, starting transfers between devices: none -> 7.97 us  [scatter_sum(): got = lax.all_to_all(parts, axis, 1, 1, tiled=True)]
    all_to_all x2 -> x1, starting transfers between devices: 11.3 us -> 6.47 us  [gather_blocks(): got = lax.all_to_all(spread, axis, 0, 0, tiled=True)]
    dot_general x2 -> x4, matrix products: 12.9 us -> 16.5 us  [the longest x2 9.04 us: body(): jnp.einsum('dt,dgf->tgf', columns, gate_up_full, preferred_element_type=j...]
  transfers between devices with their start and end apart: 4 -> 5, of which waited for: 2 -> 3; matrix products, arithmetic and copies ran while one was open for 12% -> 15% of each run, Pallas kernels for 0% -> 0%
where the time goes in v6:
time: 312 us; the launch traced here: 311 us
  blocking collectives  124 us (40%)
  waiting for transfers between devices  94.4 us (30%)
  matrix products  28.3 us (9%)
  other arithmetic  22.2 us (7%)
  between operations  15 us (5%)
  starting transfers between devices  14.5 us (5%)
  local copies, waits for them, and re-layouts  13.2 us (4%)
    all_to_all x1, blocking collectives, scatter_sum(): got = lax.all_to_all(parts, axis, 1, 1, tiled=True)  74 us
    all_to_all x1, waiting for transfers between devices, gather_blocks(): got = lax.all_to_all(spread, axis, 0, 0, tiled=True)  57.9 us
    all_to_all x1, blocking collectives, gather_blocks(): got = lax.all_to_all(spread, axis, 0, 0, tiled=True)  49.7 us
    all_to_all x2, waiting for transfers between devices, scatter_sum(): got = lax.all_to_all(parts, axis, 1, 1, tiled=True)  36.5 us
    dot_general x2, matrix products, body(): jnp.einsum('dt,dgf->tgf', columns, gate_up_full, preferred_element_type=j...  9.04 us
    all_to_all x2, starting transfers between devices, scatter_sum(): got = lax.all_to_all(parts, axis, 1, 1, tiled=True)  7.97 us
    dot_general x2, matrix products, body(): lax.dot_general(hidden, down_cols, (((1,), (1,)), ((), ())), preferred_el...  7.49 us
    dot_general x1, matrix products, body(): jnp.dot(columns, attn_pack[:, :qkv_cols], preferred_element_type=jnp.floa...  6.52 us
  transfers between devices with their start and end apart: 5, of which 3 were waited for; matrix products, arithmetic and copies ran while one was open for 15% of the time, Pallas kernels for 0%

profile of v6, /device:TPU:2, one launch (start us, length us, event | category | flops | bytes accessed | tf_op | source)
XLA Modules:
  0.0 311.4 jit_solution(15222743284701915458)
XLA Ops:
  6.5 1.0 convert_element_type.144
  7.6 0.9 convert_bitcast_fusion.1
  8.6 0.7 pad_maximum_fusion.2
  9.3 1.2 copy.17
  10.6 2.5 broadcast_in_dim.26
  13.1 6.5 %all-to-all-start = ((bf16[8,1024,256]{1,2,0:T(8,128)(2,1)}), bf16[8,1024,256]{1,2,0:T(8,128)(2,1)}, u32[]{:S(2)}, u32[]{:S(2)}) async-start(bf16[8,1024,256]{1,2,0:T(8,128)(2,1)} %broadcast_in_dim.26), calls=%async_computation | async-start | bytes 8388608 | tf_op jit(solution)/shard_map/all_to_all | solution.py:34
  19.7 0.8 pad_maximum_fusion
  20.6 0.6 multiply_reduce_fusion.4
  23.1 1.2 iota_compare_fusion.1
  24.3 1.0 multiply_cosine_fusion.1
  25.3 57.9 %all-to-all-done = bf16[8,1024,256]{1,2,0:T(8,128)(2,1)} async-done(((bf16[8,1024,256]{1,2,0:T(8,128)(2,1)}), bf16[8,1024,256]{1,2,0:T(8,128)(2,1)}, u32[]{:S(2)}, u32[]{:S(2)}) %all-to-all-start) | async-done | bytes 4194336 | tf_op jit(solution)/shard_map/all_to_all | solution.py:34
  83.2 3.1 multiply_reduce_fusion.1
  86.3 4.1 %fusion.1 = bf16[1024,2048]{0,1:T(8,128)(2,1)} fusion(f32[2048]{0:T(1024)S(1)} %copy-done.5, f32[1024]{0:T(1024)S(1)} %add_rsqrt_fusion.1, bf16[8,1024,256]{1,2,0:T(8,128)(2,1)} %all-to-all-done), kind=kLoop, calls=%fused_computation.2 | loop fusion | flops 8388608 | bytes 8400896 | tf_op jit(solution)/shard_map/convert_element_type | solution.py:82
  90.4 6.5 %fusion.4 = f32[1024,768]{0,1:T(8,128)S(1)} fusion(bf16[1024,2048]{0,1:T(8,128)(2,1)} %fusion.1, bf16[2048,1024]{1,0:T(8,128)(2,1)} %all-gather.3.cloned.1.call-done), kind=kOutput, calls=%fused_computation.13 | convolution fusion | flops 3221225472 | bytes 10485760 | tf_op jit(solution)/shard_map/dot_general | solution.py:94
  101.6 2.5 convolution_convert_fusion
  104.4 74.0 %all_to_all.25 = bf16[1024,8,256]{2,0,1:T(8,128)(2,1)S(1)} all-to-all(bf16[1024,8,256]{2,0,1:T(8,128)(2,1)S(1)} %bitcast.140), channel_id=1, replica_groups=mesh['wide'=16,'head'=8] {'head'}, dimensions={1} | all-to-all | bytes 8388608 | tf_op jit(solution)/shard_map/all_to_all | solution.py:44
  180.3 49.7 %all_to_all.26 = bf16[8,256,1024]{2,1,0:T(8,128)(2,1)S(1)} all-to-all(bf16[8,256,1024]{2,1,0:T(8,128)(2,1)S(1)} %broadcast_in_dim.34), channel_id=1, replica_groups=mesh['wide'=16,'head'=8] {'head'}, dimensions={0} | all-to-all | bytes 8388608 | tf_op jit(solution)/shard_map/all_to_all | solution.py:34
  230.0 0.9 multiply_reduce_fusion
  231.0 2.5 fusion.3
  233.5 3.3 %slice.180 = bf16[2048,1408]{0,1:T(8,128)(2,1)S(1)} slice(bf16[2048,2112]{0,1:T(8,128)(2,1)} %all-gather.5.cloned.1.call-done), slice={[0:2048], [0:1408]} | slice | bytes 11534336 | tf_op jit(solution)/shard_map/slice | solution.py:141
  237.4 3.2 %fusion.8 = f32[512,2,704]{0,2,1:T(8,128)S(1)} fusion(bf16[2048,2,704]{0,2,1:T(8,128)(2,1)S(1)} %bitcast.143, bf16[2048,1024]{1,0:T(8,128)(2,1)S(1)} %copy-done.1), kind=kOutput, calls=%fused_computation.22 | convolution fusion | flops 2952790016 | bytes 10747904 | tf_op jit(solution)/shard_map/dt,dgf->tgf/dot_general | solution.py:148
  240.6 3.7 %convolution_convert_fusion.1 = bf16[512,2048]{1,0:T(8,128)(2,1)S(1)} fusion(bf16[2048,2112]{0,1:T(8,128)(2,1)} %all-gather.5.cloned.1.call-done, f32[512,2,704]{0,2,1:T(8,128)S(1)} %fusion.8), kind=kOutput, calls=%fused_computation.15 | convolution fusion | flops 1479606272 | bytes 7864320 | tf_op jit(solution)/shard_map/dot_general | solution.py:155
  244.4 1.5 copy.30
  245.8 3.6 %all-to-all-start.4 = ((bf16[512,8,256]{2,0,1:T(8,128)(2,1)}), bf16[512,8,256]{2,0,1:T(8,128)(2,1)S(1)}, u32[]{:S(2)}, u32[]{:S(2)}) async-start(bf16[512,8,256]{2,0,1:T(8,128)(2,1)} %bitcast.141), calls=%async_computation.4 | async-start | bytes 4194304 | tf_op jit(solution)/shard_map/all_to_all | solution.py:44
  249.4 5.8 %fusion.9 = f32[512,2,704]{0,2,1:T(8,128)S(1)} fusion(bf16[2048,2,704]{0,2,1:T(8,128)(2,1)} %bitcast.144, bf16[2048,1024]{1,0:T(8,128)(2,1)} %fusion.3), kind=kOutput, calls=%fused_computation.24 | convolution fusion | flops 2952790016 | bytes 10747904 | tf_op jit(solution)/shard_map/dt,dgf->tgf/dot_general | solution.py:148
  255.3 3.7 %convolution_convert_fusion.2 = bf16[512,2048]{1,0:T(8,128)(2,1)S(1)} fusion(bf16[2048,2112]{0,1:T(8,128)(2,1)} %all-gather.5.cloned.1.call-done, f32[512,2,704]{0,2,1:T(8,128)S(1)} %fusion.9), kind=kOutput, calls=%fused_computation.16 | convolution fusion | flops 1479606272 | bytes 7864320 | tf_op jit(solution)/shard_map/dot_general | solution.py:155
  259.0 1.5 copy.31
  260.5 12.8 %all-to-all-done.4 = bf16[512,8,256]{2,0,1:T(8,128)(2,1)S(1)} async-done(((bf16[512,8,256]{2,0,1:T(8,128)(2,1)}), bf16[512,8,256]{2,0,1:T(8,128)(2,1)S(1)}, u32[]{:S(2)}, u32[]{:S(2)}) %all-to-all-start.4) | async-done | bytes 2097184 | tf_op jit(solution)/shard_map/all_to_all | solution.py:44
  273.3 4.4 %all-to-all-start.3 = ((bf16[512,8,256]{2,0,1:T(8,128)(2,1)}), bf16[512,8,256]{2,0,1:T(8,128)(2,1)}, u32[]{:S(2)}, u32[]{:S(2)}) async-start(bf16[512,8,256]{2,0,1:T(8,128)(2,1)} %bitcast.142), calls=%async_computation.3 | async-start | bytes 4194304 | tf_op jit(solution)/shard_map/all_to_all | solution.py:44
  278.0 23.7 %all-to-all-done.3 = bf16[512,8,256]{2,0,1:T(8,128)(2,1)} async-done(((bf16[512,8,256]{2,0,1:T(8,128)(2,1)}), bf16[512,8,256]{2,0,1:T(8,128)(2,1)}, u32[]{:S(2)}, u32[]{:S(2)}) %all-to-all-start.3) | async-done | bytes 2097184 | tf_op jit(solution)/shard_map/all_to_all | solution.py:44
  301.7 1.9 convert_reduce_fusion.2
  303.6 0.9 add_convert_fusion.2
  (60 shorter events, 8.5 us)
Async XLA Ops:
  6.5 83.8 %all-gather.3.cloned.1.call-start = ((), (), s32[]{:S(2)}) async-start(), calls=%async_computation.5 | async-start | bytes 4456448 | tf_op jit(solution)/shard_map/all_gather | solution.py:86
  13.1 6.5 %copy-start.3 = (f32[128,2,704]{0,2,1:T(8,128)S(1)}, f32[128,2,704]{0,2,1:T(8,128)}, u32[]{:S(2)}) copy-start(f32[128,2,704]{0,2,1:T(8,128)} %param.20) | copy-start | bytes 2162692
  13.1 6.6 %copy-start.4 = (f32[704,128]{1,0:T(8,128)S(1)}, f32[704,128]{1,0:T(8,128)}, u32[]{:S(2)}) copy-start(f32[704,128]{1,0:T(8,128)} %param.21) | copy-start | bytes 1081348
  13.1 7.5 %copy-start.8 = (f32[4,1,128]{2,1,0:T(1,128)S(1)}, f32[4,1,128]{2,1,0:T(1,128)}, u32[]{:S(2)}) copy-start(f32[4,1,128]{2,1,0:T(1,128)} %param.16) | copy-start | bytes 6148
  13.1 9.4 %copy-start.9 = (s32[2]{0:T(128)S(1)}, s32[2]{0:T(128)}, u32[]{:S(2)}) copy-start(s32[2]{0:T(128)} %param.12) | copy-start | bytes 28
  13.1 11.2 %copy-start.7 = (s32[2,512]{1,0:T(2,128)S(1)}, s32[2,512]{1,0:T(2,128)}, u32[]{:S(2)}) copy-start(s32[2,512]{1,0:T(2,128)} %param.13) | copy-start | bytes 12292
  13.1 70.1 %all-to-all-start = ((bf16[8,1024,256]{1,2,0:T(8,128)(2,1)}), bf16[8,1024,256]{1,2,0:T(8,128)(2,1)}, u32[]{:S(2)}, u32[]{:S(2)}) async-start(bf16[8,1024,256]{1,2,0:T(8,128)(2,1)} %broadcast_in_dim.26), calls=%async_computation | async-start | bytes 8388608 | tf_op jit(solution)/shard_map/all_to_all | solution.py:34
  19.6 66.7 %copy-start.5 = (f32[2048]{0:T(1024)S(1)}, f32[2048]{0:T(1024)}, u32[]{:S(2)}) copy-start(f32[2048]{0:T(1024)} %param.14) | copy-start | bytes 24580
  19.6 213.9 %all-gather.5.cloned.1.call-start = ((), (), s32[]{:S(2)}) async-start(), calls=%async_computation.6 | async-start | bytes 9191424 | tf_op jit(solution)/shard_map/all_gather | solution.py:92
  100.7 0.7 copy-start.10
  178.4 1.0 copy-start.2
  230.0 0.9 copy-start.6
  233.5 3.9 %copy-start.1 = (bf16[2048,1024]{1,0:T(8,128)(2,1)S(1)}, bf16[2048,1024]{1,0:T(8,128)(2,1)}, u32[]{:S(2)}) copy-start(bf16[2048,1024]{1,0:T(8,128)(2,1)} %fusion.3) | copy-start | bytes 12582916
  236.8 3.8 %copy-start = (bf16[2048,1408]{0,1:T(8,128)(2,1)}, bf16[2048,1408]{0,1:T(8,128)(2,1)S(1)}, u32[]{:S(2)}) copy-start(bf16[2048,1408]{0,1:T(8,128)(2,1)S(1)} %slice.180) | copy-start | bytes 17301508
  245.8 27.5 %all-to-all-start.4 = ((bf16[512,8,256]{2,0,1:T(8,128)(2,1)}), bf16[512,8,256]{2,0,1:T(8,128)(2,1)S(1)}, u32[]{:S(2)}, u32[]{:S(2)}) async-start(bf16[512,8,256]{2,0,1:T(8,128)(2,1)} %bitcast.141), calls=%async_computation.4 | async-start | bytes 4194304 | tf_op jit(solution)/shard_map/all_to_all | solution.py:44
  273.3 28.4 %all-to-all-start.3 = ((bf16[512,8,256]{2,0,1:T(8,128)(2,1)}), bf16[512,8,256]{2,0,1:T(8,128)(2,1)}, u32[]{:S(2)}, u32[]{:S(2)}) async-start(bf16[512,8,256]{2,0,1:T(8,128)(2,1)} %bitcast.142), calls=%async_computation.3 | async-start | bytes 4194304 | tf_op jit(solution)/shard_map/all_to_all | solution.py:44
Sparse Core Ops, SparseCore 0:
  9.7 71.2 all-gather.2
  83.3 102.7 all-gather.4

commit v7 on v6

--- a/solution.py
+++ b/solution.py
@@ -138,20 +138,20 @@
     scale = lax.rsqrt(jnp.mean(flat * flat, axis=0, keepdims=True) + 1e-05)
     normed2 = (flat * scale * ffn_gain[:, None]).astype(jnp.bfloat16)
     gu_cols = gu_shape[1] * gu_shape[2]
-    gate_up_full = ffn_pack[:, :gu_cols].reshape(-1, gu_shape[1], gu_shape[2])
+    units = gu_shape[2]
     down_cols = ffn_pack[:, gu_cols:]
     rows_here = middle.shape[0]
     piece = rows_here // 2
     results = []
     for part in range(2):
         columns = normed2[:, part * piece : (part + 1) * piece]
-        both = jnp.einsum(
-            "dt,dgf->tgf",
+        both = lax.dot_general(
             columns,
-            gate_up_full,
+            ffn_pack[:, :gu_cols],
+            (((0,), (0,)), ((), ())),
             preferred_element_type=jnp.float32,
         )
-        hidden = (jax.nn.silu(both[:, 0]) * both[:, 1]).astype(jnp.bfloat16)
+        hidden = (jax.nn.silu(both[:, :units]) * both[:, units:]).astype(jnp.bfloat16)
         ffn_terms = lax.dot_general(
             hidden,
             down_cols,

time: 312 us -> 312 us (level)
  matrix products: 28.3 us -> 32.2 us
  local copies, waits for them, and re-layouts: 13.2 us -> 9.39 us
    dot_general x2, matrix products: 9.04 us -> 13 us  [body(): lax.dot_general(columns, ffn_pack[:, :gu_cols], (((0,), (0,)), ((), ())),...]
    slice x1 -> x0, local copies, waits for them, and re-layouts: 3.31 us -> none  [body(): gate_up_full = ffn_pack[:, :gu_cols].reshape(-1, gu_shape[1], gu_shape[2])]
where the time goes in v7:
time: 312 us; the launch traced here: 311 us
  blocking collectives  124 us (40%)
  waiting for transfers between devices  93.8 us (30%)
  matrix products  32.2 us (10%)
  other arithmetic  22.2 us (7%)
  between operations  15 us (5%)
  starting transfers between devices  14.5 us (5%)
  local copies, waits for them, and re-layouts  9.39 us (3%)
    all_to_all x1, blocking collectives, scatter_sum(): got = lax.all_to_all(parts, axis, 1, 1, tiled=True)  74 us
    all_to_all x1, waiting for transfers between devices, gather_blocks(): got = lax.all_to_all(spread, axis, 0, 0, tiled=True)  57.9 us
    all_to_all x1, blocking collectives, gather_blocks(): got = lax.all_to_all(spread, axis, 0, 0, tiled=True)  49.7 us
    all_to_all x2, waiting for transfers between devices, scatter_sum(): got = lax.all_to_all(parts, axis, 1, 1, tiled=True)  35.9 us
    dot_general x2, matrix products, body(): lax.dot_general(columns, ffn_pack[:, :gu_cols], (((0,), (0,)), ((), ())),...  13 us
    all_to_all x2, starting transfers between devices, scatter_sum(): got = lax.all_to_all(parts, axis, 1, 1, tiled=True)  7.97 us
    dot_general x2, matrix products, body(): lax.dot_general(hidden, down_cols, (((1,), (1,)), ((), ())), preferred_el...  7.41 us
    dot_general x1, matrix products, body(): jnp.dot(columns, attn_pack[:, :qkv_cols], preferred_element_type=jnp.floa...  6.52 us
  transfers between devices with their start and end apart: 5, of which 3 were waited for; matrix products, arithmetic and copies ran while one was open for 15% of the time, Pallas kernels for 0%

profile of v7, /device:TPU:2, one launch (start us, length us, event | category | flops | bytes accessed | tf_op | source)
XLA Modules:
  0.0 310.7 jit_solution(5116372711192906720)
XLA Ops:
  6.5 1.0 convert_element_type.144
  7.6 0.9 convert_bitcast_fusion.1
  8.6 0.7 pad_maximum_fusion.2
  9.3 1.2 copy.23
  10.6 2.5 broadcast_in_dim.26
  13.1 6.5 %all-to-all-start = ((bf16[8,1024,256]{1,2,0:T(8,128)(2,1)}), bf16[8,1024,256]{1,2,0:T(8,128)(2,1)}, u32[]{:S(2)}, u32[]{:S(2)}) async-start(bf16[8,1024,256]{1,2,0:T(8,128)(2,1)} %broadcast_in_dim.26), calls=%async_computation | async-start | bytes 8388608 | tf_op jit(solution)/shard_map/all_to_all | solution.py:34
  19.7 0.8 pad_maximum_fusion
  20.6 0.6 multiply_reduce_fusion.4
  23.1 1.2 iota_compare_fusion.1
  24.3 1.0 multiply_cosine_fusion.1
  25.3 57.9 %all-to-all-done = bf16[8,1024,256]{1,2,0:T(8,128)(2,1)} async-done(((bf16[8,1024,256]{1,2,0:T(8,128)(2,1)}), bf16[8,1024,256]{1,2,0:T(8,128)(2,1)}, u32[]{:S(2)}, u32[]{:S(2)}) %all-to-all-start) | async-done | bytes 4194336 | tf_op jit(solution)/shard_map/all_to_all | solution.py:34
  83.2 3.1 %multiply_reduce_fusion.1 = f32[1024]{0:T(1024)S(1)} fusion(bf16[8,1024,256]{1,2,0:T(8,128)(2,1)} %all-to-all-done), kind=kLoop, calls=%fused_computation.8 | loop fusion | flops 6290432 | bytes 4198400 | tf_op jit(solution)/shard_map/reduce_sum | solution.py:15
  86.3 4.1 %fusion.1 = bf16[1024,2048]{0,1:T(8,128)(2,1)} fusion(f32[2048]{0:T(1024)S(1)} %copy-done.3, f32[1024]{0:T(1024)S(1)} %add_rsqrt_fusion.1, bf16[8,1024,256]{1,2,0:T(8,128)(2,1)} %all-to-all-done), kind=kLoop, calls=%fused_computation.2 | loop fusion | flops 8388608 | bytes 8400896 | tf_op jit(solution)/shard_map/convert_element_type | solution.py:82
  90.4 6.5 %fusion.8 = f32[1024,768]{0,1:T(8,128)S(1)} fusion(bf16[1024,2048]{0,1:T(8,128)(2,1)} %fusion.1, bf16[2048,1024]{1,0:T(8,128)(2,1)} %all-gather.3.cloned.1.call-done), kind=kOutput, calls=%fused_computation.17 | convolution fusion | flops 3221225472 | bytes 10485760 | tf_op jit(solution)/shard_map/dot_general | solution.py:94
  100.1 0.6 multiply_reduce_fusion.2
  101.6 2.5 convolution_convert_fusion
  104.4 74.0 %all_to_all.25 = bf16[1024,8,256]{2,0,1:T(8,128)(2,1)S(1)} all-to-all(bf16[1024,8,256]{2,0,1:T(8,128)(2,1)S(1)} %bitcast.107), channel_id=1, replica_groups=mesh['wide'=16,'head'=8] {'head'}, dimensions={1} | all-to-all | bytes 8388608 | tf_op jit(solution)/shard_map/all_to_all | solution.py:44
  180.3 49.7 %all_to_all.26 = bf16[8,256,1024]{2,1,0:T(8,128)(2,1)S(1)} all-to-all(bf16[8,256,1024]{2,1,0:T(8,128)(2,1)S(1)} %broadcast_in_dim.34), channel_id=1, replica_groups=mesh['wide'=16,'head'=8] {'head'}, dimensions={0} | all-to-all | bytes 8388608 | tf_op jit(solution)/shard_map/all_to_all | solution.py:34
  230.0 0.9 multiply_reduce_fusion
  231.0 2.5 fusion.3
  233.5 6.5 %fusion.4 = f32[512,1408]{1,0:T(8,128)S(1)} fusion(bf16[2048,2112]{0,1:T(8,128)(2,1)} %all-gather.5.cloned.1.call-done, bf16[2048,1024]{1,0:T(8,128)(2,1)} %fusion.3), kind=kOutput, calls=%fused_computation.9 | convolution fusion | flops 2952790016 | bytes 10747904 | tf_op jit(solution)/shard_map/dot_general | solution.py:148
  240.0 3.7 %convolution_convert_fusion.1 = bf16[512,2048]{1,0:T(8,128)(2,1)S(1)} fusion(bf16[2048,2112]{0,1:T(8,128)(2,1)} %all-gather.5.cloned.1.call-done, f32[512,1408]{1,0:T(8,128)S(1)} %fusion.4), kind=kOutput, calls=%fused_computation.19 | convolution fusion | flops 1479606272 | bytes 8126464 | tf_op jit(solution)/shard_map/dot_general | solution.py:155
  243.7 1.5 copy.36
  245.1 3.6 %all-to-all-start.4 = ((bf16[512,8,256]{2,0,1:T(8,128)(2,1)}), bf16[512,8,256]{2,0,1:T(8,128)(2,1)S(1)}, u32[]{:S(2)}, u32[]{:S(2)}) async-start(bf16[512,8,256]{2,0,1:T(8,128)(2,1)} %bitcast.109), calls=%async_computation.4 | async-start | bytes 4194304 | tf_op jit(solution)/shard_map/all_to_all | solution.py:44
  248.8 6.5 %fusion.6 = f32[512,1408]{1,0:T(8,128)S(1)} fusion(bf16[2048,2112]{0,1:T(8,128)(2,1)} %all-gather.5.cloned.1.call-done, bf16[2048,1024]{1,0:T(8,128)(2,1)} %fusion.3), kind=kOutput, calls=%fused_computation.11 | convolution fusion | flops 2952790016 | bytes 10747904 | tf_op jit(solution)/shard_map/dot_general | solution.py:148
  255.3 3.7 %convolution_convert_fusion.2 = bf16[512,2048]{1,0:T(8,128)(2,1)S(1)} fusion(bf16[2048,2112]{0,1:T(8,128)(2,1)} %all-gather.5.cloned.1.call-done, f32[512,1408]{1,0:T(8,128)S(1)} %fusion.6), kind=kOutput, calls=%fused_computation.20 | convolution fusion | flops 1479606272 | bytes 8126464 | tf_op jit(solution)/shard_map/dot_general | solution.py:155
  259.0 1.5 copy.37
  260.5 12.2 %all-to-all-done.4 = bf16[512,8,256]{2,0,1:T(8,128)(2,1)S(1)} async-done(((bf16[512,8,256]{2,0,1:T(8,128)(2,1)}), bf16[512,8,256]{2,0,1:T(8,128)(2,1)S(1)}, u32[]{:S(2)}, u32[]{:S(2)}) %all-to-all-start.4) | async-done | bytes 2097184 | tf_op jit(solution)/shard_map/all_to_all | solution.py:44
  272.6 4.4 %all-to-all-start.3 = ((bf16[512,8,256]{2,0,1:T(8,128)(2,1)}), bf16[512,8,256]{2,0,1:T(8,128)(2,1)}, u32[]{:S(2)}, u32[]{:S(2)}) async-start(bf16[512,8,256]{2,0,1:T(8,128)(2,1)} %bitcast.108), calls=%async_computation.3 | async-start | bytes 4194304 | tf_op jit(solution)/shard_map/all_to_all | solution.py:44
  277.3 23.7 %all-to-all-done.3 = bf16[512,8,256]{2,0,1:T(8,128)(2,1)} async-done(((bf16[512,8,256]{2,0,1:T(8,128)(2,1)}), bf16[512,8,256]{2,0,1:T(8,128)(2,1)}, u32[]{:S(2)}, u32[]{:S(2)}) %all-to-all-start.3) | async-done | bytes 2097184 | tf_op jit(solution)/shard_map/all_to_all | solution.py:44
  301.0 1.9 convert_reduce_fusion.2
  303.0 0.9 add_convert_fusion.2
  (55 shorter events, 7.4 us)
Async XLA Ops:
  6.5 83.8 %all-gather.3.cloned.1.call-start = ((), (), s32[]{:S(2)}) async-start(), calls=%async_computation.5 | async-start | bytes 4456448 | tf_op jit(solution)/shard_map/all_gather | solution.py:86
  13.1 6.5 %copy-start.1 = (f32[128,2,704]{0,2,1:T(8,128)S(1)}, f32[128,2,704]{0,2,1:T(8,128)}, u32[]{:S(2)}) copy-start(f32[128,2,704]{0,2,1:T(8,128)} %param.20) | copy-start | bytes 2162692
  13.1 6.6 %copy-start.2 = (f32[704,128]{1,0:T(8,128)S(1)}, f32[704,128]{1,0:T(8,128)}, u32[]{:S(2)}) copy-start(f32[704,128]{1,0:T(8,128)} %param.21) | copy-start | bytes 1081348
  13.1 7.5 %copy-start.6 = (f32[4,1,128]{2,1,0:T(1,128)S(1)}, f32[4,1,128]{2,1,0:T(1,128)}, u32[]{:S(2)}) copy-start(f32[4,1,128]{2,1,0:T(1,128)} %param.16) | copy-start | bytes 6148
  13.1 9.4 %copy-start.7 = (s32[2]{0:T(128)S(1)}, s32[2]{0:T(128)}, u32[]{:S(2)}) copy-start(s32[2]{0:T(128)} %param.12) | copy-start | bytes 28
  13.1 11.2 %copy-start.5 = (s32[2,512]{1,0:T(2,128)S(1)}, s32[2,512]{1,0:T(2,128)}, u32[]{:S(2)}) copy-start(s32[2,512]{1,0:T(2,128)} %param.13) | copy-start | bytes 12292
  13.1 70.1 %all-to-all-start = ((bf16[8,1024,256]{1,2,0:T(8,128)(2,1)}), bf16[8,1024,256]{1,2,0:T(8,128)(2,1)}, u32[]{:S(2)}, u32[]{:S(2)}) async-start(bf16[8,1024,256]{1,2,0:T(8,128)(2,1)} %broadcast_in_dim.26), calls=%async_computation | async-start | bytes 8388608 | tf_op jit(solution)/shard_map/all_to_all | solution.py:34
  19.6 66.7 %copy-start.3 = (f32[2048]{0:T(1024)S(1)}, f32[2048]{0:T(1024)}, u32[]{:S(2)}) copy-start(f32[2048]{0:T(1024)} %param.14) | copy-start | bytes 24580
  19.6 213.9 %all-gather.5.cloned.1.call-start = ((), (), s32[]{:S(2)}) async-start(), calls=%async_computation.6 | async-start | bytes 9191424 | tf_op jit(solution)/shard_map/all_gather | solution.py:92
  100.7 0.7 copy-start.8
  178.4 1.0 copy-start
  230.0 0.9 copy-start.4
  245.1 27.5 %all-to-all-start.4 = ((bf16[512,8,256]{2,0,1:T(8,128)(2,1)}), bf16[512,8,256]{2,0,1:T(8,128)(2,1)S(1)}, u32[]{:S(2)}, u32[]{:S(2)}) async-start(bf16[512,8,256]{2,0,1:T(8,128)(2,1)} %bitcast.109), calls=%async_computation.4 | async-start | bytes 4194304 | tf_op jit(solution)/shard_map/all_to_all | solution.py:44
  272.6 28.4 %all-to-all-start.3 = ((bf16[512,8,256]{2,0,1:T(8,128)(2,1)}), bf16[512,8,256]{2,0,1:T(8,128)(2,1)}, u32[]{:S(2)}, u32[]{:S(2)}) async-start(bf16[512,8,256]{2,0,1:T(8,128)(2,1)} %bitcast.108), calls=%async_computation.3 | async-start | bytes 4194304 | tf_op jit(solution)/shard_map/all_to_all | solution.py:44
Sparse Core Ops, SparseCore 0:
  9.7 71.2 all-gather.2
  83.3 102.7 all-gather.4

commit v8 on v7

--- a/solution.py
+++ b/solution.py
@@ -123,15 +123,14 @@
             balance,
             sub_gain,
         )
-        outputs.append(attended)
-    attn = jnp.concatenate(outputs, axis=0)
-    mix_terms = lax.dot_general(
-        attn,
-        attn_pack[:, qkv_cols:],
-        (((1,), (1,)), ((), ())),
-        preferred_element_type=jnp.float32,
-    )
-    mix = scatter_sum(mix_terms, "head", n_head)
+        mix_terms = lax.dot_general(
+            attended,
+            attn_pack[:, qkv_cols:],
+            (((1,), (1,)), ((), ())),
+            preferred_element_type=jnp.float32,
+        )
+        outputs.append(scatter_sum(mix_terms, "head", n_head))
+    mix = jnp.concatenate(outputs, axis=0)
     middle = (tokens.astype(jnp.float32) + mix).astype(jnp.bfloat16)
     middle_cols = gather_blocks(middle.T, "head", n_head, 0)
     flat = middle_cols.astype(jnp.float32)

time: 312 us -> 314 us (level)
  blocking collectives: 124 us -> 49.7 us
  waiting for transfers between devices: 93.8 us -> 154 us
  starting transfers between devices: 14.5 us -> 22.6 us
    all_to_all x1 -> x0, blocking collectives: 74 us -> none  [scatter_sum(): got = lax.all_to_all(parts, axis, 1, 1, tiled=True)]
    all_to_all x2 -> x4, waiting for transfers between devices: 35.9 us -> 95.5 us  [scatter_sum(): got = lax.all_to_all(parts, axis, 1, 1, tiled=True)]
    all_to_all x2 -> x4, starting transfers between devices: 7.97 us -> 16.1 us  [scatter_sum(): got = lax.all_to_all(parts, axis, 1, 1, tiled=True)]
  transfers between devices with their start and end apart: 5 -> 7, of which waited for: 3 -> 5; matrix products, arithmetic and copies ran while one was open for 15% -> 17% of each run, Pallas kernels for 0% -> 0%
where the time goes in v8:
time: 314 us; the launch traced here: 313 us
  waiting for transfers between devices  154 us (49%)
  blocking collectives  49.7 us (16%)
  matrix products  34.9 us (11%)
  other arithmetic  24.7 us (8%)
  starting transfers between devices  22.6 us (7%)
  between operations  15 us (5%)
  local copies, waits for them, and re-layouts  12.3 us (4%)
    all_to_all x4, waiting for transfers between devices, scatter_sum(): got = lax.all_to_all(parts, axis, 1, 1, tiled=True)  95.5 us
    all_to_all x1, waiting for transfers between devices, gather_blocks(): got = lax.all_to_all(spread, axis, 0, 0, tiled=True)  58.4 us
    all_to_all x1, blocking collectives, gather_blocks(): got = lax.all_to_all(spread, axis, 0, 0, tiled=True)  49.7 us
    all_to_all x4, starting transfers between devices, scatter_sum(): got = lax.all_to_all(parts, axis, 1, 1, tiled=True)  16.1 us
    dot_general x2, matrix products, body(): lax.dot_general(columns, ffn_pack[:, :gu_cols], (((0,), (0,)), ((), ())),...  13 us
    dot_general x2, matrix products, body(): lax.dot_general(hidden, down_cols, (((1,), (1,)), ((), ())), preferred_el...  7.41 us
    dot_general x1, matrix products, body(): jnp.dot(columns, attn_pack[:, :qkv_cols], preferred_element_type=jnp.floa...  6.51 us
    all_to_all x1, starting transfers between devices, gather_blocks(): got = lax.all_to_all(spread, axis, 0, 0, tiled=True)  6.46 us
  transfers between devices with their start and end apart: 7, of which 5 were waited for; matrix products, arithmetic and copies ran while one was open for 17% of the time, Pallas kernels for 0%

profile of v8, /device:TPU:2, one launch (start us, length us, event | category | flops | bytes accessed | tf_op | source)
XLA Modules:
  0.0 313.1 jit_solution(17717406585015174789)
XLA Ops:
  6.5 1.0 convert_element_type.150
  9.3 1.2 copy.24
  10.6 2.5 broadcast_in_dim.26
  13.1 6.5 %all-to-all-start = ((bf16[8,1024,256]{1,2,0:T(8,128)(2,1)}), bf16[8,1024,256]{1,2,0:T(8,128)(2,1)}, u32[]{:S(2)}, u32[]{:S(2)}) async-start(bf16[8,1024,256]{1,2,0:T(8,128)(2,1)} %broadcast_in_dim.26), calls=%async_computation | async-start | bytes 8388608 | tf_op jit(solution)/shard_map/all_to_all | solution.py:34
  24.7 58.4 %all-to-all-done = bf16[8,1024,256]{1,2,0:T(8,128)(2,1)} async-done(((bf16[8,1024,256]{1,2,0:T(8,128)(2,1)}), bf16[8,1024,256]{1,2,0:T(8,128)(2,1)}, u32[]{:S(2)}, u32[]{:S(2)}) %all-to-all-start) | async-done | bytes 4194336 | tf_op jit(solution)/shard_map/all_to_all | solution.py:34
  83.1 3.1 multiply_reduce_fusion.1
  86.3 4.1 %fusion.1 = bf16[1024,2048]{0,1:T(8,128)(2,1)} fusion(f32[2048]{0:T(1024)S(1)} %copy-done.3, f32[1024]{0:T(1024)S(1)} %add_rsqrt_fusion.1, bf16[8,1024,256]{1,2,0:T(8,128)(2,1)} %all-to-all-done), kind=kLoop, calls=%fused_computation.2 | loop fusion | flops 8388608 | bytes 8400896 | tf_op jit(solution)/shard_map/convert_element_type | solution.py:82
  90.3 6.5 %fusion.8 = f32[1024,768]{0,1:T(8,128)S(1)} fusion(bf16[1024,2048]{0,1:T(8,128)(2,1)} %fusion.1, bf16[2048,1024]{1,0:T(8,128)(2,1)} %all-gather.3.cloned.1.call-done), kind=kOutput, calls=%fused_computation.16 | convolution fusion | flops 3221225472 | bytes 10485760 | tf_op jit(solution)/shard_map/dot_general | solution.py:94
  100.2 2.1 convolution_convert_fusion.1
  102.3 1.5 copy.42
  103.8 3.6 %all-to-all-start.1 = ((bf16[512,8,256]{2,0,1:T(8,128)(2,1)}), bf16[512,8,256]{2,0,1:T(8,128)(2,1)S(1)}, u32[]{:S(2)}, u32[]{:S(2)}) async-start(bf16[512,8,256]{2,0,1:T(8,128)(2,1)} %bitcast.112), calls=%async_computation.1 | async-start | bytes 4194304 | tf_op jit(solution)/shard_map/all_to_all | solution.py:44
  109.2 1.6 multiply_reduce_fusion.2
  110.8 2.1 convolution_convert_fusion
  112.9 1.5 copy.41
  114.4 32.5 %all-to-all-done.1 = bf16[512,8,256]{2,0,1:T(8,128)(2,1)S(1)} async-done(((bf16[512,8,256]{2,0,1:T(8,128)(2,1)}), bf16[512,8,256]{2,0,1:T(8,128)(2,1)S(1)}, u32[]{:S(2)}, u32[]{:S(2)}) %all-to-all-start.1) | async-done | bytes 2097184 | tf_op jit(solution)/shard_map/all_to_all | solution.py:44
  147.0 4.5 %all-to-all-start.2 = ((bf16[512,8,256]{2,0,1:T(8,128)(2,1)}), bf16[512,8,256]{2,0,1:T(8,128)(2,1)}, u32[]{:S(2)}, u32[]{:S(2)}) async-start(bf16[512,8,256]{2,0,1:T(8,128)(2,1)} %bitcast.114), calls=%async_computation.2 | async-start | bytes 4194304 | tf_op jit(solution)/shard_map/all_to_all | solution.py:44
  151.8 27.1 %all-to-all-done.2 = bf16[512,8,256]{2,0,1:T(8,128)(2,1)} async-done(((bf16[512,8,256]{2,0,1:T(8,128)(2,1)}), bf16[512,8,256]{2,0,1:T(8,128)(2,1)}, u32[]{:S(2)}, u32[]{:S(2)}) %all-to-all-start.2) | async-done | bytes 2097184 | tf_op jit(solution)/shard_map/all_to_all | solution.py:44
  178.9 1.9 convert_reduce_fusion.2
  180.9 1.2 fusion.20
  182.8 49.7 %all_to_all.30 = bf16[8,256,1024]{2,1,0:T(8,128)(2,1)S(1)} all-to-all(bf16[8,256,1024]{2,1,0:T(8,128)(2,1)S(1)} %broadcast_in_dim.34), channel_id=1, replica_groups=mesh['wide'=16,'head'=8] {'head'}, dimensions={0} | all-to-all | bytes 8388608 | tf_op jit(solution)/shard_map/all_to_all | solution.py:34
  233.4 2.5 fusion.3
  235.9 6.5 %fusion.4 = f32[512,1408]{1,0:T(8,128)S(1)} fusion(bf16[2048,2112]{0,1:T(8,128)(2,1)} %all-gather.5.cloned.1.call-done, bf16[2048,1024]{1,0:T(8,128)(2,1)} %fusion.3), kind=kOutput, calls=%fused_computation.8 | convolution fusion | flops 2952790016 | bytes 10747904 | tf_op jit(solution)/shard_map/dot_general | solution.py:147
  242.4 3.7 %convolution_convert_fusion.2 = bf16[512,2048]{1,0:T(8,128)(2,1)S(1)} fusion(bf16[2048,2112]{0,1:T(8,128)(2,1)} %all-gather.5.cloned.1.call-done, f32[512,1408]{1,0:T(8,128)S(1)} %fusion.4), kind=kOutput, calls=%fused_computation.20 | convolution fusion | flops 1479606272 | bytes 8126464 | tf_op jit(solution)/shard_map/dot_general | solution.py:154
  246.1 1.5 copy.39
  247.6 3.6 %all-to-all-start.5 = ((bf16[512,8,256]{2,0,1:T(8,128)(2,1)}), bf16[512,8,256]{2,0,1:T(8,128)(2,1)S(1)}, u32[]{:S(2)}, u32[]{:S(2)}) async-start(bf16[512,8,256]{2,0,1:T(8,128)(2,1)} %bitcast.115), calls=%async_computation.5 | async-start | bytes 4194304 | tf_op jit(solution)/shard_map/all_to_all | solution.py:44
  251.2 6.5 %fusion.6 = f32[512,1408]{1,0:T(8,128)S(1)} fusion(bf16[2048,2112]{0,1:T(8,128)(2,1)} %all-gather.5.cloned.1.call-done, bf16[2048,1024]{1,0:T(8,128)(2,1)} %fusion.3), kind=kOutput, calls=%fused_computation.10 | convolution fusion | flops 2952790016 | bytes 10747904 | tf_op jit(solution)/shard_map/dot_general | solution.py:147
  257.7 3.7 %convolution_convert_fusion.3 = bf16[512,2048]{1,0:T(8,128)(2,1)S(1)} fusion(bf16[2048,2112]{0,1:T(8,128)(2,1)} %all-gather.5.cloned.1.call-done, f32[512,1408]{1,0:T(8,128)S(1)} %fusion.6), kind=kOutput, calls=%fused_computation.21 | convolution fusion | flops 1479606272 | bytes 8126464 | tf_op jit(solution)/shard_map/dot_general | solution.py:154
  261.4 1.5 copy.40
  262.9 12.2 %all-to-all-done.5 = bf16[512,8,256]{2,0,1:T(8,128)(2,1)S(1)} async-done(((bf16[512,8,256]{2,0,1:T(8,128)(2,1)}), bf16[512,8,256]{2,0,1:T(8,128)(2,1)S(1)}, u32[]{:S(2)}, u32[]{:S(2)}) %all-to-all-start.5) | async-done | bytes 2097184 | tf_op jit(solution)/shard_map/all_to_all | solution.py:44
  275.1 4.4 %all-to-all-start.4 = ((bf16[512,8,256]{2,0,1:T(8,128)(2,1)}), bf16[512,8,256]{2,0,1:T(8,128)(2,1)}, u32[]{:S(2)}, u32[]{:S(2)}) async-start(bf16[512,8,256]{2,0,1:T(8,128)(2,1)} %bitcast.113), calls=%async_computation.4 | async-start | bytes 4194304 | tf_op jit(solution)/shard_map/all_to_all | solution.py:44
  279.7 23.7 %all-to-all-done.4 = bf16[512,8,256]{2,0,1:T(8,128)(2,1)} async-done(((bf16[512,8,256]{2,0,1:T(8,128)(2,1)}), bf16[512,8,256]{2,0,1:T(8,128)(2,1)}, u32[]{:S(2)}, u32[]{:S(2)}) %all-to-all-start.4) | async-done | bytes 2097184 | tf_op jit(solution)/shard_map/all_to_all | solution.py:44
  303.4 1.9 convert_reduce_fusion.1
  (61 shorter events, 13.8 us)
Async XLA Ops:
  6.5 83.8 %all-gather.3.cloned.1.call-start = ((), (), s32[]{:S(2)}) async-start(), calls=%async_computation.6 | async-start | bytes 4456448 | tf_op jit(solution)/shard_map/all_gather | solution.py:86
  13.1 6.5 %copy-start.1 = (f32[128,2,704]{0,2,1:T(8,128)S(1)}, f32[128,2,704]{0,2,1:T(8,128)}, u32[]{:S(2)}) copy-start(f32[128,2,704]{0,2,1:T(8,128)} %param.20) | copy-start | bytes 2162692
  13.1 6.6 %copy-start.2 = (f32[704,128]{1,0:T(8,128)S(1)}, f32[704,128]{1,0:T(8,128)}, u32[]{:S(2)}) copy-start(f32[704,128]{1,0:T(8,128)} %param.21) | copy-start | bytes 1081348
  13.1 70.1 %all-to-all-start = ((bf16[8,1024,256]{1,2,0:T(8,128)(2,1)}), bf16[8,1024,256]{1,2,0:T(8,128)(2,1)}, u32[]{:S(2)}, u32[]{:S(2)}) async-start(bf16[8,1024,256]{1,2,0:T(8,128)(2,1)} %broadcast_in_dim.26), calls=%async_computation | async-start | bytes 8388608 | tf_op jit(solution)/shard_map/all_to_all | solution.py:34
  19.5 1.1 copy-start.7
  19.5 3.0 copy-start.8
  19.6 4.1 %copy-start.5 = (s32[2,512]{1,0:T(2,128)S(1)}, s32[2,512]{1,0:T(2,128)}, u32[]{:S(2)}) copy-start(s32[2,512]{1,0:T(2,128)} %param.13) | copy-start | bytes 12292
  19.6 216.3 %all-gather.5.cloned.1.call-start = ((), (), s32[]{:S(2)}) async-start(), calls=%async_computation.7 | async-start | bytes 9191424 | tf_op jit(solution)/shard_map/all_gather | solution.py:92
  19.7 66.5 %copy-start.3 = (f32[2048]{0:T(1024)S(1)}, f32[2048]{0:T(1024)}, u32[]{:S(2)}) copy-start(f32[2048]{0:T(1024)} %param.14) | copy-start | bytes 24580
  97.2 1.2 copy-start
  99.5 0.7 copy-start.6
  103.8 43.2 %all-to-all-start.1 = ((bf16[512,8,256]{2,0,1:T(8,128)(2,1)}), bf16[512,8,256]{2,0,1:T(8,128)(2,1)S(1)}, u32[]{:S(2)}, u32[]{:S(2)}) async-start(bf16[512,8,256]{2,0,1:T(8,128)(2,1)} %bitcast.112), calls=%async_computation.1 | async-start | bytes 4194304 | tf_op jit(solution)/shard_map/all_to_all | solution.py:44
  147.0 32.0 %all-to-all-start.2 = ((bf16[512,8,256]{2,0,1:T(8,128)(2,1)}), bf16[512,8,256]{2,0,1:T(8,128)(2,1)}, u32[]{:S(2)}, u32[]{:S(2)}) async-start(bf16[512,8,256]{2,0,1:T(8,128)(2,1)} %bitcast.114), calls=%async_computation.2 | async-start | bytes 4194304 | tf_op jit(solution)/shard_map/all_to_all | solution.py:44
  232.5 0.9 copy-start.4
  247.6 27.5 %all-to-all-start.5 = ((bf16[512,8,256]{2,0,1:T(8,128)(2,1)}), bf16[512,8,256]{2,0,1:T(8,128)(2,1)S(1)}, u32[]{:S(2)}, u32[]{:S(2)}) async-start(bf16[512,8,256]{2,0,1:T(8,128)(2,1)} %bitcast.115), calls=%async_computation.5 | async-start | bytes 4194304 | tf_op jit(solution)/shard_map/all_to_all | solution.py:44
  275.1 28.4 %all-to-all-start.4 = ((bf16[512,8,256]{2,0,1:T(8,128)(2,1)}), bf16[512,8,256]{2,0,1:T(8,128)(2,1)}, u32[]{:S(2)}, u32[]{:S(2)}) async-start(bf16[512,8,256]{2,0,1:T(8,128)(2,1)} %bitcast.113), calls=%async_computation.4 | async-start | bytes 4194304 | tf_op jit(solution)/shard_map/all_to_all | solution.py:44
Sparse Core Ops, SparseCore 0:
  9.7 71.2 all-gather.2
  83.3 95.4 all-gather.4

commit v9 on v7

--- a/solution.py
+++ b/solution.py
@@ -79,7 +79,11 @@
     n_head = lax.axis_size("head")
     n_wide = lax.axis_size("wide")
     full_rows = gather_blocks(tokens, "head", n_head, 1)
-    normed = rms_scale(full_rows, attn_gain).astype(jnp.bfloat16)
+    flat_rows = full_rows.astype(jnp.float32)
+    grouped = flat_rows.reshape(flat_rows.shape[0], n_head, -1)
+    partial = lax.optimization_barrier(jnp.sum(grouped * grouped, axis=2))
+    power = jnp.sum(partial, axis=1, keepdims=True) / flat_rows.shape[1]
+    normed = (flat_rows * lax.rsqrt(power + 1e-05) * attn_gain).astype(jnp.bfloat16)
     qkv_local = qkv_weight.astype(jnp.bfloat16)
     qkv_cols = qkv_local.shape[1]
     attn_pack = jnp.concatenate([qkv_local, out_weight.astype(jnp.bfloat16).T], axis=1)
@@ -135,7 +139,10 @@
     middle = (tokens.astype(jnp.float32) + mix).astype(jnp.bfloat16)
     middle_cols = gather_blocks(middle.T, "head", n_head, 0)
     flat = middle_cols.astype(jnp.float32)
-    scale = lax.rsqrt(jnp.mean(flat * flat, axis=0, keepdims=True) + 1e-05)
+    grouped = flat.reshape(n_head, -1, flat.shape[1])
+    partial = lax.optimization_barrier(jnp.sum(grouped * grouped, axis=1))
+    power = jnp.sum(partial, axis=0, keepdims=True) / flat.shape[0]
+    scale = lax.rsqrt(power + 1e-05)
     normed2 = (flat * scale * ffn_gain[:, None]).astype(jnp.bfloat16)
     gu_cols = gu_shape[1] * gu_shape[2]
     units = gu_shape[2]

time: 312 us -> 315 us (level)
  no operation moved by 1% of the time
where the time goes in v9:
time: 315 us; the launch traced here: 314 us
  blocking collectives  124 us (39%)
  waiting for transfers between devices  93.8 us (30%)
  matrix products  32.2 us (10%)
  other arithmetic  24 us (8%)
  between operations  15 us (5%)
  starting transfers between devices  14.5 us (5%)
  local copies, waits for them, and re-layouts  11.3 us (4%)
    all_to_all x1, blocking collectives, scatter_sum(): got = lax.all_to_all(parts, axis, 1, 1, tiled=True)  74 us
    all_to_all x1, waiting for transfers between devices, gather_blocks(): got = lax.all_to_all(spread, axis, 0, 0, tiled=True)  57.9 us
    all_to_all x1, blocking collectives, gather_blocks(): got = lax.all_to_all(spread, axis, 0, 0, tiled=True)  49.7 us
    all_to_all x2, waiting for transfers between devices, scatter_sum(): got = lax.all_to_all(parts, axis, 1, 1, tiled=True)  35.9 us
    dot_general x2, matrix products, body(): lax.dot_general(columns, ffn_pack[:, :gu_cols], (((0,), (0,)), ((), ())),...  13 us
    all_to_all x2, starting transfers between devices, scatter_sum(): got = lax.all_to_all(parts, axis, 1, 1, tiled=True)  7.97 us
    dot_general x2, matrix products, body(): lax.dot_general(hidden, down_cols, (((1,), (1,)), ((), ())), preferred_el...  7.41 us
    dot_general x1, matrix products, body(): jnp.dot(columns, attn_pack[:, :qkv_cols], preferred_element_type=jnp.floa...  6.54 us
  transfers between devices with their start and end apart: 5, of which 3 were waited for; matrix products, arithmetic and copies ran while one was open for 15% of the time, Pallas kernels for 0%

profile of v9, /device:TPU:2, one launch (start us, length us, event | category | flops | bytes accessed | tf_op | source)
XLA Modules:
  0.0 314.5 jit_solution(13824357620388911869)
XLA Ops:
  6.5 1.0 convert_element_type.144
  7.6 0.9 convert_bitcast_fusion.1
  8.6 0.7 pad_maximum_fusion.2
  9.3 1.2 copy.23
  10.6 2.5 broadcast_in_dim.26
  13.1 6.5 %all-to-all-start = ((bf16[8,1024,256]{1,2,0:T(8,128)(2,1)}), bf16[8,1024,256]{1,2,0:T(8,128)(2,1)}, u32[]{:S(2)}, u32[]{:S(2)}) async-start(bf16[8,1024,256]{1,2,0:T(8,128)(2,1)} %broadcast_in_dim.26), calls=%async_computation | async-start | bytes 8388608 | tf_op jit(solution)/shard_map/all_to_all | solution.py:34
  19.7 0.8 pad_maximum_fusion
  20.6 0.6 multiply_reduce_fusion.4
  23.1 1.2 iota_compare_fusion.1
  24.3 1.0 multiply_cosine_fusion.1
  25.3 57.9 %all-to-all-done = bf16[8,1024,256]{1,2,0:T(8,128)(2,1)} async-done(((bf16[8,1024,256]{1,2,0:T(8,128)(2,1)}), bf16[8,1024,256]{1,2,0:T(8,128)(2,1)}, u32[]{:S(2)}, u32[]{:S(2)}) %all-to-all-start) | async-done | bytes 4194336 | tf_op jit(solution)/shard_map/all_to_all | solution.py:34
  83.2 3.2 %multiply_reduce_fusion.1 = f32[8,1024]{1,0:T(8,128)S(1)} fusion(bf16[8,1024,256]{1,2,0:T(8,128)(2,1)} %all-to-all-done), kind=kLoop, calls=%fused_computation.8 | loop fusion | flops 6283264 | bytes 4227072 | tf_op jit(solution)/shard_map/reduce_sum | solution.py:84
  86.4 4.1 %fusion.1 = bf16[1024,2048]{0,1:T(8,128)(2,1)} fusion(f32[2048]{0:T(1024)S(1)} %copy-done.4, f32[1024]{0:T(1024)S(1)} %add_rsqrt_fusion.1, bf16[8,1024,256]{1,2,0:T(8,128)(2,1)} %all-to-all-done), kind=kLoop, calls=%fused_computation.2 | loop fusion | flops 8388608 | bytes 8400896 | tf_op jit(solution)/shard_map/convert_element_type | solution.py:86
  90.5 6.5 %fusion.8 = f32[1024,768]{0,1:T(8,128)S(1)} fusion(bf16[1024,2048]{0,1:T(8,128)(2,1)} %fusion.1, bf16[2048,1024]{1,0:T(8,128)(2,1)} %all-gather.3.cloned.1.call-done), kind=kOutput, calls=%fused_computation.17 | convolution fusion | flops 3221225472 | bytes 10485760 | tf_op jit(solution)/shard_map/dot_general | solution.py:98
  101.7 2.5 convolution_convert_fusion
  104.6 74.0 %all_to_all.25 = bf16[1024,8,256]{2,0,1:T(8,128)(2,1)S(1)} all-to-all(bf16[1024,8,256]{2,0,1:T(8,128)(2,1)S(1)} %bitcast.108), channel_id=1, replica_groups=mesh['wide'=16,'head'=8] {'head'}, dimensions={1} | all-to-all | bytes 8388608 | tf_op jit(solution)/shard_map/all_to_all | solution.py:44
  180.5 49.7 %all_to_all.26 = bf16[8,256,1024]{2,1,0:T(8,128)(2,1)S(1)} all-to-all(bf16[8,256,1024]{2,1,0:T(8,128)(2,1)S(1)} %broadcast_in_dim.34), channel_id=1, replica_groups=mesh['wide'=16,'head'=8] {'head'}, dimensions={0} | all-to-all | bytes 8388608 | tf_op jit(solution)/shard_map/all_to_all | solution.py:34
  230.2 1.9 copy-done
  232.1 1.0 multiply_reduce_fusion
  233.1 4.1 %fusion.3 = bf16[2048,1024]{1,0:T(8,128)(2,1)} fusion(f32[2048]{0:T(1024)S(1)} %copy-done.5, f32[1024]{0:T(1024)S(1)} %add_rsqrt_fusion, bf16[8,256,1024]{2,1,0:T(8,128)(2,1)} %copy-done), kind=kLoop, calls=%fused_computation.5 | loop fusion | flops 8388608 | bytes 8400896 | tf_op jit(solution)/shard_map/convert_element_type | solution.py:146
  237.2 6.5 %fusion.4 = f32[512,1408]{1,0:T(8,128)S(1)} fusion(bf16[2048,2112]{0,1:T(8,128)(2,1)} %all-gather.5.cloned.1.call-done, bf16[2048,1024]{1,0:T(8,128)(2,1)} %fusion.3), kind=kOutput, calls=%fused_computation.9 | convolution fusion | flops 2952790016 | bytes 10747904 | tf_op jit(solution)/shard_map/dot_general | solution.py:155
  243.7 3.7 %convolution_convert_fusion.1 = bf16[512,2048]{1,0:T(8,128)(2,1)S(1)} fusion(bf16[2048,2112]{0,1:T(8,128)(2,1)} %all-gather.5.cloned.1.call-done, f32[512,1408]{1,0:T(8,128)S(1)} %fusion.4), kind=kOutput, calls=%fused_computation.19 | convolution fusion | flops 1479606272 | bytes 8126464 | tf_op jit(solution)/shard_map/dot_general | solution.py:162
  247.4 1.5 copy.36
  248.9 3.6 %all-to-all-start.4 = ((bf16[512,8,256]{2,0,1:T(8,128)(2,1)}), bf16[512,8,256]{2,0,1:T(8,128)(2,1)S(1)}, u32[]{:S(2)}, u32[]{:S(2)}) async-start(bf16[512,8,256]{2,0,1:T(8,128)(2,1)} %bitcast.110), calls=%async_computation.4 | async-start | bytes 4194304 | tf_op jit(solution)/shard_map/all_to_all | solution.py:44
  252.5 6.5 %fusion.6 = f32[512,1408]{1,0:T(8,128)S(1)} fusion(bf16[2048,2112]{0,1:T(8,128)(2,1)} %all-gather.5.cloned.1.call-done, bf16[2048,1024]{1,0:T(8,128)(2,1)} %fusion.3), kind=kOutput, calls=%fused_computation.11 | convolution fusion | flops 2952790016 | bytes 10747904 | tf_op jit(solution)/shard_map/dot_general | solution.py:155
  259.0 3.7 %convolution_convert_fusion.2 = bf16[512,2048]{1,0:T(8,128)(2,1)S(1)} fusion(bf16[2048,2112]{0,1:T(8,128)(2,1)} %all-gather.5.cloned.1.call-done, f32[512,1408]{1,0:T(8,128)S(1)} %fusion.6), kind=kOutput, calls=%fused_computation.20 | convolution fusion | flops 1479606272 | bytes 8126464 | tf_op jit(solution)/shard_map/dot_general | solution.py:162
  262.7 1.5 copy.37
  264.2 12.2 %all-to-all-done.4 = bf16[512,8,256]{2,0,1:T(8,128)(2,1)S(1)} async-done(((bf16[512,8,256]{2,0,1:T(8,128)(2,1)}), bf16[512,8,256]{2,0,1:T(8,128)(2,1)S(1)}, u32[]{:S(2)}, u32[]{:S(2)}) %all-to-all-start.4) | async-done | bytes 2097184 | tf_op jit(solution)/shard_map/all_to_all | solution.py:44
  276.4 4.4 %all-to-all-start.3 = ((bf16[512,8,256]{2,0,1:T(8,128)(2,1)}), bf16[512,8,256]{2,0,1:T(8,128)(2,1)}, u32[]{:S(2)}, u32[]{:S(2)}) async-start(bf16[512,8,256]{2,0,1:T(8,128)(2,1)} %bitcast.109), calls=%async_computation.3 | async-start | bytes 4194304 | tf_op jit(solution)/shard_map/all_to_all | solution.py:44
  281.1 23.7 %all-to-all-done.3 = bf16[512,8,256]{2,0,1:T(8,128)(2,1)} async-done(((bf16[512,8,256]{2,0,1:T(8,128)(2,1)}), bf16[512,8,256]{2,0,1:T(8,128)(2,1)}, u32[]{:S(2)}, u32[]{:S(2)}) %all-to-all-start.3) | async-done | bytes 2097184 | tf_op jit(solution)/shard_map/all_to_all | solution.py:44
  304.8 1.9 convert_reduce_fusion.2
  306.7 0.9 add_convert_fusion.2
  (59 shorter events, 8.0 us)
Async XLA Ops:
  6.5 83.9 %all-gather.3.cloned.1.call-start = ((), (), s32[]{:S(2)}) async-start(), calls=%async_computation.5 | async-start | bytes 4456448 | tf_op jit(solution)/shard_map/all_gather | solution.py:90
  13.1 6.5 %copy-start.2 = (f32[128,2,704]{0,2,1:T(8,128)S(1)}, f32[128,2,704]{0,2,1:T(8,128)}, u32[]{:S(2)}) copy-start(f32[128,2,704]{0,2,1:T(8,128)} %param.20) | copy-start | bytes 2162692
  13.1 6.6 %copy-start.3 = (f32[704,128]{1,0:T(8,128)S(1)}, f32[704,128]{1,0:T(8,128)}, u32[]{:S(2)}) copy-start(f32[704,128]{1,0:T(8,128)} %param.21) | copy-start | bytes 1081348
  13.1 7.5 %copy-start.7 = (f32[4,1,128]{2,1,0:T(1,128)S(1)}, f32[4,1,128]{2,1,0:T(1,128)}, u32[]{:S(2)}) copy-start(f32[4,1,128]{2,1,0:T(1,128)} %param.16) | copy-start | bytes 6148
  13.1 9.4 %copy-start.8 = (s32[2]{0:T(128)S(1)}, s32[2]{0:T(128)}, u32[]{:S(2)}) copy-start(s32[2]{0:T(128)} %param.12) | copy-start | bytes 28
  13.1 11.2 %copy-start.6 = (s32[2,512]{1,0:T(2,128)S(1)}, s32[2,512]{1,0:T(2,128)}, u32[]{:S(2)}) copy-start(s32[2,512]{1,0:T(2,128)} %param.13) | copy-start | bytes 12292
  13.1 70.1 %all-to-all-start = ((bf16[8,1024,256]{1,2,0:T(8,128)(2,1)}), bf16[8,1024,256]{1,2,0:T(8,128)(2,1)}, u32[]{:S(2)}, u32[]{:S(2)}) async-start(bf16[8,1024,256]{1,2,0:T(8,128)(2,1)} %broadcast_in_dim.26), calls=%async_computation | async-start | bytes 8388608 | tf_op jit(solution)/shard_map/all_to_all | solution.py:34
  19.6 66.8 %copy-start.4 = (f32[2048]{0:T(1024)S(1)}, f32[2048]{0:T(1024)}, u32[]{:S(2)}) copy-start(f32[2048]{0:T(1024)} %param.14) | copy-start | bytes 24580
  19.6 217.6 %all-gather.5.cloned.1.call-start = ((), (), s32[]{:S(2)}) async-start(), calls=%async_computation.6 | async-start | bytes 9191424 | tf_op jit(solution)/shard_map/all_gather | solution.py:96
  100.8 0.7 copy-start.9
  178.6 1.0 copy-start.1
  230.2 1.9 copy-start
  232.1 1.0 copy-start.5
  248.9 27.5 %all-to-all-start.4 = ((bf16[512,8,256]{2,0,1:T(8,128)(2,1)}), bf16[512,8,256]{2,0,1:T(8,128)(2,1)S(1)}, u32[]{:S(2)}, u32[]{:S(2)}) async-start(bf16[512,8,256]{2,0,1:T(8,128)(2,1)} %bitcast.110), calls=%async_computation.4 | async-start | bytes 4194304 | tf_op jit(solution)/shard_map/all_to_all | solution.py:44
  276.4 28.4 %all-to-all-start.3 = ((bf16[512,8,256]{2,0,1:T(8,128)(2,1)}), bf16[512,8,256]{2,0,1:T(8,128)(2,1)}, u32[]{:S(2)}, u32[]{:S(2)}) async-start(bf16[512,8,256]{2,0,1:T(8,128)(2,1)} %bitcast.109), calls=%async_computation.3 | async-start | bytes 4194304 | tf_op jit(solution)/shard_map/all_to_all | solution.py:44
Sparse Core Ops, SparseCore 0:
  9.7 71.2 all-gather.2
  83.3 102.7 all-gather.4

commit v10 on v7

--- a/solution.py
+++ b/solution.py
@@ -141,10 +141,10 @@
     units = gu_shape[2]
     down_cols = ffn_pack[:, gu_cols:]
     rows_here = middle.shape[0]
-    piece = rows_here // 2
+    cuts = (0, rows_here * 3 // 8, rows_here)
     results = []
     for part in range(2):
-        columns = normed2[:, part * piece : (part + 1) * piece]
+        columns = normed2[:, cuts[part] : cuts[part + 1]]
         both = lax.dot_general(
             columns,
             ffn_pack[:, :gu_cols],
@@ -159,7 +159,7 @@
             preferred_element_type=jnp.float32,
         )
         ffn = scatter_sum(ffn_terms, "head", n_head)
-        stream = middle[part * piece : (part + 1) * piece].astype(jnp.float32)
+        stream = middle[cuts[part] : cuts[part + 1]].astype(jnp.float32)
         results.append((stream + ffn).astype(jnp.bfloat16))
     return jnp.concatenate(results, axis=0)
 

time: 312 us -> 309 us (level)
  waiting for transfers between devices: 93.8 us -> 90.2 us
    all_to_all x2, waiting for transfers between devices: 35.9 us -> 32.3 us  [scatter_sum(): got = lax.all_to_all(parts, axis, 1, 1, tiled=True)]
  transfers between devices with their start and end apart: 5 -> 5, of which waited for: 3 -> 3; matrix products, arithmetic and copies ran while one was open for 15% -> 16% of each run, Pallas kernels for 0% -> 0%
where the time goes in v10:
time: 309 us; the launch traced here: 308 us
  blocking collectives  124 us (40%)
  waiting for transfers between devices  90.2 us (29%)
  matrix products  32.5 us (11%)
  other arithmetic  22.1 us (7%)
  between operations  15 us (5%)
  starting transfers between devices  13.7 us (4%)
  local copies, waits for them, and re-layouts  10.5 us (3%)
    all_to_all x1, blocking collectives, scatter_sum(): got = lax.all_to_all(parts, axis, 1, 1, tiled=True)  74 us
    all_to_all x1, waiting for transfers between devices, gather_blocks(): got = lax.all_to_all(spread, axis, 0, 0, tiled=True)  57.9 us
    all_to_all x1, blocking collectives, gather_blocks(): got = lax.all_to_all(spread, axis, 0, 0, tiled=True)  49.7 us
    all_to_all x2, waiting for transfers between devices, scatter_sum(): got = lax.all_to_all(parts, axis, 1, 1, tiled=True)  32.3 us
    dot_general x2, matrix products, body(): lax.dot_general(columns, ffn_pack[:, :gu_cols], (((0,), (0,)), ((), ())),...  13.3 us
    dot_general x2, matrix products, body(): lax.dot_general(hidden, down_cols, (((1,), (1,)), ((), ())), preferred_el...  7.43 us
    all_to_all x2, starting transfers between devices, scatter_sum(): got = lax.all_to_all(parts, axis, 1, 1, tiled=True)  7.21 us
    dot_general x1, matrix products, body(): jnp.dot(columns, attn_pack[:, :qkv_cols], preferred_element_type=jnp.floa...  6.52 us
  transfers between devices with their start and end apart: 5, of which 3 were waited for; matrix products, arithmetic and copies ran while one was open for 16% of the time, Pallas kernels for 0%

profile of v10, /device:TPU:2, one launch (start us, length us, event | category | flops | bytes accessed | tf_op | source)
XLA Modules:
  0.0 307.7 jit_solution(3612175375507973913)
XLA Ops:
  6.5 1.0 convert_element_type.144
  7.6 0.9 convert_bitcast_fusion.1
  8.6 0.7 pad_maximum_fusion.2
  9.3 1.2 copy.23
  10.6 2.5 broadcast_in_dim.26
  13.1 6.5 %all-to-all-start = ((bf16[8,1024,256]{1,2,0:T(8,128)(2,1)}), bf16[8,1024,256]{1,2,0:T(8,128)(2,1)}, u32[]{:S(2)}, u32[]{:S(2)}) async-start(bf16[8,1024,256]{1,2,0:T(8,128)(2,1)} %broadcast_in_dim.26), calls=%async_computation | async-start | bytes 8388608 | tf_op jit(solution)/shard_map/all_to_all | solution.py:34
  19.7 0.8 pad_maximum_fusion
  20.6 0.6 multiply_reduce_fusion.4
  23.1 1.2 iota_compare_fusion.1
  24.3 1.0 multiply_cosine_fusion.1
  25.3 57.9 %all-to-all-done = bf16[8,1024,256]{1,2,0:T(8,128)(2,1)} async-done(((bf16[8,1024,256]{1,2,0:T(8,128)(2,1)}), bf16[8,1024,256]{1,2,0:T(8,128)(2,1)}, u32[]{:S(2)}, u32[]{:S(2)}) %all-to-all-start) | async-done | bytes 4194336 | tf_op jit(solution)/shard_map/all_to_all | solution.py:34
  83.2 3.1 %multiply_reduce_fusion.1 = f32[1024]{0:T(1024)S(1)} fusion(bf16[8,1024,256]{1,2,0:T(8,128)(2,1)} %all-to-all-done), kind=kLoop, calls=%fused_computation.8 | loop fusion | flops 6290432 | bytes 4198400 | tf_op jit(solution)/shard_map/reduce_sum | solution.py:15
  86.3 4.1 %fusion.1 = bf16[1024,2048]{0,1:T(8,128)(2,1)} fusion(f32[2048]{0:T(1024)S(1)} %copy-done.4, f32[1024]{0:T(1024)S(1)} %add_rsqrt_fusion.1, bf16[8,1024,256]{1,2,0:T(8,128)(2,1)} %all-to-all-done), kind=kLoop, calls=%fused_computation.2 | loop fusion | flops 8388608 | bytes 8400896 | tf_op jit(solution)/shard_map/convert_element_type | solution.py:82
  90.4 6.5 %fusion.8 = f32[1024,768]{0,1:T(8,128)S(1)} fusion(bf16[1024,2048]{0,1:T(8,128)(2,1)} %fusion.1, bf16[2048,1024]{1,0:T(8,128)(2,1)} %all-gather.3.cloned.1.call-done), kind=kOutput, calls=%fused_computation.17 | convolution fusion | flops 3221225472 | bytes 10485760 | tf_op jit(solution)/shard_map/dot_general | solution.py:94
  101.6 2.5 convolution_convert_fusion
  104.4 74.0 %all_to_all.25 = bf16[1024,8,256]{2,0,1:T(8,128)(2,1)S(1)} all-to-all(bf16[1024,8,256]{2,0,1:T(8,128)(2,1)S(1)} %bitcast.107), channel_id=1, replica_groups=mesh['wide'=16,'head'=8] {'head'}, dimensions={1} | all-to-all | bytes 8388608 | tf_op jit(solution)/shard_map/all_to_all | solution.py:44
  180.3 49.7 %all_to_all.26 = bf16[8,256,1024]{2,1,0:T(8,128)(2,1)S(1)} all-to-all(bf16[8,256,1024]{2,1,0:T(8,128)(2,1)S(1)} %broadcast_in_dim.34), channel_id=1, replica_groups=mesh['wide'=16,'head'=8] {'head'}, dimensions={0} | all-to-all | bytes 8388608 | tf_op jit(solution)/shard_map/all_to_all | solution.py:34
  230.0 0.9 multiply_reduce_fusion
  231.0 2.5 fusion.3
  233.5 5.8 %fusion.6 = f32[384,1408]{1,0:T(8,128)S(1)} fusion(bf16[2048,2112]{0,1:T(8,128)(2,1)} %all-gather.5.cloned.1.call-done, bf16[2048,1024]{1,0:T(8,128)(2,1)} %fusion.3), kind=kOutput, calls=%fused_computation.12 | convolution fusion | flops 2214592512 | bytes 9502720 | tf_op jit(solution)/shard_map/dot_general | solution.py:148
  239.3 3.3 %convolution_convert_fusion.2 = bf16[384,2048]{1,0:T(8,128)(2,1)S(1)} fusion(bf16[2048,2112]{0,1:T(8,128)(2,1)} %all-gather.5.cloned.1.call-done, f32[384,1408]{1,0:T(8,128)S(1)} %fusion.6), kind=kOutput, calls=%fused_computation.20 | convolution fusion | flops 1109704704 | bytes 6815744 | tf_op jit(solution)/shard_map/dot_general | solution.py:155
  242.6 1.3 copy.37
  243.9 3.6 %all-to-all-start.3 = ((bf16[384,8,256]{2,0,1:T(8,128)(2,1)}), bf16[384,8,256]{2,0,1:T(8,128)(2,1)S(1)}, u32[]{:S(2)}, u32[]{:S(2)}) async-start(bf16[384,8,256]{2,0,1:T(8,128)(2,1)} %bitcast.105), calls=%async_computation.3 | async-start | bytes 3145728 | tf_op jit(solution)/shard_map/all_to_all | solution.py:44
  247.4 7.5 %fusion.4 = f32[640,1408]{1,0:T(8,128)S(1)} fusion(bf16[2048,2112]{0,1:T(8,128)(2,1)} %all-gather.5.cloned.1.call-done, bf16[2048,1024]{1,0:T(8,128)(2,1)} %fusion.3), kind=kOutput, calls=%fused_computation.10 | convolution fusion | flops 3690987520 | bytes 11993088 | tf_op jit(solution)/shard_map/dot_general | solution.py:148
  255.0 4.1 %convolution_convert_fusion.1 = bf16[640,2048]{1,0:T(8,128)(2,1)S(1)} fusion(bf16[2048,2112]{0,1:T(8,128)(2,1)} %all-gather.5.cloned.1.call-done, f32[640,1408]{1,0:T(8,128)S(1)} %fusion.4), kind=kOutput, calls=%fused_computation.16 | convolution fusion | flops 1849507840 | bytes 9437184 | tf_op jit(solution)/shard_map/dot_general | solution.py:155
  259.1 1.7 copy.36
  260.8 4.9 %all-to-all-done.3 = bf16[384,8,256]{2,0,1:T(8,128)(2,1)S(1)} async-done(((bf16[384,8,256]{2,0,1:T(8,128)(2,1)}), bf16[384,8,256]{2,0,1:T(8,128)(2,1)S(1)}, u32[]{:S(2)}, u32[]{:S(2)}) %all-to-all-start.3) | async-done | bytes 1572896 | tf_op jit(solution)/shard_map/all_to_all | solution.py:44
  265.7 1.1 copy-done
  266.9 3.6 %all-to-all-start.4 = ((bf16[640,8,256]{2,0,1:T(8,128)(2,1)}), bf16[640,8,256]{2,0,1:T(8,128)(2,1)S(1)}, u32[]{:S(2)}, u32[]{:S(2)}) async-start(bf16[640,8,256]{2,0,1:T(8,128)(2,1)} %bitcast.104), calls=%async_computation.4 | async-start | bytes 5242880 | tf_op jit(solution)/shard_map/all_to_all | solution.py:44
  270.5 1.7 convert_reduce_fusion.2
  272.2 27.4 %all-to-all-done.4 = bf16[640,8,256]{2,0,1:T(8,128)(2,1)S(1)} async-done(((bf16[640,8,256]{2,0,1:T(8,128)(2,1)}), bf16[640,8,256]{2,0,1:T(8,128)(2,1)S(1)}, u32[]{:S(2)}, u32[]{:S(2)}) %all-to-all-start.4) | async-done | bytes 2621472 | tf_op jit(solution)/shard_map/all_to_all | solution.py:44
  300.1 0.8 pad_maximum_fusion.1
  (58 shorter events, 8.2 us)
Async XLA Ops:
  6.5 83.8 %all-gather.3.cloned.1.call-start = ((), (), s32[]{:S(2)}) async-start(), calls=%async_computation.5 | async-start | bytes 4456448 | tf_op jit(solution)/shard_map/all_gather | solution.py:86
  13.1 6.5 %copy-start.2 = (f32[128,2,704]{0,2,1:T(8,128)S(1)}, f32[128,2,704]{0,2,1:T(8,128)}, u32[]{:S(2)}) copy-start(f32[128,2,704]{0,2,1:T(8,128)} %param.20) | copy-start | bytes 2162692
  13.1 6.6 %copy-start.3 = (f32[704,128]{1,0:T(8,128)S(1)}, f32[704,128]{1,0:T(8,128)}, u32[]{:S(2)}) copy-start(f32[704,128]{1,0:T(8,128)} %param.21) | copy-start | bytes 1081348
  13.1 7.5 %copy-start.7 = (f32[4,1,128]{2,1,0:T(1,128)S(1)}, f32[4,1,128]{2,1,0:T(1,128)}, u32[]{:S(2)}) copy-start(f32[4,1,128]{2,1,0:T(1,128)} %param.16) | copy-start | bytes 6148
  13.1 9.4 %copy-start.8 = (s32[2]{0:T(128)S(1)}, s32[2]{0:T(128)}, u32[]{:S(2)}) copy-start(s32[2]{0:T(128)} %param.12) | copy-start | bytes 28
  13.1 11.2 %copy-start.6 = (s32[2,512]{1,0:T(2,128)S(1)}, s32[2,512]{1,0:T(2,128)}, u32[]{:S(2)}) copy-start(s32[2,512]{1,0:T(2,128)} %param.13) | copy-start | bytes 12292
  13.1 70.1 %all-to-all-start = ((bf16[8,1024,256]{1,2,0:T(8,128)(2,1)}), bf16[8,1024,256]{1,2,0:T(8,128)(2,1)}, u32[]{:S(2)}, u32[]{:S(2)}) async-start(bf16[8,1024,256]{1,2,0:T(8,128)(2,1)} %broadcast_in_dim.26), calls=%async_computation | async-start | bytes 8388608 | tf_op jit(solution)/shard_map/all_to_all | solution.py:34
  19.6 213.9 %all-gather.5.cloned.1.call-start = ((), (), s32[]{:S(2)}) async-start(), calls=%async_computation.6 | async-start | bytes 9191424 | tf_op jit(solution)/shard_map/all_gather | solution.py:92
  19.7 66.6 %copy-start.4 = (f32[2048]{0:T(1024)S(1)}, f32[2048]{0:T(1024)}, u32[]{:S(2)}) copy-start(f32[2048]{0:T(1024)} %param.14) | copy-start | bytes 24580
  100.7 0.7 copy-start.9
  178.4 1.0 copy-start.1
  230.0 0.9 copy-start.5
  243.9 21.9 %all-to-all-start.3 = ((bf16[384,8,256]{2,0,1:T(8,128)(2,1)}), bf16[384,8,256]{2,0,1:T(8,128)(2,1)S(1)}, u32[]{:S(2)}, u32[]{:S(2)}) async-start(bf16[384,8,256]{2,0,1:T(8,128)(2,1)} %bitcast.105), calls=%async_computation.3 | async-start | bytes 3145728 | tf_op jit(solution)/shard_map/all_to_all | solution.py:44
  265.7 1.1 copy-start
  266.9 32.7 %all-to-all-start.4 = ((bf16[640,8,256]{2,0,1:T(8,128)(2,1)}), bf16[640,8,256]{2,0,1:T(8,128)(2,1)S(1)}, u32[]{:S(2)}, u32[]{:S(2)}) async-start(bf16[640,8,256]{2,0,1:T(8,128)(2,1)} %bitcast.104), calls=%async_computation.4 | async-start | bytes 5242880 | tf_op jit(solution)/shard_map/all_to_all | solution.py:44
Sparse Core Ops, SparseCore 0:
  9.7 71.2 all-gather.2
  83.3 102.7 all-gather.4

commit v11 on v10

--- a/solution.py
+++ b/solution.py
@@ -141,7 +141,7 @@
     units = gu_shape[2]
     down_cols = ffn_pack[:, gu_cols:]
     rows_here = middle.shape[0]
-    cuts = (0, rows_here * 3 // 8, rows_here)
+    cuts = (0, rows_here // 4, rows_here)
     results = []
     for part in range(2):
         columns = normed2[:, cuts[part] : cuts[part + 1]]

time: 309 us -> 312 us (level)
  transfers between devices with their start and end apart: 5 -> 5, of which waited for: 3 -> 2; matrix products, arithmetic and copies ran while one was open for 16% -> 17% of each run, Pallas kernels for 0% -> 0%
where the time goes in v11:
time: 312 us; the launch traced here: 311 us
  blocking collectives  124 us (40%)
  waiting for transfers between devices  90.2 us (29%)
  matrix products  32.9 us (11%)
  other arithmetic  22.8 us (7%)
  starting transfers between devices  15.7 us (5%)
  between operations  15 us (5%)
  local copies, waits for them, and re-layouts  11 us (4%)
    all_to_all x1, blocking collectives, scatter_sum(): got = lax.all_to_all(parts, axis, 1, 1, tiled=True)  74 us
    all_to_all x1, waiting for transfers between devices, gather_blocks(): got = lax.all_to_all(spread, axis, 0, 0, tiled=True)  57.9 us
    all_to_all x1, blocking collectives, gather_blocks(): got = lax.all_to_all(spread, axis, 0, 0, tiled=True)  49.7 us
    all_to_all x2, waiting for transfers between devices, scatter_sum(): got = lax.all_to_all(parts, axis, 1, 1, tiled=True)  32.3 us
    dot_general x2, matrix products, body(): lax.dot_general(columns, ffn_pack[:, :gu_cols], (((0,), (0,)), ((), ())),...  13.4 us
    all_to_all x2, starting transfers between devices, scatter_sum(): got = lax.all_to_all(parts, axis, 1, 1, tiled=True)  9.16 us
    dot_general x2, matrix products, body(): lax.dot_general(hidden, down_cols, (((1,), (1,)), ((), ())), preferred_el...  7.77 us
    dot_general x1, matrix products, body(): jnp.dot(columns, attn_pack[:, :qkv_cols], preferred_element_type=jnp.floa...  6.52 us
  transfers between devices with their start and end apart: 5, of which 2 were waited for; matrix products, arithmetic and copies ran while one was open for 17% of the time, Pallas kernels for 0%

profile of v11, /device:TPU:2, one launch (start us, length us, event | category | flops | bytes accessed | tf_op | source)
XLA Modules:
  0.0 311.2 jit_solution(849591925330413832)
XLA Ops:
  6.5 1.0 convert_element_type.144
  7.6 0.9 convert_bitcast_fusion.1
  8.6 0.7 pad_maximum_fusion.2
  9.3 1.2 copy.23
  10.6 2.5 broadcast_in_dim.26
  13.1 6.5 %all-to-all-start = ((bf16[8,1024,256]{1,2,0:T(8,128)(2,1)}), bf16[8,1024,256]{1,2,0:T(8,128)(2,1)}, u32[]{:S(2)}, u32[]{:S(2)}) async-start(bf16[8,1024,256]{1,2,0:T(8,128)(2,1)} %broadcast_in_dim.26), calls=%async_computation | async-start | bytes 8388608 | tf_op jit(solution)/shard_map/all_to_all | solution.py:34
  19.7 0.8 pad_maximum_fusion
  20.6 0.6 multiply_reduce_fusion.4
  23.1 1.2 iota_compare_fusion.1
  24.3 1.0 multiply_cosine_fusion.1
  25.3 57.9 %all-to-all-done = bf16[8,1024,256]{1,2,0:T(8,128)(2,1)} async-done(((bf16[8,1024,256]{1,2,0:T(8,128)(2,1)}), bf16[8,1024,256]{1,2,0:T(8,128)(2,1)}, u32[]{:S(2)}, u32[]{:S(2)}) %all-to-all-start) | async-done | bytes 4194336 | tf_op jit(solution)/shard_map/all_to_all | solution.py:34
  83.2 3.1 multiply_reduce_fusion.1
  86.3 4.1 %fusion.1 = bf16[1024,2048]{0,1:T(8,128)(2,1)} fusion(f32[2048]{0:T(1024)S(1)} %copy-done.6, f32[1024]{0:T(1024)S(1)} %add_rsqrt_fusion.1, bf16[8,1024,256]{1,2,0:T(8,128)(2,1)} %all-to-all-done), kind=kLoop, calls=%fused_computation.2 | loop fusion | flops 8388608 | bytes 8400896 | tf_op jit(solution)/shard_map/convert_element_type | solution.py:82
  90.4 6.5 %fusion.9 = f32[1024,768]{0,1:T(8,128)S(1)} fusion(bf16[1024,2048]{0,1:T(8,128)(2,1)} %fusion.1, bf16[2048,1024]{1,0:T(8,128)(2,1)} %all-gather.3.cloned.1.call-done), kind=kOutput, calls=%fused_computation.19 | convolution fusion | flops 3221225472 | bytes 10485760 | tf_op jit(solution)/shard_map/dot_general | solution.py:94
  101.6 2.5 convolution_convert_fusion
  104.4 74.0 %all_to_all.25 = bf16[1024,8,256]{2,0,1:T(8,128)(2,1)S(1)} all-to-all(bf16[1024,8,256]{2,0,1:T(8,128)(2,1)S(1)} %bitcast.107), channel_id=1, replica_groups=mesh['wide'=16,'head'=8] {'head'}, dimensions={1} | all-to-all | bytes 8388608 | tf_op jit(solution)/shard_map/all_to_all | solution.py:44
  180.3 49.7 %all_to_all.26 = bf16[8,256,1024]{2,1,0:T(8,128)(2,1)S(1)} all-to-all(bf16[8,256,1024]{2,1,0:T(8,128)(2,1)S(1)} %broadcast_in_dim.34), channel_id=1, replica_groups=mesh['wide'=16,'head'=8] {'head'}, dimensions={0} | all-to-all | bytes 8388608 | tf_op jit(solution)/shard_map/all_to_all | solution.py:34
  230.1 0.9 multiply_reduce_fusion
  231.0 2.5 fusion.3
  233.5 4.8 %fusion.6 = f32[256,1408]{1,0:T(8,128)S(1)} fusion(bf16[2048,2112]{0,1:T(8,128)(2,1)} %all-gather.5.cloned.1.call-done, bf16[2048,1024]{1,0:T(8,128)(2,1)} %fusion.3), kind=kOutput, calls=%fused_computation.12 | convolution fusion | flops 1476395008 | bytes 8257536 | tf_op jit(solution)/shard_map/dot_general | solution.py:148
  238.3 2.9 convolution_convert_fusion.2
  241.2 1.1 copy.37
  242.4 3.6 %all-to-all-start.3 = ((bf16[256,8,256]{2,0,1:T(8,128)(2,1)}), bf16[256,8,256]{2,0,1:T(8,128)(2,1)S(1)}, u32[]{:S(2)}, u32[]{:S(2)}) async-start(bf16[256,8,256]{2,0,1:T(8,128)(2,1)} %bitcast.105), calls=%async_computation.3 | async-start | bytes 2097152 | tf_op jit(solution)/shard_map/all_to_all | solution.py:44
  245.9 8.5 %fusion.4 = f32[768,1408]{1,0:T(8,128)S(1)} fusion(bf16[2048,2112]{0,1:T(8,128)(2,1)} %all-gather.5.cloned.1.call-done, bf16[2048,1024]{1,0:T(8,128)(2,1)} %fusion.3), kind=kOutput, calls=%fused_computation.10 | convolution fusion | flops 4429185024 | bytes 13238272 | tf_op jit(solution)/shard_map/dot_general | solution.py:148
  254.5 4.9 %convolution_convert_fusion.1 = bf16[768,2048]{1,0:T(8,128)(2,1)S(1)} fusion(bf16[2048,2112]{0,1:T(8,128)(2,1)} %all-gather.5.cloned.1.call-done, f32[768,1408]{1,0:T(8,128)S(1)} %fusion.4), kind=kOutput, calls=%fused_computation.16 | convolution fusion | flops 2219409408 | bytes 10747904 | tf_op jit(solution)/shard_map/dot_general | solution.py:155
  259.3 1.9 copy.36
  261.2 1.0 copy-done.2
  262.2 5.6 %all-to-all-start.4 = ((bf16[768,8,256]{2,0,1:T(8,128)(2,1)}), bf16[768,8,256]{2,0,1:T(8,128)(2,1)S(1)}, u32[]{:S(2)}, u32[]{:S(2)}) async-start(bf16[768,8,256]{2,0,1:T(8,128)(2,1)} %bitcast.104), calls=%async_computation.4 | async-start | bytes 6291456 | tf_op jit(solution)/shard_map/all_to_all | solution.py:44
  267.8 1.4 convert_reduce_fusion.2
  269.2 0.9 add_convert_fusion.4
  270.1 32.3 %all-to-all-done.4 = bf16[768,8,256]{2,0,1:T(8,128)(2,1)S(1)} async-done(((bf16[768,8,256]{2,0,1:T(8,128)(2,1)}), bf16[768,8,256]{2,0,1:T(8,128)(2,1)S(1)}, u32[]{:S(2)}, u32[]{:S(2)}) %all-to-all-start.4) | async-done | bytes 3145760 | tf_op jit(solution)/shard_map/all_to_all | solution.py:44
  303.5 0.8 pad_maximum_fusion.1
  (62 shorter events, 8.8 us)
Async XLA Ops:
  6.5 83.8 %all-gather.3.cloned.1.call-start = ((), (), s32[]{:S(2)}) async-start(), calls=%async_computation.5 | async-start | bytes 4456448 | tf_op jit(solution)/shard_map/all_gather | solution.py:86
  13.1 6.5 %copy-start.4 = (f32[128,2,704]{0,2,1:T(8,128)S(1)}, f32[128,2,704]{0,2,1:T(8,128)}, u32[]{:S(2)}) copy-start(f32[128,2,704]{0,2,1:T(8,128)} %param.20) | copy-start | bytes 2162692
  13.1 6.6 %copy-start.5 = (f32[704,128]{1,0:T(8,128)S(1)}, f32[704,128]{1,0:T(8,128)}, u32[]{:S(2)}) copy-start(f32[704,128]{1,0:T(8,128)} %param.21) | copy-start | bytes 1081348
  13.1 7.5 %copy-start.9 = (f32[4,1,128]{2,1,0:T(1,128)S(1)}, f32[4,1,128]{2,1,0:T(1,128)}, u32[]{:S(2)}) copy-start(f32[4,1,128]{2,1,0:T(1,128)} %param.16) | copy-start | bytes 6148
  13.1 9.4 %copy-start.10 = (s32[2]{0:T(128)S(1)}, s32[2]{0:T(128)}, u32[]{:S(2)}) copy-start(s32[2]{0:T(128)} %param.12) | copy-start | bytes 28
  13.1 11.2 %copy-start.8 = (s32[2,512]{1,0:T(2,128)S(1)}, s32[2,512]{1,0:T(2,128)}, u32[]{:S(2)}) copy-start(s32[2,512]{1,0:T(2,128)} %param.13) | copy-start | bytes 12292
  13.1 70.1 %all-to-all-start = ((bf16[8,1024,256]{1,2,0:T(8,128)(2,1)}), bf16[8,1024,256]{1,2,0:T(8,128)(2,1)}, u32[]{:S(2)}, u32[]{:S(2)}) async-start(bf16[8,1024,256]{1,2,0:T(8,128)(2,1)} %broadcast_in_dim.26), calls=%async_computation | async-start | bytes 8388608 | tf_op jit(solution)/shard_map/all_to_all | solution.py:34
  19.6 66.7 %copy-start.6 = (f32[2048]{0:T(1024)S(1)}, f32[2048]{0:T(1024)}, u32[]{:S(2)}) copy-start(f32[2048]{0:T(1024)} %param.14) | copy-start | bytes 24580
  19.6 213.9 %all-gather.5.cloned.1.call-start = ((), (), s32[]{:S(2)}) async-start(), calls=%async_computation.6 | async-start | bytes 9191424 | tf_op jit(solution)/shard_map/all_gather | solution.py:92
  100.7 0.7 copy-start.11
  178.4 1.0 copy-start.3
  179.6 50.5 %copy-start = (bf16[1024,256]{1,0:T(8,128)(2,1)}, bf16[1024,256]{1,0:T(8,128)(2,1)S(1)}, u32[]{:S(2)}) copy-start(bf16[1024,256]{1,0:T(8,128)(2,1)S(1)} %add_convert_fusion) | copy-start | bytes 1572868
  230.1 0.9 copy-start.7
  242.4 18.9 %all-to-all-start.3 = ((bf16[256,8,256]{2,0,1:T(8,128)(2,1)}), bf16[256,8,256]{2,0,1:T(8,128)(2,1)S(1)}, u32[]{:S(2)}, u32[]{:S(2)}) async-start(bf16[256,8,256]{2,0,1:T(8,128)(2,1)} %bitcast.105), calls=%async_computation.3 | async-start | bytes 2097152 | tf_op jit(solution)/shard_map/all_to_all | solution.py:44
  261.2 1.0 copy-start.2
  262.2 40.2 %all-to-all-start.4 = ((bf16[768,8,256]{2,0,1:T(8,128)(2,1)}), bf16[768,8,256]{2,0,1:T(8,128)(2,1)S(1)}, u32[]{:S(2)}, u32[]{:S(2)}) async-start(bf16[768,8,256]{2,0,1:T(8,128)(2,1)} %bitcast.104), calls=%async_computation.4 | async-start | bytes 6291456 | tf_op jit(solution)/shard_map/all_to_all | solution.py:44
  302.4 1.0 copy-start.1
Sparse Core Ops, SparseCore 0:
  9.7 71.2 all-gather.2
  83.3 102.7 all-gather.4
